TPU v7x, 256 devices: a whole 4x4x8 slice. The times are simulated.
256 devices in a mesh: dp: 8 (over x, core), seq: 32 (over y, z).
Axes of the slice: x: 4, y: 4, z: 8, core: 2. Of those that a mesh axis runs over, the one named last changes fastest.
Arguments:
- voxels: bfloat16 [8, 4096, 4096], P('dp', 'seq'), may hold values from -6 to 6
- patch_weight: bfloat16 [4096, 1024], replicated, may hold values from -0.09375 to 0.09375
- patch_bias: float32 [1024], replicated, may hold values from -3 to 3
- enc_position: bfloat16 [4096, 1024], P('seq'), may hold values from -5 to 5
- visible: int32 [8, 4096], P('dp', 'seq'), may hold values from 0 to 1, as said below
- enc_project: bfloat16 [1024, 3072], P(('dp', 'seq')), may hold values from -1 to 1
- enc_merge: bfloat16 [1024, 1024], P(('dp', 'seq')), may hold values from -0.1875 to 0.1875
- dec_lift: bfloat16 [1024, 512], P(('dp', 'seq')), may hold values from -0.1875 to 0.1875
- mask_token: float32 [512], replicated, may hold values from -4 to 4
- dec_position: bfloat16 [4096, 512], P('seq'), may hold values from -5 to 5
- dec_project: bfloat16 [512, 1536], P(('dp', 'seq')), may hold values from -1 to 1
- dec_merge: bfloat16 [512, 512], P(('dp', 'seq')), may hold values from -0.25 to 0.25
- dec_predict: bfloat16 [512, 4096], P(('dp', 'seq')), may hold values from -0.25 to 0.25
Outputs:
- decoded: bfloat16 [8, 4096, 512], P('dp', 'seq')
- patch_loss: float32 [8, 4096], P('dp', 'seq')
Inputs may be any that keep to these rules, and one draw needn't show every extreme that they name: `visible`: each cube has exactly 1024 ones. Each slab of 128 consecutive patches holds between 0 and 64 ones, and in every cube some slab holds exactly 64.
All inputs are finite; a program needn't handle non-finite values.
Results may differ from a plain program's by a relative error of at most 0.008.
Values may be sent and summed in bfloat16 or wider, within the bound.
No kernel may reach another device: no remote copies, remote signals or barrier semaphores. Data moves between devices by JAX's collectives and lax.ppermute only.
A program may use at most 128 MiB of HBM per device.

v0:
```python
import math

import jax
import jax.numpy as jnp
from jax import lax
from jax.sharding import PartitionSpec as P

ENC_HEADS = 16
DEC_HEADS = 16


def layer_norm(values):
    centre = values - jnp.mean(values, axis=-1, keepdims=True)
    spread = jnp.mean(centre * centre, axis=-1, keepdims=True)
    return centre * lax.rsqrt(spread + 1e-06)


def attend_rows(queries, key_rows, value_rows, key_ok):
    query_rows, local_heads, head_size = queries.shape
    block_rows = math.gcd(query_rows, 512)
    score_scale = 1.0 / math.sqrt(head_size)
    query_blocks = queries[:, 0].reshape(query_rows // block_rows, block_rows, head_size)
    keys_one = key_rows[:, 0]
    values_one = value_rows[:, 0]

    def one_block(query_block):
        scores = (
            jnp.einsum("qd,kd->qk", query_block, keys_one, preferred_element_type=jnp.float32)
            * score_scale
        )
        if key_ok is not None:
            scores = jnp.where(key_ok[None, :], scores, -1e30)
        top_score = jnp.max(scores, axis=-1, keepdims=True)
        exponent = jnp.exp(scores - top_score)
        weights = (exponent / jnp.sum(exponent, axis=-1, keepdims=True)).astype(jnp.bfloat16)
        return jnp.einsum(
            "qk,kd->qd", weights, values_one, preferred_element_type=jnp.float32
        ).astype(jnp.bfloat16)

    head_outputs = [lax.map(one_block, query_blocks).reshape(query_rows, head_size)]
    return jnp.stack(head_outputs, axis=1)


def spread_heads(packed, heads, seq_count):
    row_count = packed.shape[0]
    head_size = packed.shape[1] // (3 * heads)
    query_parts = max(seq_count // heads, 1)
    local_heads = max(heads // seq_count, 1)
    layout = packed.reshape(row_count, 3, heads, head_size)
    layout = jnp.repeat(layout, query_parts, axis=2)
    layout = layout.reshape(row_count, 3, seq_count, local_heads, head_size).transpose(
        2, 0, 1, 3, 4
    )
    return layout.reshape(seq_count, row_count, 3 * local_heads * head_size)


def attend_heads(incoming, key_ok, heads, query_part, query_parts):
    sources, row_count, triple_width = incoming.shape
    local_heads = max(heads // sources, 1)
    head_size = triple_width // (3 * local_heads)
    all_rows = sources * row_count
    layout = incoming.reshape(all_rows, 3, local_heads, head_size)
    query_rows = all_rows // query_parts
    queries = lax.dynamic_slice_in_dim(layout[:, 0], query_part * query_rows, query_rows, 0)
    return attend_rows(queries, layout[:, 1], layout[:, 2], key_ok)


def place_rows(mixed_part, all_rows, query_part, sources):
    query_rows = mixed_part.shape[0]
    flat_part = mixed_part.reshape(query_rows, -1)
    buffer = jnp.zeros((all_rows, flat_part.shape[1]), jnp.bfloat16)
    buffer = lax.dynamic_update_slice(buffer, flat_part, (query_part * query_rows, 0))
    return buffer.reshape(sources, all_rows // sources, flat_part.shape[1])


def collect_heads(returned, heads, query_parts):
    sources, row_count, piece_width = returned.shape
    local_heads = max(heads // sources, 1)
    head_size = piece_width // local_heads
    arranged = returned.reshape(sources, row_count, local_heads, head_size).transpose(1, 0, 2, 3)
    arranged = arranged.reshape(row_count, heads, query_parts, head_size)
    summed = jnp.sum(arranged.astype(jnp.float32), axis=2).astype(jnp.bfloat16)
    return summed.reshape(row_count, heads * head_size)


def shards(
    voxels,
    patch_weight,
    patch_bias,
    enc_position,
    visible,
    enc_project,
    enc_merge,
    dec_lift,
    mask_token,
    dec_position,
    dec_project,
    dec_merge,
    dec_predict,
):
    seq_count = lax.axis_size("seq")
    seq_place = lax.axis_index("seq")
    enc_parts = max(seq_count // ENC_HEADS, 1)
    dec_parts = max(seq_count // DEC_HEADS, 1)
    enc_part = seq_place % enc_parts
    dec_part = seq_place % dec_parts
    full_project, full_merge, full_lift = (
        lax.all_gather(enc_project, ("dp", "seq"), axis=0, tiled=True),
        lax.all_gather(enc_merge, ("dp", "seq"), axis=0, tiled=True),
        lax.all_gather(dec_lift, ("dp", "seq"), axis=0, tiled=True),
    )
    tok_local = voxels.shape[1]
    slab_max = tok_local // 2
    slot_ids = jnp.arange(slab_max, dtype=jnp.int32)
    cube_index = 0
    cube_flags = visible[cube_index]
    embedded = (
        jnp.dot(voxels[cube_index], patch_weight, preferred_element_type=jnp.float32)
        + patch_bias
        + enc_position.astype(jnp.float32)
    ).astype(jnp.bfloat16)
    ranking = jnp.cumsum(cube_flags) - 1
    slot_index = jnp.where(cube_flags == 1, ranking, slab_max)
    chooser = (slot_index[None, :] == slot_ids[:, None]).astype(jnp.bfloat16)
    kept_rows = jnp.dot(chooser, embedded, preferred_element_type=jnp.float32).astype(jnp.bfloat16)
    present = slot_ids < jnp.sum(cube_flags)
    packed = jnp.dot(
        layer_norm(kept_rows.astype(jnp.float32)).astype(jnp.bfloat16),
        full_project,
        preferred_element_type=jnp.float32,
    ).astype(jnp.bfloat16)
    key_marks = jnp.broadcast_to(present.astype(jnp.bfloat16)[None, :], (seq_count, slab_max))
    outgoing = spread_heads(packed, ENC_HEADS, seq_count)
    incoming = lax.all_to_all(outgoing, "seq", split_axis=0, concat_axis=0, tiled=True)
    in_marks = lax.all_to_all(key_marks, "seq", split_axis=0, concat_axis=0, tiled=True)
    key_ok = in_marks.reshape(-1) > 0.5
    mixed_part = attend_heads(incoming, key_ok, ENC_HEADS, enc_part, enc_parts)
    returning = place_rows(mixed_part, incoming.shape[0] * incoming.shape[1], enc_part, seq_count)
    returned = lax.all_to_all(returning, "seq", split_axis=0, concat_axis=0, tiled=True)
    mixed_rows = collect_heads(returned, ENC_HEADS, enc_parts)
    encoded = kept_rows.astype(jnp.float32) + jnp.dot(
        mixed_rows, full_merge, preferred_element_type=jnp.float32
    )
    lifted_list = [
        jnp.dot(
            layer_norm(encoded).astype(jnp.bfloat16), full_lift, preferred_element_type=jnp.float32
        )
    ]
    rank_list = [ranking]
    dec_weights = (
        lax.all_gather(dec_project, ("dp", "seq"), axis=0, tiled=True),
        lax.all_gather(dec_merge, ("dp", "seq"), axis=0, tiled=True),
        lax.all_gather(dec_predict, ("dp", "seq"), axis=0, tiled=True),
    )
    cube_index = 0
    cube_flags = visible[cube_index]
    taken_rows = jnp.take(
        lifted_list[cube_index], jnp.clip(rank_list[cube_index], 0, slab_max - 1), axis=0
    )
    dec_in = (
        jnp.where(cube_flags[:, None] == 1, taken_rows, mask_token[None, :])
        + dec_position.astype(jnp.float32)
    ).astype(jnp.bfloat16)
    dec_packed = jnp.dot(
        layer_norm(dec_in.astype(jnp.float32)).astype(jnp.bfloat16),
        dec_weights[0],
        preferred_element_type=jnp.float32,
    ).astype(jnp.bfloat16)
    outgoing = spread_heads(dec_packed, DEC_HEADS, seq_count)
    incoming = lax.all_to_all(outgoing, "seq", split_axis=0, concat_axis=0, tiled=True)
    mixed_part = attend_heads(incoming, None, DEC_HEADS, dec_part, dec_parts)
    returning = place_rows(mixed_part, incoming.shape[0] * incoming.shape[1], dec_part, seq_count)
    returned = lax.all_to_all(returning, "seq", split_axis=0, concat_axis=0, tiled=True)
    mixed_rows = collect_heads(returned, DEC_HEADS, dec_parts)
    decoded = (
        dec_in.astype(jnp.float32)
        + jnp.dot(mixed_rows, dec_weights[1], preferred_element_type=jnp.float32)
    ).astype(jnp.bfloat16)
    predicted = jnp.dot(
        layer_norm(decoded.astype(jnp.float32)).astype(jnp.bfloat16),
        dec_weights[2],
        preferred_element_type=jnp.float32,
    )
    target = layer_norm(voxels[cube_index].astype(jnp.float32))
    squared = jnp.mean((predicted - target) * (predicted - target), axis=-1)
    loss_list = [jnp.where(cube_flags == 1, jnp.zeros_like(squared), squared)]
    decoded_list = [decoded]
    return (jnp.stack(decoded_list), jnp.stack(loss_list))


def solution(mesh):
    return jax.shard_map(
        shards,
        mesh=mesh,
        in_specs=(
            P("dp", "seq", None),
            P(),
            P(),
            P("seq", None),
            P("dp", "seq"),
            P(("dp", "seq"), None),
            P(("dp", "seq"), None),
            P(("dp", "seq"), None),
            P(),
            P("seq", None),
            P(("dp", "seq"), None),
            P(("dp", "seq"), None),
            P(("dp", "seq"), None),
        ),
        out_specs=(P("dp", "seq", None), P("dp", "seq")),
        check_vma=False,
    )
```

profile of v0, /device:TPU:32, one launch (start us, length us, event | category | flops | bytes accessed | tf_op | source)
XLA Modules:
  0.0 605.3 jit_solution(10778908084649927215)
XLA Ops:
  7.2 0.7 all-gather.12.cloned.1.call-update
  7.9 0.7 all-gather.16.cloned.1.call-update
  8.7 0.7 all-gather.18.cloned.1.call-update
  9.4 0.8 copy.60
  10.5 1.3 fusion.60
  11.8 0.6 compare_convert_fusion
  12.4 0.6 broadcast_in_dim.98
  13.0 11.4 %all-to-all-start = ((bf16[32,1,64]{2,1,0:T(2,128)(2,1)}), bf16[32,1,64]{2,1,0:T(2,128)(2,1)S(1)}, u32[]{:S(2)}, u32[]{:S(2)}) async-start(bf16[32,1,64]{2,1,0:T(2,128)(2,1)} %broadcast_in_dim.98), calls=%async_computation | async-start | bytes 32768 | tf_op jit(solution)/shard_map/all_to_all | solution.py:135
  24.4 5.2 fusion.61
  29.8 99.7 %all-gather.12.cloned.1.call-done = bf16[256,4,3072]{2,1,0:T(4,128)(2,1)} async-done(((bf16[1,4,3072]{2,1,0:T(4,128)(2,1)}), bf16[256,4,3072]{2,1,0:T(4,128)(2,1)}) %all-gather.12.cloned.1.call-update) | async-done | bytes 6291472 | tf_op jit(solution)/shard_map/all_gather | solution.py:108
  129.5 10.7 %reshape.216 = bf16[1024,3072]{1,0:T(8,128)(2,1)} reshape(bf16[256,4,3072]{2,1,0:T(4,128)(2,1)} %all-gather.12.cloned.1.call-done) | data formatting | bytes 12582912
  140.2 4.0 convolution_convert_fusion
  144.7 0.8 copy.61
  146.0 1.6 copy.62
  147.6 8.5 %all-to-all-start.1 = ((bf16[32,64,192]{2,1,0:T(8,128)(2,1)}), bf16[32,64,192]{2,1,0:T(8,128)(2,1)S(1)}, u32[]{:S(2)}, u32[]{:S(2)}) async-start(bf16[32,64,192]{2,1,0:T(8,128)(2,1)} %copy.62), calls=%async_computation.1 | async-start | bytes 2097152 | tf_op jit(solution)/shard_map/all_to_all | solution.py:134
  156.9 28.0 %all-to-all-done.1 = bf16[32,64,192]{2,1,0:T(8,128)(2,1)S(1)} async-done(((bf16[32,64,192]{2,1,0:T(8,128)(2,1)}), bf16[32,64,192]{2,1,0:T(8,128)(2,1)S(1)}, u32[]{:S(2)}, u32[]{:S(2)}) %all-to-all-start.1) | async-done | bytes 786464 | tf_op jit(solution)/shard_map/all_to_all | solution.py:134
  184.8 1.4 copy.63
  186.2 1.3 reshape.195
  188.4 6.0 while.20
  188.4 0.8 fusion.90
  189.2 0.9 fusion.91
  190.1 1.3 fusion.92
  191.4 0.8 fusion.90
  192.2 0.9 fusion.91
  193.2 1.3 fusion.92
  194.5 0.5 reshape.196
  195.2 1.1 reshape.231
  196.4 5.5 all-to-all-start.2
  201.9 0.5 compare_and_fusion
  202.4 34.0 %all-gather.16.cloned.1.call-done = bf16[256,4,512]{2,1,0:T(4,128)(2,1)} async-done(((bf16[1,4,512]{2,1,0:T(4,128)(2,1)}), bf16[256,4,512]{2,1,0:T(4,128)(2,1)}) %all-gather.16.cloned.1.call-update) | async-done | bytes 1048592 | tf_op jit(solution)/shard_map/all_gather | solution.py:110
  236.4 1.3 reshape.220
  237.8 104.0 %all-gather.18.cloned.1.call-done = bf16[256,2,1536]{2,1,0:T(2,128)(2,1)} async-done(((bf16[1,2,1536]{2,1,0:T(2,128)(2,1)}), bf16[256,2,1536]{2,1,0:T(2,128)(2,1)}) %all-gather.18.cloned.1.call-update) | async-done | bytes 1572880 | tf_op jit(solution)/shard_map/all_gather | solution.py:151
  341.7 4.6 reshape.222
  346.3 102.0 %all-gather.14.cloned.1.call-done = bf16[256,4,1024]{2,1,0:T(4,128)(2,1)} async-done(((bf16[1,4,1024]{2,1,0:T(4,128)(2,1)}), bf16[256,4,1024]{2,1,0:T(4,128)(2,1)}) %all-gather.14.cloned.1.call-update) | async-done | bytes 2097168 | tf_op jit(solution)/shard_map/all_gather | solution.py:109
  448.3 2.5 reshape.218
  450.9 2.2 reshape.232
  453.1 1.2 bitcast_reduce_fusion
  454.2 0.6 fusion.64
  455.4 0.8 gather_fusion
  456.2 0.9 convert_reduce_fusion.1
  458.0 1.0 broadcast_in_dim.104
  459.0 8.1 %all-to-all-start.3 = ((bf16[32,128,96]{1,2,0:T(8,128)(2,1)}), bf16[32,128,96]{1,2,0:T(8,128)(2,1)S(1)}, u32[]{:S(2)}, u32[]{:S(2)}) async-start(bf16[32,128,96]{1,2,0:T(8,128)(2,1)} %bitcast.24), calls=%async_computation.3 | async-start | bytes 1572864 | tf_op jit(solution)/shard_map/all_to_all | solution.py:170
  467.1 0.5 all-gather.20.cloned.1.call-update
  467.7 81.8 %all-gather.4 = bf16[256,2,512]{2,1,0:T(2,128)(2,1)S(1)} all-gather(bf16[1,2,512]{2,1,0:T(2,128)(2,1)S(1)} %bitcast.146), channel_id=1, replica_groups=mesh['dp'=8,'seq'=32] {'dp','seq'}, dimensions={0}, use_global_device_ids=true | all-gather | bytes 526336 | tf_op jit(solution)/shard_map/all_gather | solution.py:152
  550.9 1.3 copy.76
  552.5 20.5 %while.21 = (s32[]{:T(128)}, bf16[4,512,32]{1,2,0:T(8,128)(2,1)S(1)}, bf16[4,512,32]{2,1,0:T(8,128)(2,1)S(1)}, bf16[4096,32]{1,0:T(8,128)(2,1)S(1)}, bf16[4096,32]{1,0:T(8,128)(2,1)}, /*index=5*/s32[]{:T(128)}) while((s32[]{:T(128)}, bf16[4,512,32]{1,2,0:T(8,128)(2,1)S(1)}, bf16[4,512,32]{2,1,0:T(8,128)(2,1)S(1)}, ...), condition=%wide.region_16.17_spmd, body=%wide.region_13.16_spmd.sunk | while | flops 287325184 | bytes 28485736 | solution.py:40
  552.6 1.3 multiply_reduce_fusion.4
  553.9 1.5 fusion.95
  555.4 2.3 fusion.96
  557.7 1.3 multiply_reduce_fusion.4
  559.0 1.5 fusion.95
  560.5 2.3 fusion.96
  562.8 1.3 multiply_reduce_fusion.4
  564.2 1.5 fusion.95
  565.7 2.3 fusion.96
  568.0 1.3 multiply_reduce_fusion.4
  569.3 1.5 fusion.95
  570.8 2.3 fusion.96
  573.2 0.8 copy_bitcast_fusion
  573.9 7.4 %all-to-all-start.4 = ((bf16[32,128,32]{1,2,0:T(8,128)(2,1)}), bf16[32,128,32]{1,2,0:T(8,128)(2,1)S(1)}, u32[]{:S(2)}, u32[]{:S(2)}) async-start(bf16[32,128,32]{1,2,0:T(8,128)(2,1)} %copy_bitcast_fusion), calls=%async_computation.4 | async-start | bytes 524288 | tf_op jit(solution)/shard_map/all_to_all | solution.py:173
  582.0 5.0 all-gather.20.cloned.1.call-done
  587.0 7.2 %reshape.226 = bf16[512,4096]{1,0:T(8,128)(2,1)} reshape(bf16[256,2,4096]{2,1,0:T(2,128)(2,1)} %all-gather.20.cloned.1.call-done) | data formatting | bytes 8388608
  594.8 3.4 fusion.26
  598.2 0.5 bitcast_select_fusion.1
  (82 shorter events, 7.8 us)
Async XLA Ops:
  7.2 122.3 %all-gather.12.cloned.1.call-start = ((), (), s32[]{:S(2)}) async-start(), calls=%async_computation.5 | async-start | bytes 6316032 | tf_op jit(solution)/shard_map/all_gather | solution.py:108
  7.9 228.5 %all-gather.16.cloned.1.call-start = ((), (), s32[]{:S(2)}) async-start(), calls=%async_computation.7 | async-start | bytes 1052672 | tf_op jit(solution)/shard_map/all_gather | solution.py:110
  8.6 333.1 %all-gather.18.cloned.1.call-start = ((), (), s32[]{:S(2)}) async-start(), calls=%async_computation.8 | async-start | bytes 1579008 | tf_op jit(solution)/shard_map/all_gather | solution.py:151
  13.0 134.5 %all-to-all-start = ((bf16[32,1,64]{2,1,0:T(2,128)(2,1)}), bf16[32,1,64]{2,1,0:T(2,128)(2,1)S(1)}, u32[]{:S(2)}, u32[]{:S(2)}) async-start(bf16[32,1,64]{2,1,0:T(2,128)(2,1)} %broadcast_in_dim.98), calls=%async_computation | async-start | bytes 32768 | tf_op jit(solution)/shard_map/all_to_all | solution.py:135
  147.6 37.2 %all-to-all-start.1 = ((bf16[32,64,192]{2,1,0:T(8,128)(2,1)}), bf16[32,64,192]{2,1,0:T(8,128)(2,1)S(1)}, u32[]{:S(2)}, u32[]{:S(2)}) async-start(bf16[32,64,192]{2,1,0:T(8,128)(2,1)} %copy.62), calls=%async_computation.1 | async-start | bytes 2097152 | tf_op jit(solution)/shard_map/all_to_all | solution.py:134
  156.1 292.3 %all-gather.14.cloned.1.call-start = ((), (), s32[]{:S(2)}) async-start(), calls=%async_computation.6 | async-start | bytes 2105344 | tf_op jit(solution)/shard_map/all_gather | solution.py:109
  188.4 13.5 %copy-start.7 = (s32[1,128]{1,0:T(1,128)S(1)}, s32[1,128]{1,0:T(1,128)}, u32[]{:S(2)}) copy-start(s32[1,128]{1,0:T(1,128)} %param.21) | copy-start | bytes 1540
  196.4 254.5 %all-to-all-start.2 = ((bf16[32,2,2048]{2,1,0:T(2,128)(2,1)}), bf16[32,2,2048]{2,1,0:T(2,128)(2,1)}, u32[]{:S(2)}, u32[]{:S(2)}) async-start(bf16[32,2,2048]{2,1,0:T(2,128)(2,1)} %reshape.231), calls=%async_computation.2 | async-start | bytes 524288 | tf_op jit(solution)/shard_map/all_to_all | solution.py:139
  450.9 5.3 copy-start.4
  450.9 5.3 copy-start.5
  454.8 2.4 copy-start.1
  455.4 12.3 %copy-start.6 = (bf16[2,512]{1,0:T(2,128)(2,1)S(1)}, bf16[2,512]{1,0:T(2,128)(2,1)}, u32[]{:S(2)}) copy-start(bf16[2,512]{1,0:T(2,128)(2,1)} %param.28) | copy-start | bytes 6148
  459.0 90.7 %all-to-all-start.3 = ((bf16[32,128,96]{1,2,0:T(8,128)(2,1)}), bf16[32,128,96]{1,2,0:T(8,128)(2,1)S(1)}, u32[]{:S(2)}, u32[]{:S(2)}) async-start(bf16[32,128,96]{1,2,0:T(8,128)(2,1)} %bitcast.24), calls=%async_computation.3 | async-start | bytes 1572864 | tf_op jit(solution)/shard_map/all_to_all | solution.py:170
  467.1 119.9 %all-gather.20.cloned.1.call-start = ((), (), s32[]{:S(2)}) async-start(), calls=%async_computation.9 | async-start | bytes 4210688 | tf_op jit(solution)/shard_map/all_gather | solution.py:153
  552.5 28.8 %copy-start = (bf16[1,128,4096]{2,1,0:T(8,128)(2,1)S(1)}, bf16[1,128,4096]{2,1,0:T(8,128)(2,1)}, u32[]{:S(2)}) copy-start(bf16[1,128,4096]{2,1,0:T(8,128)(2,1)} %param.17) | copy-start | bytes 3145732
  553.9 1.5 copy-start.2
  559.0 1.5 copy-start.2
  564.2 1.5 copy-start.2
  569.3 1.5 copy-start.2
  573.9 20.3 %all-to-all-start.4 = ((bf16[32,128,32]{1,2,0:T(8,128)(2,1)}), bf16[32,128,32]{1,2,0:T(8,128)(2,1)S(1)}, u32[]{:S(2)}, u32[]{:S(2)}) async-start(bf16[32,128,32]{1,2,0:T(8,128)(2,1)} %copy_bitcast_fusion), calls=%async_computation.4 | async-start | bytes 524288 | tf_op jit(solution)/shard_map/all_to_all | solution.py:173
  594.6 3.6 copy-start.3
Sparse Core Ops, SparseCore 0:
  11.8 117.6 all-gather.11
  133.2 103.1 all-gather.15
  240.0 101.7 all-gather.17
  345.3 102.9 all-gather.13
  471.4 115.5 all-gather.19
where the time goes:
time: 610 us; the launch traced here: 605 us
  waiting for transfers between devices  376 us (62%)
  blocking collectives  81.8 us (13%)
  local copies, waits for them, and re-layouts  44.6 us (7%)
  starting transfers between devices  41.2 us (7%)
  matrix products  32.8 us (5%)
  other arithmetic  14.8 us (2%)
  between operations  14.3 us (2%)
    all_gather x1, waiting for transfers between devices, shards(): lax.all_gather(dec_project, ('dp', 'seq'), axis=0, tiled=True)  104 us
    all_gather x1, waiting for transfers between devices, shards(): lax.all_gather(enc_merge, ('dp', 'seq'), axis=0, tiled=True)  102 us
    all_gather x1, waiting for transfers between devices, shards(): lax.all_gather(enc_project, ('dp', 'seq'), axis=0, tiled=True)  99.7 us
    all_gather x1, blocking collectives, shards(): lax.all_gather(dec_merge, ('dp', 'seq'), axis=0, tiled=True)  81.8 us
    all_gather x1, waiting for transfers between devices, shards(): lax.all_gather(dec_lift, ('dp', 'seq'), axis=0, tiled=True)  34 us
    unnamed x22, local copies, waits for them, and re-layouts  29.9 us
    all_to_all x2, waiting for transfers between devices, shards(): lax.all_to_all(outgoing, 'seq', split_axis=0, concat_axis=0, tiled=True)  28 us
    all_to_all x2, starting transfers between devices, shards(): lax.all_to_all(outgoing, 'seq', split_axis=0, concat_axis=0, tiled=True)  16.6 us
  transfers between devices with their start and end apart: 10, of which 6 were waited for; matrix products, arithmetic and copies ran while one was open for 13% of the time, Pallas kernels for 0%

commit v1 on v0

--- a/solution.py
+++ b/solution.py
@@ -81,6 +81,19 @@
     arranged = arranged.reshape(row_count, heads, query_parts, head_size)
     summed = jnp.sum(arranged.astype(jnp.float32), axis=2).astype(jnp.bfloat16)
     return summed.reshape(row_count, heads * head_size)
+
+
+def gather_weights(pieces):
+    flat = jnp.concatenate([piece.reshape(-1) for piece in pieces])
+    every = lax.all_gather(flat, ("dp", "seq"), axis=0, tiled=False)
+    wholes = []
+    start = 0
+    for piece in pieces:
+        size = piece.size
+        part = every[:, start : start + size].reshape(-1, piece.shape[1])
+        wholes.append(part)
+        start += size
+    return wholes
 
 
 def shards(
@@ -104,10 +117,8 @@
     dec_parts = max(seq_count // DEC_HEADS, 1)
     enc_part = seq_place % enc_parts
     dec_part = seq_place % dec_parts
-    full_project, full_merge, full_lift = (
-        lax.all_gather(enc_project, ("dp", "seq"), axis=0, tiled=True),
-        lax.all_gather(enc_merge, ("dp", "seq"), axis=0, tiled=True),
-        lax.all_gather(dec_lift, ("dp", "seq"), axis=0, tiled=True),
+    (full_project, full_merge, full_lift, *dec_weights) = gather_weights(
+        (enc_project, enc_merge, dec_lift, dec_project, dec_merge, dec_predict)
     )
     tok_local = voxels.shape[1]
     slab_max = tok_local // 2
@@ -147,11 +158,6 @@
         )
     ]
     rank_list = [ranking]
-    dec_weights = (
-        lax.all_gather(dec_project, ("dp", "seq"), axis=0, tiled=True),
-        lax.all_gather(dec_merge, ("dp", "seq"), axis=0, tiled=True),
-        lax.all_gather(dec_predict, ("dp", "seq"), axis=0, tiled=True),
-    )
     cube_index = 0
     cube_flags = visible[cube_index]
     taken_rows = jnp.take(

time: 610 us -> 342 us (0.56)
  waiting for transfers between devices: 376 us -> 158 us
  blocking collectives: 81.8 us -> 0 us
  local copies, waits for them, and re-layouts: 44.6 us -> 82 us
    all_gather x5 -> x1, waiting for transfers between devices: 345 us -> 106 us  [gather_weights(): every = lax.all_gather(flat, ('dp', 'seq'), axis=0, tiled=False)]
    all_gather x1 -> x0, blocking collectives: 81.8 us -> none  [shards(): lax.all_gather(dec_merge, ('dp', 'seq'), axis=0, tiled=True)]
    reshape x0 -> x7, local copies, waits for them, and re-layouts: none -> 26.9 us  [the longest x6 26.2 us: gather_weights(): part = every[:, start:start + size].reshape(-1, piece.shape[1])]
    all_to_all x2, waiting for transfers between devices: 28 us -> 50.7 us  [shards(): lax.all_to_all(outgoing, 'seq', split_axis=0, concat_axis=0, tiled=True)]
    unnamed x22 -> x29, local copies, waits for them, and re-layouts: 29.9 us -> 7.48 us
    all_gather x0 -> x1, local copies, waits for them, and re-layouts: none -> 19.3 us  [gather_weights(): every = lax.all_gather(flat, ('dp', 'seq'), axis=0, tiled=False)]
    slice x0 -> x9, local copies, waits for them, and re-layouts: none -> 13.5 us  [gather_weights(): part = every[:, start:start + size].reshape(-1, piece.shape[1])]
  transfers between devices with their start and end apart: 10 -> 6, of which waited for: 6 -> 4; matrix products, arithmetic and copies ran while one was open for 13% -> 23% of each run, Pallas kernels for 0% -> 0%
where the time goes in v1:
time: 342 us; the launch traced here: 340 us
  waiting for transfers between devices  158 us (46%)
  local copies, waits for them, and re-layouts  82 us (24%)
  starting transfers between devices  38.2 us (11%)
  matrix products  32.8 us (10%)
  other arithmetic  14.9 us (4%)
  between operations  14.6 us (4%)
    all_gather x1, waiting for transfers between devices, gather_weights(): every = lax.all_gather(flat, ('dp', 'seq'), axis=0, tiled=False)  106 us
    all_to_all x2, waiting for transfers between devices, shards(): lax.all_to_all(outgoing, 'seq', split_axis=0, concat_axis=0, tiled=True)  50.7 us
    reshape x6, local copies, waits for them, and re-layouts, gather_weights(): part = every[:, start:start + size].reshape(-1, piece.shape[1])  26.2 us
    all_gather x1, local copies, waits for them, and re-layouts, gather_weights(): every = lax.all_gather(flat, ('dp', 'seq'), axis=0, tiled=False)  19.3 us
    all_to_all x2, starting transfers between devices, shards(): lax.all_to_all(outgoing, 'seq', split_axis=0, concat_axis=0, tiled=True)  16.4 us
    slice x9, local copies, waits for them, and re-layouts, gather_weights(): part = every[:, start:start + size].reshape(-1, piece.shape[1])  13.5 us
    dot_general x6, matrix products, one_block(): jnp.einsum('qk,kd->qd', weights, values_one, preferred_element_type=jnp.f...  11.6 us
    all_to_all x1, starting transfers between devices, shards(): lax.all_to_all(key_marks, 'seq', split_axis=0, concat_axis=0, tiled=True)  11.4 us
  transfers between devices with their start and end apart: 6, of which 4 were waited for; matrix products, arithmetic and copies ran while one was open for 23% of the time, Pallas kernels for 0%

profile of v1, /device:TPU:32, one launch (start us, length us, event | category | flops | bytes accessed | tf_op | source)
XLA Modules:
  0.0 340.3 jit_solution(1609906147790389829)
XLA Ops:
  7.2 0.7 copy.90
  8.0 0.7 copy.92
  8.6 0.7 reshape.232
  9.4 0.7 copy.93
  10.0 0.7 copy.94
  10.8 0.7 bitcast_dynamic-update-slice_fusion
  11.5 0.6 copy-done.7
  12.1 0.8 copy.60
  13.2 1.4 fusion.60
  14.6 0.7 compare_convert_fusion
  15.3 0.6 broadcast_in_dim.98
  15.9 11.4 %all-to-all-start = ((bf16[32,1,64]{2,1,0:T(2,128)(2,1)}), bf16[32,1,64]{2,1,0:T(2,128)(2,1)S(1)}, u32[]{:S(2)}, u32[]{:S(2)}) async-start(bf16[32,1,64]{2,1,0:T(2,128)(2,1)} %broadcast_in_dim.98), calls=%async_computation | async-start | bytes 32768 | tf_op jit(solution)/shard_map/all_to_all | solution.py:146
  27.3 5.2 %fusion.61 = (f32[64]{0:T(128)S(1)}, f32[64,1024]{1,0:T(8,128)S(1)}) fusion(bf16[4096,1024]{1,0:T(8,128)(2,1)} %param.18, bf16[1,128,4096]{2,1,0:T(8,128)(2,1)} %param.17, bf16[128,1024]{1,0:T(8,128)(2,1)} %param.20, f32[1024]{0:T(1024)} %param.19, s32[128]{0:T(128)S(1)} %get-tuple-element.145), kind=kOutput, calls=%fused_computation.121 | convolution fusion | flops 1091248128 | bytes 9966336 | tf_op jit(solution)/shard_map/dot_general | solution.py:136
  32.7 106.1 %all-gather.3.cloned.1.call-done = bf16[7864320]{0:T(1024)(128)(2,1)} async-done(((bf16[30720]{0:T(1024)(128)(2,1)}), bf16[7864320]{0:T(1024)(128)(2,1)}) %all-gather.3.cloned.1.call-update) | async-done | bytes 15728656 | tf_op jit(solution)/shard_map/all_gather | solution.py:88
  138.8 19.3 %reshape.263 = bf16[256,30720]{1,0:T(8,128)(2,1)} reshape(bf16[7864320]{0:T(1024)(128)(2,1)} %all-gather.3.cloned.1.call-done) | data formatting | bytes 31457280 | tf_op jit(solution)/shard_map/all_gather | solution.py:88
  158.1 6.1 %slice.50 = bf16[256,12288]{1,0:T(8,128)(2,1)} slice(bf16[256,30720]{1,0:T(8,128)(2,1)} %reshape.263), slice={[0:256], [0:12288]} | slice | bytes 12582912 | tf_op jit(solution)/shard_map/slice | solution.py:93
  164.2 11.1 %reshape.235 = bf16[1024,3072]{1,0:T(8,128)(2,1)} reshape(bf16[256,12288]{1,0:T(8,128)(2,1)} %slice.50) | data formatting | bytes 12582912 | tf_op jit(solution)/shard_map/reshape | solution.py:93
  175.3 4.0 %convolution_convert_fusion = bf16[64,3072]{1,0:T(8,128)(2,1)S(1)} fusion(bf16[1024,3072]{1,0:T(8,128)(2,1)} %reshape.235, f32[64,1024]{1,0:T(8,128)S(1)} %get-tuple-element.147, f32[64]{0:T(128)S(1)} %add_rsqrt_fusion.4, f32[64]{0:T(128)S(1)} %broadcast_multiply_fusion.4), kind=kOutput, calls=%fused_computation.31 | convolution fusion | flops 403046400 | bytes 6947328 | tf_op jit(solution)/shard_map/dot_general | solution.py:138
  179.8 0.8 copy.61
  181.1 1.6 copy.62
  182.7 7.4 %all-to-all-start.1 = ((bf16[32,64,192]{2,1,0:T(8,128)(2,1)}), bf16[32,64,192]{2,1,0:T(8,128)(2,1)S(1)}, u32[]{:S(2)}, u32[]{:S(2)}) async-start(bf16[32,64,192]{2,1,0:T(8,128)(2,1)} %copy.62), calls=%async_computation.1 | async-start | bytes 2097152 | tf_op jit(solution)/shard_map/all_to_all | solution.py:145
  190.3 28.5 %all-to-all-done.1 = bf16[32,64,192]{2,1,0:T(8,128)(2,1)S(1)} async-done(((bf16[32,64,192]{2,1,0:T(8,128)(2,1)}), bf16[32,64,192]{2,1,0:T(8,128)(2,1)S(1)}, u32[]{:S(2)}, u32[]{:S(2)}) %all-to-all-start.1) | async-done | bytes 786464 | tf_op jit(solution)/shard_map/all_to_all | solution.py:145
  218.8 1.4 copy.63
  220.2 1.3 reshape.238
  222.4 6.0 %while.20 = (s32[]{:T(128)}, bf16[2,512,64]{1,2,0:T(8,128)(2,1)S(1)}, pred[2048]{0:T(1024)(128)(4,1)S(1)}, bf16[2,512,64]{2,1,0:T(8,128)(2,1)S(1)}, bf16[2048,64...) while((s32[]{:T(128)}, bf16[2,512,64]{1,2,0:T(8,128)(2,1)S(1)}, ...), condition=%wide.region_7.8_spmd, body=%wide.region_4.7_spmd.sunk | while | flops 281050112 | bytes 13844565 | solution.py:40
  222.4 0.8 fusion.90
  223.2 0.9 fusion.91
  224.1 1.3 fusion.92
  225.4 0.8 fusion.90
  226.2 0.9 fusion.91
  227.2 1.3 fusion.92
  229.3 1.1 reshape.268
  230.4 5.5 %all-to-all-start.2 = ((bf16[32,2,2048]{2,1,0:T(2,128)(2,1)}), bf16[32,2,2048]{2,1,0:T(2,128)(2,1)}, u32[]{:S(2)}, u32[]{:S(2)}) async-start(bf16[32,2,2048]{2,1,0:T(2,128)(2,1)} %reshape.268), calls=%async_computation.2 | async-start | bytes 524288 | tf_op jit(solution)/shard_map/all_to_all | solution.py:150
  236.4 2.8 slice.56
  239.2 2.6 reshape.243
  241.8 1.5 reshape.244
  243.2 3.7 %reshape.245 = bf16[512,1536]{1,0:T(8,128)(2,1)} reshape(bf16[256,3072]{1,0:T(8,128)(2,1)} %slice.56) | data formatting | bytes 3145728 | tf_op jit(solution)/shard_map/reshape | solution.py:93
  246.9 0.9 all-to-all-done.2
  247.8 2.1 reshape.269
  249.9 1.2 bitcast_reduce_fusion
  252.3 0.8 gather_fusion
  253.0 0.9 convert_reduce_fusion.1
  254.8 1.0 broadcast_in_dim.104
  255.8 9.0 %all-to-all-start.3 = ((bf16[32,128,96]{1,2,0:T(8,128)(2,1)}), bf16[32,128,96]{1,2,0:T(8,128)(2,1)S(1)}, u32[]{:S(2)}, u32[]{:S(2)}) async-start(bf16[32,128,96]{1,2,0:T(8,128)(2,1)} %bitcast.20), calls=%async_computation.3 | async-start | bytes 1572864 | tf_op jit(solution)/shard_map/all_to_all | solution.py:176
  264.8 22.2 %all-to-all-done.3 = bf16[32,128,96]{1,2,0:T(8,128)(2,1)S(1)} async-done(((bf16[32,128,96]{1,2,0:T(8,128)(2,1)}), bf16[32,128,96]{1,2,0:T(8,128)(2,1)S(1)}, u32[]{:S(2)}, u32[]{:S(2)}) %all-to-all-start.3) | async-done | bytes 786464 | tf_op jit(solution)/shard_map/all_to_all | solution.py:176
  288.2 1.3 copy.76
  289.8 20.5 %while.21 = (s32[]{:T(128)}, bf16[4,512,32]{1,2,0:T(8,128)(2,1)S(1)}, bf16[4,512,32]{2,1,0:T(8,128)(2,1)S(1)}, bf16[4096,32]{1,0:T(8,128)(2,1)S(1)}, bf16[4096,32]{1,0:T(8,128)(2,1)}, /*index=5*/s32[]{:T(128)}) while((s32[]{:T(128)}, bf16[4,512,32]{1,2,0:T(8,128)(2,1)S(1)}, bf16[4,512,32]{2,1,0:T(8,128)(2,1)S(1)}, ...), condition=%wide.region_16.17_spmd, body=%wide.region_13.16_spmd.sunk | while | flops 287325184 | bytes 28485736 | solution.py:40
  289.9 1.3 multiply_reduce_fusion.4
  291.2 1.5 fusion.95
  292.7 2.3 fusion.96
  295.0 1.3 multiply_reduce_fusion.4
  296.3 1.5 fusion.95
  297.8 2.3 fusion.96
  300.1 1.3 multiply_reduce_fusion.4
  301.5 1.5 fusion.95
  303.0 2.3 fusion.96
  305.3 1.3 multiply_reduce_fusion.4
  306.6 1.5 fusion.95
  308.1 2.3 fusion.96
  310.5 0.8 copy_bitcast_fusion
  311.2 4.9 %all-to-all-start.4 = ((bf16[32,128,32]{1,2,0:T(8,128)(2,1)}), bf16[32,128,32]{1,2,0:T(8,128)(2,1)S(1)}, u32[]{:S(2)}, u32[]{:S(2)}) async-start(bf16[32,128,32]{1,2,0:T(8,128)(2,1)} %copy_bitcast_fusion), calls=%async_computation.4 | async-start | bytes 524288 | tf_op jit(solution)/shard_map/all_to_all | solution.py:179
  316.8 4.7 %slice.61 = bf16[256,8192]{1,0:T(8,128)(2,1)} slice(bf16[256,30720]{1,0:T(8,128)(2,1)} %reshape.263), slice={[0:256], [22528:30720]} | slice | bytes 8388608 | tf_op jit(solution)/shard_map/slice | solution.py:93
  321.7 7.2 %reshape.254 = bf16[512,4096]{1,0:T(8,128)(2,1)} reshape(bf16[256,8192]{1,0:T(8,128)(2,1)} %slice.61) | data formatting | bytes 8388608 | tf_op jit(solution)/shard_map/reshape | solution.py:93
  329.5 3.4 fusion.26
  (94 shorter events, 9.3 us)
Async XLA Ops:
  7.2 131.6 %all-gather.3.cloned.1.call-start = ((), (), s32[]{:S(2)}) async-start(), calls=%async_computation.5 | async-start | bytes 15790080 | tf_op jit(solution)/shard_map/all_gather | solution.py:88
  11.5 0.6 copy-start.7
  15.9 166.8 %all-to-all-start = ((bf16[32,1,64]{2,1,0:T(2,128)(2,1)}), bf16[32,1,64]{2,1,0:T(2,128)(2,1)S(1)}, u32[]{:S(2)}, u32[]{:S(2)}) async-start(bf16[32,1,64]{2,1,0:T(2,128)(2,1)} %broadcast_in_dim.98), calls=%async_computation | async-start | bytes 32768 | tf_op jit(solution)/shard_map/all_to_all | solution.py:146
  182.7 36.1 %all-to-all-start.1 = ((bf16[32,64,192]{2,1,0:T(8,128)(2,1)}), bf16[32,64,192]{2,1,0:T(8,128)(2,1)S(1)}, u32[]{:S(2)}, u32[]{:S(2)}) async-start(bf16[32,64,192]{2,1,0:T(8,128)(2,1)} %copy.62), calls=%async_computation.1 | async-start | bytes 2097152 | tf_op jit(solution)/shard_map/all_to_all | solution.py:145
  222.4 13.5 %copy-start.9 = (s32[1,128]{1,0:T(1,128)S(1)}, s32[1,128]{1,0:T(1,128)}, u32[]{:S(2)}) copy-start(s32[1,128]{1,0:T(1,128)} %param.21) | copy-start | bytes 1540
  230.4 17.4 %all-to-all-start.2 = ((bf16[32,2,2048]{2,1,0:T(2,128)(2,1)}), bf16[32,2,2048]{2,1,0:T(2,128)(2,1)}, u32[]{:S(2)}, u32[]{:S(2)}) async-start(bf16[32,2,2048]{2,1,0:T(2,128)(2,1)} %reshape.268), calls=%async_computation.2 | async-start | bytes 524288 | tf_op jit(solution)/shard_map/all_to_all | solution.py:150
  236.4 2.8 slice-start
  236.4 5.4 %slice-start.1 = ((bf16[256,30720]{1,0:T(8,128)(2,1)}), bf16[256,2048]{1,0:T(8,128)(2,1)S(1)}, s32[]{:S(2)}) async-start(bf16[256,30720]{1,0:T(8,128)(2,1)} %reshape.263), calls=%async_computation.7 | async-start | bytes 2097152 | tf_op jit(solution)/shard_map/slice | solution.py:93
  241.8 9.3 %copy-start.1 = (bf16[1024,1024]{1,0:T(8,128)(2,1)S(1)}, bf16[1024,1024]{1,0:T(8,128)(2,1)}, u32[]{:S(2)}) copy-start(bf16[1024,1024]{1,0:T(8,128)(2,1)} %reshape.243) | copy-start | bytes 6291460
  243.2 8.7 %copy-start.3 = (bf16[1024,512]{1,0:T(8,128)(2,1)S(1)}, bf16[1024,512]{1,0:T(8,128)(2,1)}, u32[]{:S(2)}) copy-start(bf16[1024,512]{1,0:T(8,128)(2,1)} %reshape.244) | copy-start | bytes 3145732
  246.9 6.1 %copy-start.6 = (bf16[128,512]{1,0:T(8,128)(2,1)S(1)}, bf16[128,512]{1,0:T(8,128)(2,1)}, u32[]{:S(2)}) copy-start(bf16[128,512]{1,0:T(8,128)(2,1)} %param.26) | copy-start | bytes 393220
  246.9 6.1 %copy-start.8 = (f32[512]{0:T(512)S(1)}, f32[512]{0:T(512)}, u32[]{:S(2)}) copy-start(f32[512]{0:T(512)} %param.25) | copy-start | bytes 6148
  251.7 2.4 copy-start.2
  255.8 31.2 %all-to-all-start.3 = ((bf16[32,128,96]{1,2,0:T(8,128)(2,1)}), bf16[32,128,96]{1,2,0:T(8,128)(2,1)S(1)}, u32[]{:S(2)}, u32[]{:S(2)}) async-start(bf16[32,128,96]{1,2,0:T(8,128)(2,1)} %bitcast.20), calls=%async_computation.3 | async-start | bytes 1572864 | tf_op jit(solution)/shard_map/all_to_all | solution.py:176
  289.8 26.3 %copy-start = (bf16[1,128,4096]{2,1,0:T(8,128)(2,1)S(1)}, bf16[1,128,4096]{2,1,0:T(8,128)(2,1)}, u32[]{:S(2)}) copy-start(bf16[1,128,4096]{2,1,0:T(8,128)(2,1)} %param.17) | copy-start | bytes 3145732
  291.2 1.5 copy-start.4
  296.3 1.5 copy-start.4
  301.5 1.5 copy-start.4
  306.6 1.5 copy-start.4
  311.2 17.7 %all-to-all-start.4 = ((bf16[32,128,32]{1,2,0:T(8,128)(2,1)}), bf16[32,128,32]{1,2,0:T(8,128)(2,1)S(1)}, u32[]{:S(2)}, u32[]{:S(2)}) async-start(bf16[32,128,32]{1,2,0:T(8,128)(2,1)} %copy_bitcast_fusion), calls=%async_computation.4 | async-start | bytes 524288 | tf_op jit(solution)/shard_map/all_to_all | solution.py:179
  316.8 4.7 %slice-start.2 = ((bf16[256,30720]{1,0:T(8,128)(2,1)}), bf16[256,1024]{1,0:T(8,128)(2,1)S(1)}, s32[]{:S(2)}) async-start(bf16[256,30720]{1,0:T(8,128)(2,1)} %reshape.263), calls=%async_computation.8 | async-start | bytes 1048576 | tf_op jit(solution)/shard_map/slice | solution.py:93
  329.3 3.6 %copy-start.5 = (bf16[128,512]{1,0:T(8,128)(2,1)}, bf16[128,512]{1,0:T(8,128)(2,1)S(1)}, u32[]{:S(2)}) copy-start(bf16[128,512]{1,0:T(8,128)(2,1)S(1)} %get-tuple-element.151) | copy-start | bytes 393220
Sparse Core Ops, SparseCore 0:
  12.4 126.3 all-gather.2

commit v2 on v1

--- a/solution.py
+++ b/solution.py
@@ -85,15 +85,22 @@
 
 def gather_weights(pieces):
     flat = jnp.concatenate([piece.reshape(-1) for piece in pieces])
-    every = lax.all_gather(flat, ("dp", "seq"), axis=0, tiled=False)
+    every = lax.all_gather(flat, ("dp", "seq"), axis=0, tiled=True)
+    lane = 128
+    sources = every.shape[0] // flat.shape[0]
+    tiles = every.reshape(sources, flat.shape[0] // lane, lane)
     wholes = []
     start = 0
     for piece in pieces:
         size = piece.size
-        part = every[:, start : start + size].reshape(-1, piece.shape[1])
-        wholes.append(part)
+        part = tiles[:, start // lane : (start + size) // lane, :]
+        wholes.append(part.reshape(sources * piece.shape[0], piece.shape[1]))
         start += size
     return wholes
+
+
+def weight_dot(rows, weight):
+    return jnp.dot(rows, weight, preferred_element_type=jnp.float32)
 
 
 def shards(
@@ -135,10 +142,8 @@
     chooser = (slot_index[None, :] == slot_ids[:, None]).astype(jnp.bfloat16)
     kept_rows = jnp.dot(chooser, embedded, preferred_element_type=jnp.float32).astype(jnp.bfloat16)
     present = slot_ids < jnp.sum(cube_flags)
-    packed = jnp.dot(
-        layer_norm(kept_rows.astype(jnp.float32)).astype(jnp.bfloat16),
-        full_project,
-        preferred_element_type=jnp.float32,
+    packed = weight_dot(
+        layer_norm(kept_rows.astype(jnp.float32)).astype(jnp.bfloat16), full_project
     ).astype(jnp.bfloat16)
     key_marks = jnp.broadcast_to(present.astype(jnp.bfloat16)[None, :], (seq_count, slab_max))
     outgoing = spread_heads(packed, ENC_HEADS, seq_count)
@@ -149,13 +154,9 @@
     returning = place_rows(mixed_part, incoming.shape[0] * incoming.shape[1], enc_part, seq_count)
     returned = lax.all_to_all(returning, "seq", split_axis=0, concat_axis=0, tiled=True)
     mixed_rows = collect_heads(returned, ENC_HEADS, enc_parts)
-    encoded = kept_rows.astype(jnp.float32) + jnp.dot(
-        mixed_rows, full_merge, preferred_element_type=jnp.float32
-    )
+    encoded = kept_rows.astype(jnp.float32) + weight_dot(mixed_rows, full_merge)
     lifted_list = [
-        jnp.dot(
-            layer_norm(encoded).astype(jnp.bfloat16), full_lift, preferred_element_type=jnp.float32
-        )
+        weight_dot(layer_norm(encoded).astype(jnp.bfloat16), full_lift)
     ]
     rank_list = [ranking]
     cube_index = 0
@@ -167,10 +168,8 @@
         jnp.where(cube_flags[:, None] == 1, taken_rows, mask_token[None, :])
         + dec_position.astype(jnp.float32)
     ).astype(jnp.bfloat16)
-    dec_packed = jnp.dot(
-        layer_norm(dec_in.astype(jnp.float32)).astype(jnp.bfloat16),
-        dec_weights[0],
-        preferred_element_type=jnp.float32,
+    dec_packed = weight_dot(
+        layer_norm(dec_in.astype(jnp.float32)).astype(jnp.bfloat16), dec_weights[0]
     ).astype(jnp.bfloat16)
     outgoing = spread_heads(dec_packed, DEC_HEADS, seq_count)
     incoming = lax.all_to_all(outgoing, "seq", split_axis=0, concat_axis=0, tiled=True)
@@ -180,13 +179,9 @@
     mixed_rows = collect_heads(returned, DEC_HEADS, dec_parts)
     decoded = (
         dec_in.astype(jnp.float32)
-        + jnp.dot(mixed_rows, dec_weights[1], preferred_element_type=jnp.float32)
-    ).astype(jnp.bfloat16)
-    predicted = jnp.dot(
-        layer_norm(decoded.astype(jnp.float32)).astype(jnp.bfloat16),
-        dec_weights[2],
-        preferred_element_type=jnp.float32,
-    )
+        + weight_dot(mixed_rows, dec_weights[1])
+    ).astype(jnp.bfloat16)
+    predicted = weight_dot(layer_norm(decoded.astype(jnp.float32)).astype(jnp.bfloat16), dec_weights[2])
     target = layer_norm(voxels[cube_index].astype(jnp.float32))
     squared = jnp.mean((predicted - target) * (predicted - target), axis=-1)
     loss_list = [jnp.where(cube_flags == 1, jnp.zeros_like(squared), squared)]

time: 342 us -> 331 us (0.968)
  local copies, waits for them, and re-layouts: 82 us -> 71.2 us
    all_gather x1 -> x0, local copies, waits for them, and re-layouts: 19.3 us -> none  [gather_weights(): every = lax.all_gather(flat, ('dp', 'seq'), axis=0, tiled=False)]
    slice x9 -> x6, local copies, waits for them, and re-layouts: 13.5 us -> 21.5 us  [gather_weights(): part = tiles[:, start // lane:(start + size) // lane, :]]
    unnamed x29 -> x25, local copies, waits for them, and re-layouts: 7.48 us -> 7.49 us
  transfers between devices with their start and end apart: 6 -> 6, of which waited for: 4 -> 3; matrix products, arithmetic and copies ran while one was open for 23% -> 20% of each run, Pallas kernels for 0% -> 0%
where the time goes in v2:
time: 331 us; the launch traced here: 329 us
  waiting for transfers between devices  157 us (47%)
  local copies, waits for them, and re-layouts  71.2 us (22%)
  starting transfers between devices  39 us (12%)
  matrix products  32.9 us (10%)
  other arithmetic  14.8 us (4%)
  between operations  14.5 us (4%)
    all_gather x1, waiting for transfers between devices, gather_weights(): every = lax.all_gather(flat, ('dp', 'seq'), axis=0, tiled=True)  106 us
    all_to_all x2, waiting for transfers between devices, shards(): lax.all_to_all(outgoing, 'seq', split_axis=0, concat_axis=0, tiled=True)  50.7 us
    reshape x6, local copies, waits for them, and re-layouts, gather_weights(): wholes.append(part.reshape(sources * piece.shape[0], piece.shape[1]))  26.7 us
    slice x6, local copies, waits for them, and re-layouts, gather_weights(): part = tiles[:, start // lane:(start + size) // lane, :]  21.5 us
    all_to_all x2, starting transfers between devices, shards(): lax.all_to_all(outgoing, 'seq', split_axis=0, concat_axis=0, tiled=True)  17.2 us
    dot_general x6, matrix products, one_block(): jnp.einsum('qk,kd->qd', weights, values_one, preferred_element_type=jnp.f...  11.6 us
    all_to_all x1, starting transfers between devices, shards(): lax.all_to_all(key_marks, 'seq', split_axis=0, concat_axis=0, tiled=True)  11.4 us
    all_to_all x2, starting transfers between devices, shards(): lax.all_to_all(returning, 'seq', split_axis=0, concat_axis=0, tiled=True)  10.4 us
  transfers between devices with their start and end apart: 6, of which 3 were waited for; matrix products, arithmetic and copies ran while one was open for 20% of the time, Pallas kernels for 0%

profile of v2, /device:TPU:32, one launch (start us, length us, event | category | flops | bytes accessed | tf_op | source)
XLA Modules:
  0.0 329.4 jit_solution(9431051390930105412)
XLA Ops:
  7.2 0.7 copy.90
  8.0 0.7 copy.92
  8.6 0.7 reshape.235
  9.4 0.7 copy.93
  10.0 0.7 copy.94
  10.8 0.7 bitcast_dynamic-update-slice_fusion
  11.5 0.6 copy-done.5
  12.1 0.8 copy.60
  13.2 1.3 fusion.60
  14.5 0.6 compare_convert_fusion
  15.8 11.4 %all-to-all-start = ((bf16[32,1,64]{2,1,0:T(2,128)(2,1)}), bf16[32,1,64]{2,1,0:T(2,128)(2,1)S(1)}, u32[]{:S(2)}, u32[]{:S(2)}) async-start(bf16[32,1,64]{2,1,0:T(2,128)(2,1)} %broadcast_in_dim.98), calls=%async_computation | async-start | bytes 32768 | tf_op jit(solution)/shard_map/all_to_all | solution.py:151
  27.2 5.2 %fusion.61 = (f32[64]{0:T(128)S(1)}, f32[64,1024]{1,0:T(8,128)S(1)}) fusion(bf16[4096,1024]{1,0:T(8,128)(2,1)} %param.18, bf16[1,128,4096]{2,1,0:T(8,128)(2,1)} %param.17, bf16[128,1024]{1,0:T(8,128)(2,1)} %param.20, f32[1024]{0:T(1024)} %param.19, s32[128]{0:T(128)S(1)} %get-tuple-element.145), kind=kOutput, calls=%fused_computation.121 | convolution fusion | flops 1091248128 | bytes 9966336 | tf_op jit(solution)/shard_map/dot_general | solution.py:143
  32.6 106.2 %all-gather.2.cloned.1.call-done = bf16[7864320]{0:T(1024)(128)(2,1)} async-done(((bf16[30720]{0:T(1024)(128)(2,1)}), bf16[7864320]{0:T(1024)(128)(2,1)}) %all-gather.2.cloned.1.call-update) | async-done | bytes 15728656 | tf_op jit(solution)/shard_map/all_gather | solution.py:88
  138.8 6.6 %slice.50 = bf16[256,96,128]{2,1,0:T(8,128)(2,1)} slice(bf16[256,240,128]{2,1,0:T(8,128)(2,1)} %bitcast.135), slice={[0:256], [0:96], [0:128]} | slice | bytes 12582912 | tf_op jit(solution)/shard_map/slice | solution.py:96
  145.4 10.3 %reshape.239 = bf16[1024,3072]{1,0:T(8,128)(2,1)} reshape(bf16[256,96,128]{2,1,0:T(8,128)(2,1)} %slice.50) | data formatting | bytes 12582912 | tf_op jit(solution)/shard_map/reshape | solution.py:97
  155.7 4.0 %convolution_convert_fusion = bf16[64,3072]{1,0:T(8,128)(2,1)S(1)} fusion(bf16[1024,3072]{1,0:T(8,128)(2,1)} %reshape.239, f32[64,1024]{1,0:T(8,128)S(1)} %get-tuple-element.147, f32[64]{0:T(128)S(1)} %add_rsqrt_fusion.4, f32[64]{0:T(128)S(1)} %broadcast_multiply_fusion.4), kind=kOutput, calls=%fused_computation.31 | convolution fusion | flops 403046400 | bytes 6947328 | tf_op jit(solution)/shard_map/dot_general | solution.py:103
  160.2 0.8 copy.61
  161.5 1.6 copy.62
  163.1 7.4 %all-to-all-start.1 = ((bf16[32,64,192]{2,1,0:T(8,128)(2,1)}), bf16[32,64,192]{2,1,0:T(8,128)(2,1)S(1)}, u32[]{:S(2)}, u32[]{:S(2)}) async-start(bf16[32,64,192]{2,1,0:T(8,128)(2,1)} %copy.62), calls=%async_computation.1 | async-start | bytes 2097152 | tf_op jit(solution)/shard_map/all_to_all | solution.py:150
  170.7 28.5 %all-to-all-done.1 = bf16[32,64,192]{2,1,0:T(8,128)(2,1)S(1)} async-done(((bf16[32,64,192]{2,1,0:T(8,128)(2,1)}), bf16[32,64,192]{2,1,0:T(8,128)(2,1)S(1)}, u32[]{:S(2)}, u32[]{:S(2)}) %all-to-all-start.1) | async-done | bytes 786464 | tf_op jit(solution)/shard_map/all_to_all | solution.py:150
  199.2 1.4 copy.63
  200.7 1.3 reshape.242
  202.8 6.0 %while.20 = (s32[]{:T(128)}, bf16[2,512,64]{1,2,0:T(8,128)(2,1)S(1)}, pred[2048]{0:T(1024)(128)(4,1)S(1)}, bf16[2,512,64]{2,1,0:T(8,128)(2,1)S(1)}, bf16[2048,64...) while((s32[]{:T(128)}, bf16[2,512,64]{1,2,0:T(8,128)(2,1)S(1)}, ...), condition=%wide.region_7.8_spmd, body=%wide.region_4.7_spmd.sunk | while | flops 281050112 | bytes 13844565 | solution.py:40
  202.8 0.8 fusion.90
  203.6 0.9 fusion.91
  204.6 1.3 fusion.92
  205.8 0.8 fusion.90
  206.6 0.9 fusion.91
  207.6 1.3 fusion.92
  209.7 1.1 reshape.271
  210.8 5.5 %all-to-all-start.2 = ((bf16[32,2,2048]{2,1,0:T(2,128)(2,1)}), bf16[32,2,2048]{2,1,0:T(2,128)(2,1)}, u32[]{:S(2)}, u32[]{:S(2)}) async-start(bf16[32,2,2048]{2,1,0:T(2,128)(2,1)} %reshape.271), calls=%async_computation.2 | async-start | bytes 524288 | tf_op jit(solution)/shard_map/all_to_all | solution.py:155
  216.8 3.3 %slice.54 = bf16[256,32,128]{2,1,0:T(8,128)(2,1)} slice(bf16[256,240,128]{2,1,0:T(8,128)(2,1)} %bitcast.136), slice={[0:256], [96:128], [0:128]} | slice | bytes 4194304 | tf_op jit(solution)/shard_map/slice | solution.py:96
  220.2 2.4 slice.55
  222.6 2.9 slice.56
  225.5 2.8 reshape.247
  228.3 1.7 reshape.248
  230.0 4.3 %reshape.249 = bf16[512,1536]{1,0:T(8,128)(2,1)} reshape(bf16[256,24,128]{2,1,0:T(8,128)(2,1)} %slice.56) | data formatting | bytes 3145728 | tf_op jit(solution)/shard_map/reshape | solution.py:97
  234.3 2.2 reshape.272
  236.5 1.2 bitcast_reduce_fusion
  238.8 0.8 gather_fusion
  239.6 0.9 convert_reduce_fusion.1
  241.3 1.0 broadcast_in_dim.104
  242.4 9.8 %all-to-all-start.3 = ((bf16[32,128,96]{1,2,0:T(8,128)(2,1)}), bf16[32,128,96]{1,2,0:T(8,128)(2,1)S(1)}, u32[]{:S(2)}, u32[]{:S(2)}) async-start(bf16[32,128,96]{1,2,0:T(8,128)(2,1)} %bitcast.21), calls=%async_computation.3 | async-start | bytes 1572864 | tf_op jit(solution)/shard_map/all_to_all | solution.py:175
  252.2 22.2 %all-to-all-done.3 = bf16[32,128,96]{1,2,0:T(8,128)(2,1)S(1)} async-done(((bf16[32,128,96]{1,2,0:T(8,128)(2,1)}), bf16[32,128,96]{1,2,0:T(8,128)(2,1)S(1)}, u32[]{:S(2)}, u32[]{:S(2)}) %all-to-all-start.3) | async-done | bytes 786464 | tf_op jit(solution)/shard_map/all_to_all | solution.py:175
  275.6 1.3 copy.76
  277.2 20.5 %while.21 = (s32[]{:T(128)}, bf16[4,512,32]{1,2,0:T(8,128)(2,1)S(1)}, bf16[4,512,32]{2,1,0:T(8,128)(2,1)S(1)}, bf16[4096,32]{1,0:T(8,128)(2,1)S(1)}, bf16[4096,32]{1,0:T(8,128)(2,1)}, /*index=5*/s32[]{:T(128)}) while((s32[]{:T(128)}, bf16[4,512,32]{1,2,0:T(8,128)(2,1)S(1)}, bf16[4,512,32]{2,1,0:T(8,128)(2,1)S(1)}, ...), condition=%wide.region_16.17_spmd, body=%wide.region_13.16_spmd.sunk | while | flops 287325184 | bytes 28485736 | solution.py:40
  277.2 1.3 multiply_reduce_fusion.4
  278.6 1.5 fusion.95
  280.1 2.3 fusion.96
  282.4 1.3 multiply_reduce_fusion.4
  283.7 1.5 fusion.95
  285.2 2.3 fusion.96
  287.5 1.3 multiply_reduce_fusion.4
  288.8 1.5 fusion.95
  290.3 2.3 fusion.96
  292.6 1.3 multiply_reduce_fusion.4
  294.0 1.5 fusion.95
  295.5 2.3 fusion.96
  297.8 0.8 copy_bitcast_fusion
  298.6 4.9 %all-to-all-start.4 = ((bf16[32,128,32]{1,2,0:T(8,128)(2,1)}), bf16[32,128,32]{1,2,0:T(8,128)(2,1)S(1)}, u32[]{:S(2)}, u32[]{:S(2)}) async-start(bf16[32,128,32]{1,2,0:T(8,128)(2,1)} %copy_bitcast_fusion), calls=%async_computation.4 | async-start | bytes 524288 | tf_op jit(solution)/shard_map/all_to_all | solution.py:178
  304.2 1.1 slice.60
  305.3 5.2 %slice.61 = bf16[256,64,128]{2,1,0:T(8,128)(2,1)} slice(bf16[256,240,128]{2,1,0:T(8,128)(2,1)} %bitcast.140), slice={[0:256], [176:240], [0:128]} | slice | bytes 8388608 | tf_op jit(solution)/shard_map/slice | solution.py:96
  310.8 7.3 %reshape.258 = bf16[512,4096]{1,0:T(8,128)(2,1)} reshape(bf16[256,64,128]{2,1,0:T(8,128)(2,1)} %slice.61) | data formatting | bytes 8388608 | tf_op jit(solution)/shard_map/reshape | solution.py:97
  318.7 3.4 %fusion.26 = f32[128]{0:T(128)S(1)} fusion(bf16[512,4096]{1,0:T(8,128)(2,1)} %reshape.258, bf16[1,128,4096]{2,1,0:T(8,128)(2,1)S(1)} %copy-done, f32[128]{0:T(128)S(1)} %get-tuple-element.152, f32[128]{0:T(128)S(1)} %broadcast_multiply_fusion, bf16[128,512]{1,0:T(8,128)(2,1)S(1)} %get-tuple-element.151, f32[128]{0:T(128)S(1)} %get-tuple-element.153, ...), kind=kOutput, calls=%fused_computation.38 | convolution fusion | flops 540278656 | bytes 5376512 | tf_op jit(solution)/shard_map/dot_general | solution.py:103
  (86 shorter events, 10.0 us)
Async XLA Ops:
  7.2 131.6 %all-gather.2.cloned.1.call-start = ((), (), s32[]{:S(2)}) async-start(), calls=%async_computation.5 | async-start | bytes 15790080 | tf_op jit(solution)/shard_map/all_gather | solution.py:88
  11.5 0.6 copy-start.5
  15.8 147.3 %all-to-all-start = ((bf16[32,1,64]{2,1,0:T(2,128)(2,1)}), bf16[32,1,64]{2,1,0:T(2,128)(2,1)S(1)}, u32[]{:S(2)}, u32[]{:S(2)}) async-start(bf16[32,1,64]{2,1,0:T(2,128)(2,1)} %broadcast_in_dim.98), calls=%async_computation | async-start | bytes 32768 | tf_op jit(solution)/shard_map/all_to_all | solution.py:151
  163.1 36.1 %all-to-all-start.1 = ((bf16[32,64,192]{2,1,0:T(8,128)(2,1)}), bf16[32,64,192]{2,1,0:T(8,128)(2,1)S(1)}, u32[]{:S(2)}, u32[]{:S(2)}) async-start(bf16[32,64,192]{2,1,0:T(8,128)(2,1)} %copy.62), calls=%async_computation.1 | async-start | bytes 2097152 | tf_op jit(solution)/shard_map/all_to_all | solution.py:150
  202.8 13.5 %copy-start.7 = (s32[1,128]{1,0:T(1,128)S(1)}, s32[1,128]{1,0:T(1,128)}, u32[]{:S(2)}) copy-start(s32[1,128]{1,0:T(1,128)} %param.21) | copy-start | bytes 1540
  210.8 23.5 %all-to-all-start.2 = ((bf16[32,2,2048]{2,1,0:T(2,128)(2,1)}), bf16[32,2,2048]{2,1,0:T(2,128)(2,1)}, u32[]{:S(2)}, u32[]{:S(2)}) async-start(bf16[32,2,2048]{2,1,0:T(2,128)(2,1)} %reshape.271), calls=%async_computation.2 | async-start | bytes 524288 | tf_op jit(solution)/shard_map/all_to_all | solution.py:155
  234.3 5.3 %copy-start.4 = (bf16[128,512]{1,0:T(8,128)(2,1)S(1)}, bf16[128,512]{1,0:T(8,128)(2,1)}, u32[]{:S(2)}) copy-start(bf16[128,512]{1,0:T(8,128)(2,1)} %param.26) | copy-start | bytes 393220
  234.3 5.3 %copy-start.6 = (f32[512]{0:T(512)S(1)}, f32[512]{0:T(512)}, u32[]{:S(2)}) copy-start(f32[512]{0:T(512)} %param.25) | copy-start | bytes 6148
  238.2 2.4 copy-start.1
  242.4 32.0 %all-to-all-start.3 = ((bf16[32,128,96]{1,2,0:T(8,128)(2,1)}), bf16[32,128,96]{1,2,0:T(8,128)(2,1)S(1)}, u32[]{:S(2)}, u32[]{:S(2)}) async-start(bf16[32,128,96]{1,2,0:T(8,128)(2,1)} %bitcast.21), calls=%async_computation.3 | async-start | bytes 1572864 | tf_op jit(solution)/shard_map/all_to_all | solution.py:175
  277.2 26.3 %copy-start = (bf16[1,128,4096]{2,1,0:T(8,128)(2,1)S(1)}, bf16[1,128,4096]{2,1,0:T(8,128)(2,1)}, u32[]{:S(2)}) copy-start(bf16[1,128,4096]{2,1,0:T(8,128)(2,1)} %param.17) | copy-start | bytes 3145732
  278.6 1.5 copy-start.2
  283.7 1.5 copy-start.2
  288.8 1.5 copy-start.2
  294.0 1.5 copy-start.2
  298.6 19.5 %all-to-all-start.4 = ((bf16[32,128,32]{1,2,0:T(8,128)(2,1)}), bf16[32,128,32]{1,2,0:T(8,128)(2,1)S(1)}, u32[]{:S(2)}, u32[]{:S(2)}) async-start(bf16[32,128,32]{1,2,0:T(8,128)(2,1)} %copy_bitcast_fusion), calls=%async_computation.4 | async-start | bytes 524288 | tf_op jit(solution)/shard_map/all_to_all | solution.py:178
  318.5 3.6 %copy-start.3 = (bf16[128,512]{1,0:T(8,128)(2,1)}, bf16[128,512]{1,0:T(8,128)(2,1)S(1)}, u32[]{:S(2)}) copy-start(bf16[128,512]{1,0:T(8,128)(2,1)S(1)} %get-tuple-element.151) | copy-start | bytes 393220
Sparse Core Ops, SparseCore 0:
  12.4 126.3 all-gather.1

commit v3 on v2

--- a/solution.py
+++ b/solution.py
@@ -148,6 +148,9 @@
     key_marks = jnp.broadcast_to(present.astype(jnp.bfloat16)[None, :], (seq_count, slab_max))
     outgoing = spread_heads(packed, ENC_HEADS, seq_count)
     incoming = lax.all_to_all(outgoing, "seq", split_axis=0, concat_axis=0, tiled=True)
+    incoming, full_merge, full_lift, dec_weights[0] = lax.optimization_barrier(
+        (incoming, full_merge, full_lift, dec_weights[0])
+    )
     in_marks = lax.all_to_all(key_marks, "seq", split_axis=0, concat_axis=0, tiled=True)
     key_ok = in_marks.reshape(-1) > 0.5
     mixed_part = attend_heads(incoming, key_ok, ENC_HEADS, enc_part, enc_parts)
@@ -173,6 +176,9 @@
     ).astype(jnp.bfloat16)
     outgoing = spread_heads(dec_packed, DEC_HEADS, seq_count)
     incoming = lax.all_to_all(outgoing, "seq", split_axis=0, concat_axis=0, tiled=True)
+    incoming, dec_weights[1], dec_weights[2] = lax.optimization_barrier(
+        (incoming, dec_weights[1], dec_weights[2])
+    )
     mixed_part = attend_heads(incoming, None, DEC_HEADS, dec_part, dec_parts)
     returning = place_rows(mixed_part, incoming.shape[0] * incoming.shape[1], dec_part, seq_count)
     returned = lax.all_to_all(returning, "seq", split_axis=0, concat_axis=0, tiled=True)

time: 331 us -> 322 us (0.973)
  waiting for transfers between devices: 157 us -> 147 us
  local copies, waits for them, and re-layouts: 71.2 us -> 77.6 us
  starting transfers between devices: 39 us -> 33.7 us
    all_to_all x2, waiting for transfers between devices: 50.7 us -> 18.4 us  [shards(): lax.all_to_all(outgoing, 'seq', split_axis=0, concat_axis=0, tiled=True)]
    all_to_all x2, waiting for transfers between devices: 0.01 us -> 22.3 us  [shards(): lax.all_to_all(returning, 'seq', split_axis=0, concat_axis=0, tiled=True)]
    all_to_all x2, starting transfers between devices: 17.2 us -> 12 us  [shards(): lax.all_to_all(outgoing, 'seq', split_axis=0, concat_axis=0, tiled=True)]
    optimization_barrier x0 -> x2, local copies, waits for them, and re-layouts: none -> 3.5 us  [the longest x1 3.19 us: shards(): lax.optimization_barrier((incoming, full_merge, full_lift, dec_weights[0]))]
  transfers between devices with their start and end apart: 6 -> 6, of which waited for: 3 -> 5; matrix products, arithmetic and copies ran while one was open for 20% -> 21% of each run, Pallas kernels for 0% -> 0%
where the time goes in v3:
time: 322 us; the launch traced here: 320 us
  waiting for transfers between devices  147 us (46%)
  local copies, waits for them, and re-layouts  77.6 us (24%)
  matrix products  34.2 us (11%)
  starting transfers between devices  33.7 us (10%)
  between operations  14.5 us (5%)
  other arithmetic  12.6 us (4%)
    all_gather x1, waiting for transfers between devices, gather_weights(): every = lax.all_gather(flat, ('dp', 'seq'), axis=0, tiled=True)  106 us
    reshape x6, local copies, waits for them, and re-layouts, gather_weights(): wholes.append(part.reshape(sources * piece.shape[0], piece.shape[1]))  27.5 us
    all_to_all x2, waiting for transfers between devices, shards(): lax.all_to_all(returning, 'seq', split_axis=0, concat_axis=0, tiled=True)  22.3 us
    slice x6, local copies, waits for them, and re-layouts, gather_weights(): part = tiles[:, start // lane:(start + size) // lane, :]  21.5 us
    all_to_all x2, waiting for transfers between devices, shards(): lax.all_to_all(outgoing, 'seq', split_axis=0, concat_axis=0, tiled=True)  18.4 us
    all_to_all x2, starting transfers between devices, shards(): lax.all_to_all(outgoing, 'seq', split_axis=0, concat_axis=0, tiled=True)  12 us
    dot_general x6, matrix products, one_block(): jnp.einsum('qk,kd->qd', weights, values_one, preferred_element_type=jnp.f...  11.6 us
    all_to_all x1, starting transfers between devices, shards(): lax.all_to_all(key_marks, 'seq', split_axis=0, concat_axis=0, tiled=True)  11.4 us
  transfers between devices with their start and end apart: 6, of which 5 were waited for; matrix products, arithmetic and copies ran while one was open for 21% of the time, Pallas kernels for 0%

profile of v3, /device:TPU:32, one launch (start us, length us, event | category | flops | bytes accessed | tf_op | source)
XLA Modules:
  0.0 319.8 jit_solution(12365643308890750605)
XLA Ops:
  7.2 0.7 copy.90
  8.0 0.7 copy.92
  8.6 0.7 reshape.235
  10.0 0.7 copy.94
  10.8 0.7 bitcast_dynamic-update-slice_fusion
  12.1 0.8 copy.60
  13.2 1.3 fusion.60
  15.8 11.4 %all-to-all-start = ((bf16[32,1,64]{2,1,0:T(2,128)(2,1)}), bf16[32,1,64]{2,1,0:T(2,128)(2,1)S(1)}, u32[]{:S(2)}, u32[]{:S(2)}) async-start(bf16[32,1,64]{2,1,0:T(2,128)(2,1)} %broadcast_in_dim.98), calls=%async_computation | async-start | bytes 32768 | tf_op jit(solution)/shard_map/all_to_all | solution.py:154
  27.2 5.2 %fusion.61 = (f32[64]{0:T(128)S(1)}, f32[64,1024]{1,0:T(8,128)S(1)}) fusion(bf16[4096,1024]{1,0:T(8,128)(2,1)} %param.18, bf16[1,128,4096]{2,1,0:T(8,128)(2,1)} %param.17, bf16[128,1024]{1,0:T(8,128)(2,1)} %param.20, f32[1024]{0:T(1024)} %param.19, s32[128]{0:T(128)S(1)} %get-tuple-element.159), kind=kOutput, calls=%fused_computation.121 | convolution fusion | flops 1091248128 | bytes 9966336 | tf_op jit(solution)/shard_map/dot_general | solution.py:143
  32.6 106.2 %all-gather.2.cloned.1.call-done = bf16[7864320]{0:T(1024)(128)(2,1)} async-done(((bf16[30720]{0:T(1024)(128)(2,1)}), bf16[7864320]{0:T(1024)(128)(2,1)}) %all-gather.2.cloned.1.call-update) | async-done | bytes 15728656 | tf_op jit(solution)/shard_map/all_gather | solution.py:88
  138.8 6.6 %slice.50 = bf16[256,96,128]{2,1,0:T(8,128)(2,1)} slice(bf16[256,240,128]{2,1,0:T(8,128)(2,1)} %bitcast.135), slice={[0:256], [0:96], [0:128]} | slice | bytes 12582912 | tf_op jit(solution)/shard_map/slice | solution.py:96
  145.4 10.3 %reshape.239 = bf16[1024,3072]{1,0:T(8,128)(2,1)} reshape(bf16[256,96,128]{2,1,0:T(8,128)(2,1)} %slice.50) | data formatting | bytes 12582912 | tf_op jit(solution)/shard_map/reshape | solution.py:97
  155.7 4.0 %convolution_convert_fusion = bf16[64,3072]{1,0:T(8,128)(2,1)S(1)} fusion(bf16[1024,3072]{1,0:T(8,128)(2,1)} %reshape.239, f32[64,1024]{1,0:T(8,128)S(1)} %get-tuple-element.161, f32[64]{0:T(128)S(1)} %add_rsqrt_fusion.4, f32[64]{0:T(128)S(1)} %broadcast_multiply_fusion.4), kind=kOutput, calls=%fused_computation.31 | convolution fusion | flops 403046400 | bytes 6947328 | tf_op jit(solution)/shard_map/dot_general | solution.py:103
  160.2 0.8 copy.61
  161.5 1.6 copy.62
  163.1 7.5 %all-to-all-start.1 = ((bf16[32,64,192]{2,1,0:T(8,128)(2,1)}), bf16[32,64,192]{2,1,0:T(8,128)(2,1)}, u32[]{:S(2)}, u32[]{:S(2)}) async-start(bf16[32,64,192]{2,1,0:T(8,128)(2,1)} %copy.62), calls=%async_computation.1 | async-start | bytes 2097152 | tf_op jit(solution)/shard_map/all_to_all | solution.py:150
  170.8 3.3 %slice.51 = bf16[256,32,128]{2,1,0:T(8,128)(2,1)} slice(bf16[256,240,128]{2,1,0:T(8,128)(2,1)} %bitcast.136), slice={[0:256], [96:128], [0:128]} | slice | bytes 4194304 | tf_op jit(solution)/shard_map/slice | solution.py:96
  174.1 2.9 slice.53
  177.0 2.5 slice.52
  179.5 2.8 reshape.242
  182.3 4.3 %reshape.244 = bf16[512,1536]{1,0:T(8,128)(2,1)} reshape(bf16[256,24,128]{2,1,0:T(8,128)(2,1)} %slice.53) | data formatting | bytes 3145728 | tf_op jit(solution)/shard_map/reshape | solution.py:97
  186.6 2.5 reshape.243
  189.1 10.3 %all-to-all-done.1 = bf16[32,64,192]{2,1,0:T(8,128)(2,1)} async-done(((bf16[32,64,192]{2,1,0:T(8,128)(2,1)}), bf16[32,64,192]{2,1,0:T(8,128)(2,1)}, u32[]{:S(2)}, u32[]{:S(2)}) %all-to-all-start.1) | async-done | bytes 786464 | tf_op jit(solution)/shard_map/all_to_all | solution.py:150
  199.4 3.2 copy.63
  202.6 3.5 %reshape.245 = bf16[2048,3,1,64]{0,3,1,2:T(8,128)(2,1)} reshape(bf16[32,64,192]{1,0,2:T(8,128)(2,1)} %copy.63) | data formatting | bytes 1572864 | tf_op jit(solution)/shard_map/reshape | solution.py:62
  206.1 1.9 slice_bitcast_fusion.2
  208.1 1.2 copy.65
  209.4 1.0 copy.66
  210.4 6.0 %while.20 = (s32[]{:T(128)}, bf16[2,512,64]{1,2,0:T(8,128)(2,1)S(1)}, pred[2048]{0:T(1024)(128)(4,1)S(1)}, bf16[2,512,64]{2,1,0:T(8,128)(2,1)S(1)}, bf16[2048,64...) while((s32[]{:T(128)}, bf16[2,512,64]{1,2,0:T(8,128)(2,1)S(1)}, pred[2048]{0:T(1024)(128)(4,1)S(1)}, ...), condition=%wide.region_7.8_spmd, body=%wide.region_4.7_spmd.sunk | while | flops 281050112 | bytes 14893169 | solution.py:40
  210.4 0.8 fusion.90
  211.2 0.9 fusion.91
  212.1 1.3 fusion.92
  213.4 0.8 fusion.90
  214.2 0.9 fusion.91
  215.2 1.3 fusion.92
  217.3 1.1 reshape.271
  218.4 5.4 %all-to-all-start.2 = ((bf16[32,2,2048]{2,1,0:T(2,128)(2,1)}), bf16[32,2,2048]{2,1,0:T(2,128)(2,1)S(1)}, u32[]{:S(2)}, u32[]{:S(2)}) async-start(bf16[32,2,2048]{2,1,0:T(2,128)(2,1)} %reshape.271), calls=%async_computation.2 | async-start | bytes 524288 | tf_op jit(solution)/shard_map/all_to_all | solution.py:158
  223.9 11.8 %all-to-all-done.2 = bf16[32,2,2048]{2,1,0:T(2,128)(2,1)S(1)} async-done(((bf16[32,2,2048]{2,1,0:T(2,128)(2,1)}), bf16[32,2,2048]{2,1,0:T(2,128)(2,1)S(1)}, u32[]{:S(2)}, u32[]{:S(2)}) %all-to-all-start.2) | async-done | bytes 262176 | tf_op jit(solution)/shard_map/all_to_all | solution.py:158
  237.0 1.7 fusion.45
  238.7 0.8 gather_fusion
  240.5 1.0 broadcast_in_dim.104
  241.6 4.6 %all-to-all-start.3 = ((bf16[32,128,96]{1,2,0:T(8,128)(2,1)}), bf16[32,128,96]{1,2,0:T(8,128)(2,1)S(1)}, u32[]{:S(2)}, u32[]{:S(2)}) async-start(bf16[32,128,96]{1,2,0:T(8,128)(2,1)} %bitcast.21), calls=%async_computation.3 | async-start | bytes 1572864 | tf_op jit(solution)/shard_map/all_to_all | solution.py:178
  246.1 5.2 %slice.58 = bf16[256,64,128]{2,1,0:T(8,128)(2,1)} slice(bf16[256,240,128]{2,1,0:T(8,128)(2,1)} %bitcast.139), slice={[0:256], [176:240], [0:128]} | slice | bytes 8388608 | tf_op jit(solution)/shard_map/slice | solution.py:96
  251.3 1.1 slice.57
  252.4 7.3 %reshape.253 = bf16[512,4096]{1,0:T(8,128)(2,1)} reshape(bf16[256,64,128]{2,1,0:T(8,128)(2,1)} %slice.58) | data formatting | bytes 8388608 | tf_op jit(solution)/shard_map/reshape | solution.py:97
  260.0 8.1 %all-to-all-done.3 = bf16[32,128,96]{1,2,0:T(8,128)(2,1)S(1)} async-done(((bf16[32,128,96]{1,2,0:T(8,128)(2,1)}), bf16[32,128,96]{1,2,0:T(8,128)(2,1)S(1)}, u32[]{:S(2)}, u32[]{:S(2)}) %all-to-all-start.3) | async-done | bytes 786464 | tf_op jit(solution)/shard_map/all_to_all | solution.py:178
  269.3 1.3 copy.76
  271.0 20.5 %while.21 = (s32[]{:T(128)}, bf16[4,512,32]{1,2,0:T(8,128)(2,1)S(1)}, bf16[4,512,32]{2,1,0:T(8,128)(2,1)S(1)}, bf16[4096,32]{1,0:T(8,128)(2,1)S(1)}, bf16[4096,32]{1,0:T(8,128)(2,1)}, /*index=5*/s32[]{:T(128)}) while((s32[]{:T(128)}, bf16[4,512,32]{1,2,0:T(8,128)(2,1)S(1)}, bf16[4,512,32]{2,1,0:T(8,128)(2,1)S(1)}, ...), condition=%wide.region_16.17_spmd, body=%wide.region_13.16_spmd.sunk | while | flops 287325184 | bytes 28485736 | solution.py:40
  271.0 1.3 multiply_reduce_fusion.4
  272.3 1.5 fusion.95
  273.8 2.3 fusion.96
  276.1 1.3 multiply_reduce_fusion.4
  277.5 1.5 fusion.95
  279.0 2.3 fusion.96
  281.3 1.3 multiply_reduce_fusion.4
  282.6 1.5 fusion.95
  284.1 2.3 fusion.96
  286.4 1.3 multiply_reduce_fusion.4
  287.7 1.5 fusion.95
  289.2 2.3 fusion.96
  291.6 0.7 copy_bitcast_fusion
  292.3 4.9 %all-to-all-start.4 = ((bf16[32,128,32]{1,2,0:T(8,128)(2,1)}), bf16[32,128,32]{1,2,0:T(8,128)(2,1)S(1)}, u32[]{:S(2)}, u32[]{:S(2)}) async-start(bf16[32,128,32]{1,2,0:T(8,128)(2,1)} %copy_bitcast_fusion), calls=%async_computation.4 | async-start | bytes 524288 | tf_op jit(solution)/shard_map/all_to_all | solution.py:184
  297.9 10.5 %all-to-all-done.4 = bf16[32,128,32]{1,2,0:T(8,128)(2,1)S(1)} async-done(((bf16[32,128,32]{1,2,0:T(8,128)(2,1)}), bf16[32,128,32]{1,2,0:T(8,128)(2,1)S(1)}, u32[]{:S(2)}, u32[]{:S(2)}) %all-to-all-start.4) | async-done | bytes 262176 | tf_op jit(solution)/shard_map/all_to_all | solution.py:184
  309.0 3.4 %fusion.26 = f32[128]{0:T(128)S(1)} fusion(bf16[512,4096]{1,0:T(8,128)(2,1)} %reshape.253, bf16[1,128,4096]{2,1,0:T(8,128)(2,1)S(1)} %copy-done, f32[128]{0:T(128)S(1)} %get-tuple-element.166, f32[128]{0:T(128)S(1)} %broadcast_multiply_fusion, bf16[128,512]{1,0:T(8,128)(2,1)S(1)} %get-tuple-element.165, f32[128]{0:T(128)S(1)} %get-tuple-element.167, ...), kind=kOutput, calls=%fused_computation.38 | convolution fusion | flops 540278656 | bytes 5376512 | tf_op jit(solution)/shard_map/dot_general | solution.py:103
  (90 shorter events, 11.2 us)
Async XLA Ops:
  7.2 131.6 %all-gather.2.cloned.1.call-start = ((), (), s32[]{:S(2)}) async-start(), calls=%async_computation.5 | async-start | bytes 15790080 | tf_op jit(solution)/shard_map/all_gather | solution.py:88
  11.5 0.6 copy-start.6
  15.8 147.3 %all-to-all-start = ((bf16[32,1,64]{2,1,0:T(2,128)(2,1)}), bf16[32,1,64]{2,1,0:T(2,128)(2,1)S(1)}, u32[]{:S(2)}, u32[]{:S(2)}) async-start(bf16[32,1,64]{2,1,0:T(2,128)(2,1)} %broadcast_in_dim.98), calls=%async_computation | async-start | bytes 32768 | tf_op jit(solution)/shard_map/all_to_all | solution.py:154
  163.1 36.2 %all-to-all-start.1 = ((bf16[32,64,192]{2,1,0:T(8,128)(2,1)}), bf16[32,64,192]{2,1,0:T(8,128)(2,1)}, u32[]{:S(2)}, u32[]{:S(2)}) async-start(bf16[32,64,192]{2,1,0:T(8,128)(2,1)} %copy.62), calls=%async_computation.1 | async-start | bytes 2097152 | tf_op jit(solution)/shard_map/all_to_all | solution.py:150
  210.4 13.4 %copy-start.8 = (s32[1,128]{1,0:T(1,128)S(1)}, s32[1,128]{1,0:T(1,128)}, u32[]{:S(2)}) copy-start(s32[1,128]{1,0:T(1,128)} %param.21) | copy-start | bytes 1540
  210.4 1.7 copy-start.4
  213.4 1.7 copy-start.4
  218.4 17.3 %all-to-all-start.2 = ((bf16[32,2,2048]{2,1,0:T(2,128)(2,1)}), bf16[32,2,2048]{2,1,0:T(2,128)(2,1)S(1)}, u32[]{:S(2)}, u32[]{:S(2)}) async-start(bf16[32,2,2048]{2,1,0:T(2,128)(2,1)} %reshape.271), calls=%async_computation.2 | async-start | bytes 524288 | tf_op jit(solution)/shard_map/all_to_all | solution.py:158
  223.8 15.6 %copy-start.5 = (bf16[128,512]{1,0:T(8,128)(2,1)S(1)}, bf16[128,512]{1,0:T(8,128)(2,1)}, u32[]{:S(2)}) copy-start(bf16[128,512]{1,0:T(8,128)(2,1)} %param.26) | copy-start | bytes 393220
  223.9 15.6 %copy-start.7 = (f32[512]{0:T(512)S(1)}, f32[512]{0:T(512)}, u32[]{:S(2)}) copy-start(f32[512]{0:T(512)} %param.25) | copy-start | bytes 6148
  236.7 3.1 copy-start.1
  241.6 26.6 %all-to-all-start.3 = ((bf16[32,128,96]{1,2,0:T(8,128)(2,1)}), bf16[32,128,96]{1,2,0:T(8,128)(2,1)S(1)}, u32[]{:S(2)}, u32[]{:S(2)}) async-start(bf16[32,128,96]{1,2,0:T(8,128)(2,1)} %bitcast.21), calls=%async_computation.3 | async-start | bytes 1572864 | tf_op jit(solution)/shard_map/all_to_all | solution.py:178
  271.0 26.3 %copy-start = (bf16[1,128,4096]{2,1,0:T(8,128)(2,1)S(1)}, bf16[1,128,4096]{2,1,0:T(8,128)(2,1)}, u32[]{:S(2)}) copy-start(bf16[1,128,4096]{2,1,0:T(8,128)(2,1)} %param.17) | copy-start | bytes 3145732
  272.3 1.5 copy-start.2
  277.5 1.5 copy-start.2
  282.6 1.5 copy-start.2
  287.7 1.5 copy-start.2
  292.3 16.1 %all-to-all-start.4 = ((bf16[32,128,32]{1,2,0:T(8,128)(2,1)}), bf16[32,128,32]{1,2,0:T(8,128)(2,1)S(1)}, u32[]{:S(2)}, u32[]{:S(2)}) async-start(bf16[32,128,32]{1,2,0:T(8,128)(2,1)} %copy_bitcast_fusion), calls=%async_computation.4 | async-start | bytes 524288 | tf_op jit(solution)/shard_map/all_to_all | solution.py:184
  308.8 3.6 %copy-start.3 = (bf16[128,512]{1,0:T(8,128)(2,1)}, bf16[128,512]{1,0:T(8,128)(2,1)S(1)}, u32[]{:S(2)}) copy-start(bf16[128,512]{1,0:T(8,128)(2,1)S(1)} %get-tuple-element.165) | copy-start | bytes 393220
Sparse Core Ops, SparseCore 0:
  12.4 126.3 all-gather.1

commit v4 on v3

--- a/solution.py
+++ b/solution.py
@@ -96,11 +96,35 @@
         part = tiles[:, start // lane : (start + size) // lane, :]
         wholes.append(part.reshape(sources * piece.shape[0], piece.shape[1]))
         start += size
-    return wholes
+    return wholes, tiles
 
 
 def weight_dot(rows, weight):
     return jnp.dot(rows, weight, preferred_element_type=jnp.float32)
+
+
+def head_columns(tiles, shape, heads, seq_count, seq_place):
+    shard_rows, width = shape
+    lane = tiles.shape[2]
+    sources = tiles.shape[0]
+    piece_width = width // 3
+    head_size = piece_width // heads
+    local_heads = max(heads // seq_count, 1)
+    query_parts = max(seq_count // heads, 1)
+    local = jnp.arange(local_heads, dtype=jnp.int32)
+    head_ids = (seq_place * local_heads + local) // query_parts
+    offsets = jnp.arange(head_size, dtype=jnp.int32)
+    thirds = jnp.arange(3, dtype=jnp.int32)
+    columns = (
+        thirds[:, None, None] * piece_width
+        + head_ids[None, :, None] * head_size
+        + offsets[None, None, :]
+    ).reshape(-1)
+    shard_ids = jnp.arange(shard_rows, dtype=jnp.int32)
+    groups = shard_ids[:, None] * (width // lane) + (columns // lane)[None, :]
+    lanes = jnp.broadcast_to((columns % lane)[None, :], groups.shape)
+    chosen = tiles[:, groups, lanes]
+    return chosen.reshape(sources * shard_rows, columns.shape[0])
 
 
 def shards(
@@ -124,7 +148,7 @@
     dec_parts = max(seq_count // DEC_HEADS, 1)
     enc_part = seq_place % enc_parts
     dec_part = seq_place % dec_parts
-    (full_project, full_merge, full_lift, *dec_weights) = gather_weights(
+    (_, full_merge, full_lift, *dec_weights), tiles = gather_weights(
         (enc_project, enc_merge, dec_lift, dec_project, dec_merge, dec_predict)
     )
     tok_local = voxels.shape[1]
@@ -142,20 +166,23 @@
     chooser = (slot_index[None, :] == slot_ids[:, None]).astype(jnp.bfloat16)
     kept_rows = jnp.dot(chooser, embedded, preferred_element_type=jnp.float32).astype(jnp.bfloat16)
     present = slot_ids < jnp.sum(cube_flags)
-    packed = weight_dot(
-        layer_norm(kept_rows.astype(jnp.float32)).astype(jnp.bfloat16), full_project
-    ).astype(jnp.bfloat16)
+    enc_in = layer_norm(kept_rows.astype(jnp.float32)).astype(jnp.bfloat16)
     key_marks = jnp.broadcast_to(present.astype(jnp.bfloat16)[None, :], (seq_count, slab_max))
-    outgoing = spread_heads(packed, ENC_HEADS, seq_count)
-    incoming = lax.all_to_all(outgoing, "seq", split_axis=0, concat_axis=0, tiled=True)
-    incoming, full_merge, full_lift, dec_weights[0] = lax.optimization_barrier(
-        (incoming, full_merge, full_lift, dec_weights[0])
-    )
+    spread_in = jnp.broadcast_to(enc_in[None], (seq_count,) + enc_in.shape)
+    all_in = lax.all_to_all(spread_in, "seq", split_axis=0, concat_axis=0, tiled=True)
+    head_project = head_columns(tiles, enc_project.shape, ENC_HEADS, seq_count, seq_place)
+    incoming = jnp.dot(
+        all_in.reshape(-1, all_in.shape[-1]), head_project, preferred_element_type=jnp.float32
+    ).astype(jnp.bfloat16)
+    incoming = incoming.reshape(seq_count, slab_max, head_project.shape[1])
     in_marks = lax.all_to_all(key_marks, "seq", split_axis=0, concat_axis=0, tiled=True)
     key_ok = in_marks.reshape(-1) > 0.5
     mixed_part = attend_heads(incoming, key_ok, ENC_HEADS, enc_part, enc_parts)
     returning = place_rows(mixed_part, incoming.shape[0] * incoming.shape[1], enc_part, seq_count)
     returned = lax.all_to_all(returning, "seq", split_axis=0, concat_axis=0, tiled=True)
+    returned, full_merge, full_lift, dec_weights[0] = lax.optimization_barrier(
+        (returned, full_merge, full_lift, dec_weights[0])
+    )
     mixed_rows = collect_heads(returned, ENC_HEADS, enc_parts)
     encoded = kept_rows.astype(jnp.float32) + weight_dot(mixed_rows, full_merge)
     lifted_list = [

time: 322 us -> 340 us (1.056)
  starting transfers between devices: 33.7 us -> 41.2 us
  local copies, waits for them, and re-layouts: 77.6 us -> 82.1 us
    all_gather x1, waiting for transfers between devices: 106 us -> 126 us  [gather_weights(): every = lax.all_gather(flat, ('dp', 'seq'), axis=0, tiled=True)]
    reshape x1 -> x2, local copies, waits for them, and re-layouts: 1.61 us -> 21 us  [the longest x1 20.7 us: gather_weights(): tiles = every.reshape(sources, flat.shape[0] // lane, lane)]
    reshape x6 -> x5, local copies, waits for them, and re-layouts: 27.5 us -> 16.4 us  [gather_weights(): wholes.append(part.reshape(sources * piece.shape[0], piece.shape[1]))]
    all_to_all x2, waiting for transfers between devices: 22.3 us -> 11.3 us  [shards(): lax.all_to_all(returning, 'seq', split_axis=0, concat_axis=0, tiled=True)]
    all_to_all x2 -> x1, waiting for transfers between devices: 18.4 us -> 8.9 us  [shards(): lax.all_to_all(outgoing, 'seq', split_axis=0, concat_axis=0, tiled=True)]
    gather x0 -> x2, local copies, waits for them, and re-layouts: none -> 7.93 us  [head_columns(): chosen = tiles[:, groups, lanes]]
    all_to_all x0 -> x1, starting transfers between devices: none -> 6.78 us  [shards(): lax.all_to_all(spread_in, 'seq', split_axis=0, concat_axis=0, tiled=True)]
    slice x6 -> x5, local copies, waits for them, and re-layouts: 21.5 us -> 14.9 us  [gather_weights(): part = tiles[:, start // lane:(start + size) // lane, :]]
  transfers between devices with their start and end apart: 6 -> 6, of which waited for: 5 -> 4; matrix products, arithmetic and copies ran while one was open for 21% -> 22% of each run, Pallas kernels for 0% -> 0%
where the time goes in v4:
time: 340 us; the launch traced here: 338 us
  waiting for transfers between devices  149 us (44%)
  local copies, waits for them, and re-layouts  82.1 us (24%)
  starting transfers between devices  41.2 us (12%)
  matrix products  36.5 us (11%)
  other arithmetic  14.8 us (4%)
  between operations  14.5 us (4%)
    all_gather x1, waiting for transfers between devices, gather_weights(): every = lax.all_gather(flat, ('dp', 'seq'), axis=0, tiled=True)  126 us
    reshape x1, local copies, waits for them, and re-layouts, gather_weights(): tiles = every.reshape(sources, flat.shape[0] // lane, lane)  20.7 us
    reshape x5, local copies, waits for them, and re-layouts, gather_weights(): wholes.append(part.reshape(sources * piece.shape[0], piece.shape[1]))  16.4 us
    slice x5, local copies, waits for them, and re-layouts, gather_weights(): part = tiles[:, start // lane:(start + size) // lane, :]  14.9 us
    dot_general x6, matrix products, one_block(): jnp.einsum('qk,kd->qd', weights, values_one, preferred_element_type=jnp.f...  14.1 us
    all_to_all x2, starting transfers between devices, shards(): lax.all_to_all(returning, 'seq', split_axis=0, concat_axis=0, tiled=True)  13.2 us
    all_to_all x1, starting transfers between devices, shards(): lax.all_to_all(key_marks, 'seq', split_axis=0, concat_axis=0, tiled=True)  11.4 us
    all_to_all x2, waiting for transfers between devices, shards(): lax.all_to_all(returning, 'seq', split_axis=0, concat_axis=0, tiled=True)  11.3 us
  transfers between devices with their start and end apart: 6, of which 4 were waited for; matrix products, arithmetic and copies ran while one was open for 22% of the time, Pallas kernels for 0%

profile of v4, /device:TPU:32, one launch (start us, length us, event | category | flops | bytes accessed | tf_op | source)
XLA Modules:
  0.0 338.4 jit_solution(18059278869542639639)
XLA Ops:
  7.2 0.7 copy.93
  8.0 0.7 copy.95
  8.6 0.7 reshape.413
  9.4 0.7 copy.96
  10.0 0.7 copy.97
  10.8 0.7 bitcast_dynamic-update-slice_fusion
  12.1 0.8 copy.63
  13.2 1.3 fusion.59
  15.8 11.4 %all-to-all-start = ((bf16[32,1,64]{2,1,0:T(2,128)(2,1)}), bf16[32,1,64]{2,1,0:T(2,128)(2,1)S(1)}, u32[]{:S(2)}, u32[]{:S(2)}) async-start(bf16[32,1,64]{2,1,0:T(2,128)(2,1)} %broadcast_in_dim.79), calls=%async_computation | async-start | bytes 32768 | tf_op jit(solution)/shard_map/all_to_all | solution.py:178
  27.2 5.2 %fusion.62 = (f32[64]{0:T(128)S(1)}, f32[64,1024]{1,0:T(8,128)S(1)}) fusion(bf16[4096,1024]{1,0:T(8,128)(2,1)} %param.18, bf16[1,128,4096]{2,1,0:T(8,128)(2,1)} %param.17, bf16[128,1024]{1,0:T(8,128)(2,1)} %param.20, f32[1024]{0:T(1024)} %param.19, s32[128]{0:T(128)S(1)} %get-tuple-element.136), kind=kOutput, calls=%fused_computation.134 | convolution fusion | flops 1091248128 | bytes 9966336 | tf_op jit(solution)/shard_map/dot_general | solution.py:167
  32.7 3.1 all-to-all-done
  35.8 2.5 broadcast_in_dim.80
  38.3 6.8 %all-to-all-start.1 = ((bf16[32,64,1024]{2,1,0:T(8,128)(2,1)}), bf16[32,64,1024]{2,1,0:T(8,128)(2,1)}, u32[]{:S(2)}, u32[]{:S(2)}) async-start(bf16[32,64,1024]{2,1,0:T(8,128)(2,1)} %broadcast_in_dim.80), calls=%async_computation.1 | async-start | bytes 8388608 | tf_op jit(solution)/shard_map/all_to_all | solution.py:172
  45.6 125.8 %all-gather.2.cloned.1.call-done = bf16[7864320]{0:T(1024)(128)(2,1)} async-done(((bf16[30720]{0:T(1024)(128)(2,1)}), bf16[7864320]{0:T(1024)(128)(2,1)}) %all-gather.2.cloned.1.call-update) | async-done | bytes 15728656 | tf_op jit(solution)/shard_map/all_gather | solution.py:88
  171.4 20.7 %copy.64 = bf16[256,240,128]{0,2,1:T(8,128)(2,1)} copy(bf16[256,240,128]{2,1,0:T(8,128)(2,1)} %bitcast.134) | data formatting | bytes 31457280 | tf_op jit(solution)/shard_map/reshape | solution.py:91
  192.1 7.6 %gather_fusion = bf16[768,256]{1,0:T(8,128)(2,1)S(1)} fusion(bf16[256,240,128]{0,2,1:T(8,128)(2,1)} %copy.64, s32[768]{0:T(1024)S(1)} %reshape.434), kind=kCustom, calls=%fused_computation | custom fusion | bytes 792576 | tf_op jit(solution)/shard_map/gather | solution.py:126
  200.4 3.7 %convolution_convert_fusion = bf16[2048,192]{0,1:T(8,128)(2,1)S(1)} fusion(bf16[2048,1024]{1,0:T(8,128)(2,1)} %bitcast.8, bf16[1024,192]{1,0:T(8,128)(2,1)S(1)} %reshape.417), kind=kOutput, calls=%fused_computation.34 | convolution fusion | flops 805699584 | bytes 5373952 | tf_op jit(solution)/shard_map/dot_general | solution.py:174
  205.0 6.1 %while.20 = (s32[]{:T(128)}, bf16[2,512,64]{1,2,0:T(8,128)(2,1)S(1)}, pred[2048]{0:T(1024)(128)(4,1)S(1)}, bf16[2,512,64]{2,1,0:T(8,128)(2,1)S(1)}, bf16[2048,64...) while((s32[]{:T(128)}, bf16[2,512,64]{1,2,0:T(8,128)(2,1)S(1)}, ...), condition=%wide.region_7.8_spmd, body=%wide.region_4.7_spmd.sunk | while | flops 281050112 | bytes 13844565 | solution.py:40
  205.0 0.8 fusion.92
  205.8 0.9 fusion.93
  206.7 1.3 fusion.94
  208.0 0.8 fusion.92
  208.8 0.9 fusion.93
  209.7 1.3 fusion.94
  211.8 1.1 reshape.453
  212.9 8.3 %all-to-all-start.2 = ((bf16[32,2,2048]{2,1,0:T(2,128)(2,1)}), bf16[32,2,2048]{2,1,0:T(2,128)(2,1)}, u32[]{:S(2)}, u32[]{:S(2)}) async-start(bf16[32,2,2048]{2,1,0:T(2,128)(2,1)} %reshape.453), calls=%async_computation.2 | async-start | bytes 524288 | tf_op jit(solution)/shard_map/all_to_all | solution.py:182
  221.3 3.4 slice.51
  224.6 2.9 slice.53
  227.5 2.4 slice.52
  229.9 2.8 reshape.419
  232.8 4.3 %reshape.421 = bf16[512,1536]{1,0:T(8,128)(2,1)} reshape(bf16[256,24,128]{2,1,0:T(8,128)(2,1)} %slice.53) | data formatting | bytes 3145728 | tf_op jit(solution)/shard_map/reshape | solution.py:97
  237.0 1.7 reshape.420
  238.8 2.1 reshape.454
  240.9 1.2 bitcast_reduce_fusion
  243.2 0.8 gather_fusion.1
  244.0 1.1 convert_reduce_fusion.1
  245.3 1.8 convolution_convert_fusion.1
  247.4 1.0 broadcast_in_dim.127
  248.4 9.8 %all-to-all-start.3 = ((bf16[32,128,96]{1,2,0:T(8,128)(2,1)}), bf16[32,128,96]{1,2,0:T(8,128)(2,1)S(1)}, u32[]{:S(2)}, u32[]{:S(2)}) async-start(bf16[32,128,96]{1,2,0:T(8,128)(2,1)} %bitcast.24), calls=%async_computation.3 | async-start | bytes 1572864 | tf_op jit(solution)/shard_map/all_to_all | solution.py:205
  258.5 5.2 %slice.55 = bf16[256,64,128]{2,1,0:T(8,128)(2,1)} slice(bf16[256,240,128]{2,1,0:T(8,128)(2,1)} %bitcast.138), slice={[0:256], [176:240], [0:128]} | slice | bytes 8388608 | tf_op jit(solution)/shard_map/slice | solution.py:96
  263.7 1.1 slice.54
  264.7 7.3 %reshape.428 = bf16[512,4096]{1,0:T(8,128)(2,1)} reshape(bf16[256,64,128]{2,1,0:T(8,128)(2,1)} %slice.55) | data formatting | bytes 8388608 | tf_op jit(solution)/shard_map/reshape | solution.py:97
  272.4 8.9 %all-to-all-done.3 = bf16[32,128,96]{1,2,0:T(8,128)(2,1)S(1)} async-done(((bf16[32,128,96]{1,2,0:T(8,128)(2,1)}), bf16[32,128,96]{1,2,0:T(8,128)(2,1)S(1)}, u32[]{:S(2)}, u32[]{:S(2)}) %all-to-all-start.3) | async-done | bytes 786464 | tf_op jit(solution)/shard_map/all_to_all | solution.py:205
  282.5 1.3 copy.78
  283.8 0.6 constant_dynamic-slice_fusion
  284.4 1.2 copy.83
  285.6 23.0 %while.21 = (s32[]{:T(128)}, bf16[4,512,32]{1,2,0:T(8,128)(2,1)}, bf16[4,512,32]{2,1,0:T(8,128)(2,1)S(1)}, bf16[4096,32]{1,0:T(8,128)(2,1)S(1)}, bf16[4096,32]{1,0:T(8,128)(2,1)}, /*index=5*/s32[]{:T(128)}) while((s32[]{:T(128)}, bf16[4,512,32]{1,2,0:T(8,128)(2,1)}, bf16[4,512,32]{2,1,0:T(8,128)(2,1)S(1)}, bf16[4096,32]{1,0:T(8,128)(2,1)S(1)}, ...), condition=%wide.region_16.17_spmd, body=%wide.region_13.16_spmd.sunk | while | flops 287325184 | bytes 27699812 | solution.py:40
  285.6 1.3 multiply_reduce_fusion.4
  287.0 1.5 fusion.97
  288.5 2.9 fusion.98
  291.4 1.3 multiply_reduce_fusion.4
  292.7 1.5 fusion.97
  294.2 2.9 fusion.98
  297.1 1.3 multiply_reduce_fusion.4
  298.4 1.5 fusion.97
  300.0 2.9 fusion.98
  302.8 1.3 multiply_reduce_fusion.4
  304.2 1.5 fusion.97
  305.7 2.9 fusion.98
  308.6 0.9 copy.92
  309.6 0.7 copy_bitcast_fusion
  310.3 4.9 %all-to-all-start.4 = ((bf16[32,128,32]{1,2,0:T(8,128)(2,1)}), bf16[32,128,32]{1,2,0:T(8,128)(2,1)S(1)}, u32[]{:S(2)}, u32[]{:S(2)}) async-start(bf16[32,128,32]{1,2,0:T(8,128)(2,1)} %copy_bitcast_fusion), calls=%async_computation.4 | async-start | bytes 524288 | tf_op jit(solution)/shard_map/all_to_all | solution.py:211
  315.7 11.3 %all-to-all-done.4 = bf16[32,128,32]{1,2,0:T(8,128)(2,1)S(1)} async-done(((bf16[32,128,32]{1,2,0:T(8,128)(2,1)}), bf16[32,128,32]{1,2,0:T(8,128)(2,1)S(1)}, u32[]{:S(2)}, u32[]{:S(2)}) %all-to-all-start.4) | async-done | bytes 262176 | tf_op jit(solution)/shard_map/all_to_all | solution.py:211
  327.6 3.4 %fusion.26 = f32[128]{0:T(128)S(1)} fusion(bf16[512,4096]{1,0:T(8,128)(2,1)} %reshape.428, bf16[1,128,4096]{2,1,0:T(8,128)(2,1)S(1)} %copy-done, f32[128]{0:T(128)S(1)} %add_rsqrt_fusion, f32[128]{0:T(128)S(1)} %broadcast_multiply_fusion, bf16[128,512]{1,0:T(8,128)(2,1)S(1)} %get-tuple-element.143, f32[128]{0:T(128)S(1)} %add_rsqrt_fusion.1, ...), kind=kOutput, calls=%fused_computation.39 | convolution fusion | flops 540278656 | bytes 5376512 | tf_op jit(solution)/shard_map/dot_general | solution.py:103
  (89 shorter events, 10.2 us)
Async XLA Ops:
  7.2 164.3 %all-gather.2.cloned.1.call-start = ((), (), s32[]{:S(2)}) async-start(), calls=%async_computation.5 | async-start | bytes 15790080 | tf_op jit(solution)/shard_map/all_gather | solution.py:88
  11.5 0.6 copy-start.3
  15.8 20.0 %all-to-all-start = ((bf16[32,1,64]{2,1,0:T(2,128)(2,1)}), bf16[32,1,64]{2,1,0:T(2,128)(2,1)S(1)}, u32[]{:S(2)}, u32[]{:S(2)}) async-start(bf16[32,1,64]{2,1,0:T(2,128)(2,1)} %broadcast_in_dim.79), calls=%async_computation | async-start | bytes 32768 | tf_op jit(solution)/shard_map/all_to_all | solution.py:178
  38.3 162.1 %all-to-all-start.1 = ((bf16[32,64,1024]{2,1,0:T(8,128)(2,1)}), bf16[32,64,1024]{2,1,0:T(8,128)(2,1)}, u32[]{:S(2)}, u32[]{:S(2)}) async-start(bf16[32,64,1024]{2,1,0:T(8,128)(2,1)} %broadcast_in_dim.80), calls=%async_computation.1 | async-start | bytes 8388608 | tf_op jit(solution)/shard_map/all_to_all | solution.py:172
  204.9 16.3 %copy-start.5 = (s32[1,128]{1,0:T(1,128)S(1)}, s32[1,128]{1,0:T(1,128)}, u32[]{:S(2)}) copy-start(s32[1,128]{1,0:T(1,128)} %param.21) | copy-start | bytes 1540
  212.9 25.8 %all-to-all-start.2 = ((bf16[32,2,2048]{2,1,0:T(2,128)(2,1)}), bf16[32,2,2048]{2,1,0:T(2,128)(2,1)}, u32[]{:S(2)}, u32[]{:S(2)}) async-start(bf16[32,2,2048]{2,1,0:T(2,128)(2,1)} %reshape.453), calls=%async_computation.2 | async-start | bytes 524288 | tf_op jit(solution)/shard_map/all_to_all | solution.py:182
  238.7 5.3 %copy-start.4 = (f32[512]{0:T(512)S(1)}, f32[512]{0:T(512)}, u32[]{:S(2)}) copy-start(f32[512]{0:T(512)} %param.25) | copy-start | bytes 6148
  243.2 15.0 %copy-start = (bf16[1,128,4096]{2,1,0:T(8,128)(2,1)S(1)}, bf16[1,128,4096]{2,1,0:T(8,128)(2,1)}, u32[]{:S(2)}) copy-start(bf16[1,128,4096]{2,1,0:T(8,128)(2,1)} %param.17) | copy-start | bytes 3145732
  248.4 32.8 %all-to-all-start.3 = ((bf16[32,128,96]{1,2,0:T(8,128)(2,1)}), bf16[32,128,96]{1,2,0:T(8,128)(2,1)S(1)}, u32[]{:S(2)}, u32[]{:S(2)}) async-start(bf16[32,128,96]{1,2,0:T(8,128)(2,1)} %bitcast.24), calls=%async_computation.3 | async-start | bytes 1572864 | tf_op jit(solution)/shard_map/all_to_all | solution.py:205
  287.0 1.5 copy-start.1
  292.7 1.5 copy-start.1
  298.4 1.5 copy-start.1
  304.2 1.5 copy-start.1
  310.3 16.7 %all-to-all-start.4 = ((bf16[32,128,32]{1,2,0:T(8,128)(2,1)}), bf16[32,128,32]{1,2,0:T(8,128)(2,1)S(1)}, u32[]{:S(2)}, u32[]{:S(2)}) async-start(bf16[32,128,32]{1,2,0:T(8,128)(2,1)} %copy_bitcast_fusion), calls=%async_computation.4 | async-start | bytes 524288 | tf_op jit(solution)/shard_map/all_to_all | solution.py:211
  327.4 3.6 %copy-start.2 = (bf16[128,512]{1,0:T(8,128)(2,1)}, bf16[128,512]{1,0:T(8,128)(2,1)S(1)}, u32[]{:S(2)}) copy-start(bf16[128,512]{1,0:T(8,128)(2,1)S(1)} %get-tuple-element.143) | copy-start | bytes 393220
Sparse Core Ops, SparseCore 0:
  12.4 158.9 all-gather.1

commit v5 on v3

--- a/solution.py
+++ b/solution.py
@@ -1,8 +1,10 @@
+import functools
 import math
 
 import jax
 import jax.numpy as jnp
 from jax import lax
+from jax.experimental import pallas as pl
 from jax.sharding import PartitionSpec as P
 
 ENC_HEADS = 16
@@ -15,30 +17,48 @@
     return centre * lax.rsqrt(spread + 1e-06)
 
 
+def attention_kernel(mark_ref, query_ref, key_ref, value_ref, out_ref, *, score_scale):
+    scores = (
+        lax.dot_general(
+            query_ref[...],
+            key_ref[...],
+            (((1,), (1,)), ((), ())),
+            preferred_element_type=jnp.float32,
+        )
+        * score_scale
+    )
+    scores = jnp.where(mark_ref[...] > 0.5, scores, -1e30)
+    top_score = jnp.max(scores, axis=-1, keepdims=True)
+    exponent = jnp.exp(scores - top_score)
+    weights = (exponent / jnp.sum(exponent, axis=-1, keepdims=True)).astype(jnp.bfloat16)
+    out_ref[...] = jnp.dot(weights, value_ref[...], preferred_element_type=jnp.float32).astype(
+        jnp.bfloat16
+    )
+
+
 def attend_rows(queries, key_rows, value_rows, key_ok):
     query_rows, local_heads, head_size = queries.shape
-    block_rows = math.gcd(query_rows, 512)
+    key_count = key_rows.shape[0]
+    block_rows = math.gcd(query_rows, 256)
     score_scale = 1.0 / math.sqrt(head_size)
-    query_blocks = queries[:, 0].reshape(query_rows // block_rows, block_rows, head_size)
-    keys_one = key_rows[:, 0]
-    values_one = value_rows[:, 0]
-
-    def one_block(query_block):
-        scores = (
-            jnp.einsum("qd,kd->qk", query_block, keys_one, preferred_element_type=jnp.float32)
-            * score_scale
-        )
-        if key_ok is not None:
-            scores = jnp.where(key_ok[None, :], scores, -1e30)
-        top_score = jnp.max(scores, axis=-1, keepdims=True)
-        exponent = jnp.exp(scores - top_score)
-        weights = (exponent / jnp.sum(exponent, axis=-1, keepdims=True)).astype(jnp.bfloat16)
-        return jnp.einsum(
-            "qk,kd->qd", weights, values_one, preferred_element_type=jnp.float32
-        ).astype(jnp.bfloat16)
-
-    head_outputs = [lax.map(one_block, query_blocks).reshape(query_rows, head_size)]
-    return jnp.stack(head_outputs, axis=1)
+    if key_ok is None:
+        marks = jnp.ones((1, key_count), jnp.float32)
+    else:
+        marks = key_ok.astype(jnp.float32).reshape(1, key_count)
+    whole = pl.BlockSpec((key_count, head_size), lambda step: (0, 0))
+    mixed = pl.pallas_call(
+        functools.partial(attention_kernel, score_scale=score_scale),
+        grid=(query_rows // block_rows,),
+        in_specs=[
+            pl.BlockSpec((1, key_count), lambda step: (0, 0)),
+            pl.BlockSpec((block_rows, head_size), lambda step: (step, 0)),
+            whole,
+            whole,
+        ],
+        out_specs=pl.BlockSpec((block_rows, head_size), lambda step: (step, 0)),
+        out_shape=jax.ShapeDtypeStruct((query_rows, head_size), jnp.bfloat16),
+    )(marks, queries[:, 0], key_rows[:, 0], value_rows[:, 0])
+    return mixed[:, None, :]
 
 
 def spread_heads(packed, heads, seq_count):

time: 322 us -> 334 us (1.037)
  Pallas kernels: 0 us -> 26.3 us
  matrix products: 34.2 us -> 14.3 us
  local copies, waits for them, and re-layouts: 77.6 us -> 90 us
  other arithmetic: 12.6 us -> 6.72 us
    pallas_call x0 -> x2, Pallas kernels: none -> 26.3 us  [attend_rows(): pl.pallas_call(functools.partial(attention_kernel, score_scale=score_scal...]
    dot_general x12 -> x0, matrix products: 18.5 us -> none  [the longest x6 11.6 us: one_block(): jnp.einsum('qk,kd->qd', weights, values_one, preferred_element_type=jnp.f...]
    unnamed x25 -> x33, local copies, waits for them, and re-layouts: 5.67 us -> 15.1 us
    reduce_sum x6 -> x0, other arithmetic: 7.89 us -> none  [one_block(): jnp.sum(exponent, axis=-1, keepdims=True)]
    while x18 -> x0, local copies, waits for them, and re-layouts: 4.52 us -> none  [the longest x6 4.49 us: attend_rows(): lax.map(one_block, query_blocks).reshape(query_rows, head_size)]
  transfers between devices with their start and end apart: 6 -> 6, of which waited for: 5 -> 5; matrix products, arithmetic and copies ran while one was open for 21% -> 20% of each run, Pallas kernels for 0% -> 0%
where the time goes in v5:
time: 334 us; the launch traced here: 332 us
  waiting for transfers between devices  146 us (44%)
  local copies, waits for them, and re-layouts  90 us (27%)
  starting transfers between devices  33.8 us (10%)
  Pallas kernels  26.3 us (8%)
  between operations  14.4 us (4%)
  matrix products  14.3 us (4%)
  other arithmetic  6.72 us (2%)
    all_gather x1, waiting for transfers between devices, gather_weights(): every = lax.all_gather(flat, ('dp', 'seq'), axis=0, tiled=True)  106 us
    reshape x6, local copies, waits for them, and re-layouts, gather_weights(): wholes.append(part.reshape(sources * piece.shape[0], piece.shape[1]))  26.7 us
    pallas_call x2, Pallas kernels, attend_rows(): pl.pallas_call(functools.partial(attention_kernel, score_scale=score_scal...  26.3 us
    slice x6, local copies, waits for them, and re-layouts, gather_weights(): part = tiles[:, start // lane:(start + size) // lane, :]  21.5 us
    all_to_all x2, waiting for transfers between devices, shards(): lax.all_to_all(returning, 'seq', split_axis=0, concat_axis=0, tiled=True)  21.4 us
    all_to_all x2, waiting for transfers between devices, shards(): lax.all_to_all(outgoing, 'seq', split_axis=0, concat_axis=0, tiled=True)  18.6 us
    unnamed x33, local copies, waits for them, and re-layouts  15.1 us
    all_to_all x2, starting transfers between devices, shards(): lax.all_to_all(outgoing, 'seq', split_axis=0, concat_axis=0, tiled=True)  12 us
  transfers between devices with their start and end apart: 6, of which 5 were waited for; matrix products, arithmetic and copies ran while one was open for 20% of the time, Pallas kernels for 0%

profile of v5, /device:TPU:32, one launch (start us, length us, event | category | flops | bytes accessed | tf_op | source)
XLA Modules:
  0.0 331.9 jit_solution(4419165616885188244)
XLA Ops:
  7.2 0.7 copy.67
  8.0 0.7 copy.69
  8.6 0.7 reshape.246
  9.4 0.7 copy.70
  10.0 0.7 copy.71
  10.8 0.7 bitcast_dynamic-update-slice_fusion
  11.5 0.6 copy-done.4
  12.1 0.8 copy.43
  13.2 1.3 fusion.41
  14.5 0.6 compare_convert_fusion.1
  15.2 0.6 broadcast_in_dim.69
  15.8 11.4 %all-to-all-start = ((bf16[32,1,64]{2,1,0:T(2,128)(2,1)}), bf16[32,1,64]{2,1,0:T(2,128)(2,1)S(1)}, u32[]{:S(2)}, u32[]{:S(2)}) async-start(bf16[32,1,64]{2,1,0:T(2,128)(2,1)} %broadcast_in_dim.69), calls=%async_computation | async-start | bytes 32768 | tf_op jit(solution)/shard_map/all_to_all | solution.py:174
  27.1 5.2 %fusion.42 = (f32[64]{0:T(128)S(1)}, f32[64,1024]{1,0:T(8,128)S(1)}) fusion(bf16[4096,1024]{1,0:T(8,128)(2,1)} %param.14, bf16[1,128,4096]{2,1,0:T(8,128)(2,1)} %param.13, bf16[128,1024]{1,0:T(8,128)(2,1)} %param.16, f32[1024]{0:T(1024)} %param.15, s32[128]{0:T(128)S(1)} %get-tuple-element.28), kind=kOutput, calls=%fused_computation.92 | convolution fusion | flops 1091248128 | bytes 9966336 | tf_op jit(solution)/shard_map/dot_general | solution.py:163
  32.6 106.2 %all-gather.2.cloned.1.call-done = bf16[7864320]{0:T(1024)(128)(2,1)} async-done(((bf16[30720]{0:T(1024)(128)(2,1)}), bf16[7864320]{0:T(1024)(128)(2,1)}) %all-gather.2.cloned.1.call-update) | async-done | bytes 15728656 | tf_op jit(solution)/shard_map/all_gather | solution.py:108
  138.8 6.6 %slice.50 = bf16[256,96,128]{2,1,0:T(8,128)(2,1)} slice(bf16[256,240,128]{2,1,0:T(8,128)(2,1)} %bitcast.82), slice={[0:256], [0:96], [0:128]} | slice | bytes 12582912 | tf_op jit(solution)/shard_map/slice | solution.py:116
  145.4 10.3 %reshape.250 = bf16[1024,3072]{1,0:T(8,128)(2,1)} reshape(bf16[256,96,128]{2,1,0:T(8,128)(2,1)} %slice.50) | data formatting | bytes 12582912 | tf_op jit(solution)/shard_map/reshape | solution.py:117
  155.7 4.0 %convolution_convert_fusion = bf16[64,3072]{1,0:T(8,128)(2,1)S(1)} fusion(bf16[1024,3072]{1,0:T(8,128)(2,1)} %reshape.250, f32[64,1024]{1,0:T(8,128)S(1)} %get-tuple-element.30, f32[64]{0:T(128)S(1)} %add_rsqrt_fusion.4, f32[64]{0:T(128)S(1)} %broadcast_multiply_fusion.4), kind=kOutput, calls=%fused_computation.3 | convolution fusion | flops 403046400 | bytes 6947328 | tf_op jit(solution)/shard_map/dot_general | solution.py:123
  160.2 0.8 copy.44
  161.5 1.6 copy.45
  163.1 7.5 %all-to-all-start.1 = ((bf16[32,64,192]{2,1,0:T(8,128)(2,1)}), bf16[32,64,192]{2,1,0:T(8,128)(2,1)}, u32[]{:S(2)}, u32[]{:S(2)}) async-start(bf16[32,64,192]{2,1,0:T(8,128)(2,1)} %copy.45), calls=%async_computation.1 | async-start | bytes 2097152 | tf_op jit(solution)/shard_map/all_to_all | solution.py:170
  170.7 0.7 reshape.270.mark_ref
  171.3 3.3 %slice.51 = bf16[256,32,128]{2,1,0:T(8,128)(2,1)} slice(bf16[256,240,128]{2,1,0:T(8,128)(2,1)} %bitcast.83), slice={[0:256], [96:128], [0:128]} | slice | bytes 4194304 | tf_op jit(solution)/shard_map/slice | solution.py:116
  174.7 2.9 slice.53
  177.6 2.5 slice.52
  180.0 2.8 reshape.253
  182.9 4.3 %reshape.255 = bf16[512,1536]{1,0:T(8,128)(2,1)} reshape(bf16[256,24,128]{2,1,0:T(8,128)(2,1)} %slice.53) | data formatting | bytes 3145728 | tf_op jit(solution)/shard_map/reshape | solution.py:117
  187.1 1.7 reshape.254
  188.8 10.5 %all-to-all-done.1 = bf16[32,64,192]{2,1,0:T(8,128)(2,1)} async-done(((bf16[32,64,192]{2,1,0:T(8,128)(2,1)}), bf16[32,64,192]{2,1,0:T(8,128)(2,1)}, u32[]{:S(2)}, u32[]{:S(2)}) %all-to-all-start.1) | async-done | bytes 786464 | tf_op jit(solution)/shard_map/all_to_all | solution.py:170
  199.3 3.2 copy.46
  202.5 3.5 %reshape.256 = bf16[2048,3,1,64]{0,3,1,2:T(8,128)(2,1)} reshape(bf16[32,64,192]{1,0,2:T(8,128)(2,1)} %copy.46) | data formatting | bytes 1572864 | tf_op jit(solution)/shard_map/reshape | solution.py:82
  206.1 2.0 fusion.40
  208.1 0.8 copy.47
  208.9 2.0 copy.63
  210.9 2.0 copy.62
  212.9 7.0 %shard_map.140 = bf16[1024,64]{1,0:T(8,128)(2,1)} custom-call(f32[1,2048]{1,0:T(1,128)} %reshape.270.mark_ref, bf16[1024,64]{1,0:T(8,128)(2,1)} %bitcast.95, bf16[2048,64]{1,0:T(8,128)(2,1)} %bitcast.92, bf16[2048,64]{1,0:T(8,128)(2,1)} %bitcast.91), custom_call_target="tpu_custom_call" | custom-call | tf_op jit(solution)/shard_map/pallas_call | solution.py:49
  219.9 0.9 broadcast_in_dim.68
  220.7 1.7 constant_dynamic-update-slice_fusion.6
  222.4 2.2 reshape.289
  224.6 5.5 %all-to-all-start.2 = ((bf16[32,2,2048]{2,1,0:T(2,128)(2,1)}), bf16[32,2,2048]{2,1,0:T(2,128)(2,1)}, u32[]{:S(2)}, u32[]{:S(2)}) async-start(bf16[32,2,2048]{2,1,0:T(2,128)(2,1)} %reshape.289), calls=%async_computation.2 | async-start | bytes 524288 | tf_op jit(solution)/shard_map/all_to_all | solution.py:178
  230.6 0.5 compare_and_fusion
  231.1 10.9 %all-to-all-done.2 = bf16[32,2,2048]{2,1,0:T(2,128)(2,1)} async-done(((bf16[32,2,2048]{2,1,0:T(2,128)(2,1)}), bf16[32,2,2048]{2,1,0:T(2,128)(2,1)}, u32[]{:S(2)}, u32[]{:S(2)}) %all-to-all-start.2) | async-done | bytes 262176 | tf_op jit(solution)/shard_map/all_to_all | solution.py:178
  242.0 2.1 reshape.290
  244.1 1.2 bitcast_reduce_fusion
  245.3 0.9 copy.50
  246.2 1.1 reshape.260
  247.3 0.6 fusion.45
  248.5 0.8 gather_fusion
  250.4 1.0 broadcast_in_dim.75
  251.4 4.6 %all-to-all-start.3 = ((bf16[32,128,96]{1,2,0:T(8,128)(2,1)}), bf16[32,128,96]{1,2,0:T(8,128)(2,1)S(1)}, u32[]{:S(2)}, u32[]{:S(2)}) async-start(bf16[32,128,96]{1,2,0:T(8,128)(2,1)} %bitcast.18), calls=%async_computation.3 | async-start | bytes 1572864 | tf_op jit(solution)/shard_map/all_to_all | solution.py:198
  256.0 5.2 %slice.58 = bf16[256,64,128]{2,1,0:T(8,128)(2,1)} slice(bf16[256,240,128]{2,1,0:T(8,128)(2,1)} %bitcast.86), slice={[0:256], [176:240], [0:128]} | slice | bytes 8388608 | tf_op jit(solution)/shard_map/slice | solution.py:116
  261.2 1.1 slice.57
  262.3 7.3 %reshape.264 = bf16[512,4096]{1,0:T(8,128)(2,1)} reshape(bf16[256,64,128]{2,1,0:T(8,128)(2,1)} %slice.58) | data formatting | bytes 8388608 | tf_op jit(solution)/shard_map/reshape | solution.py:117
  269.9 8.1 %all-to-all-done.3 = bf16[32,128,96]{1,2,0:T(8,128)(2,1)S(1)} async-done(((bf16[32,128,96]{1,2,0:T(8,128)(2,1)}), bf16[32,128,96]{1,2,0:T(8,128)(2,1)S(1)}, u32[]{:S(2)}, u32[]{:S(2)}) %all-to-all-start.3) | async-done | bytes 786464 | tf_op jit(solution)/shard_map/all_to_all | solution.py:198
  278.7 1.3 copy.64
  280.1 1.4 copy.65
  281.4 1.0 copy.54
  282.5 0.6 broadcast_in_dim.74.mark_ref
  283.1 19.3 %shard_map.141 = bf16[2048,32]{1,0:T(8,128)(2,1)} custom-call(f32[1,4096]{1,0:T(1,128)} %broadcast_in_dim.74.mark_ref, bf16[2048,32]{1,0:T(8,128)(2,1)} %bitcast.93, bf16[4096,32]{1,0:T(8,128)(2,1)} %bitcast.89, bf16[4096,32]{1,0:T(8,128)(2,1)} %bitcast.90), custom_call_target="tpu_custom_call" | custom-call | tf_op jit(solution)/shard_map/pallas_call | solution.py:49
  302.4 1.2 copy.57
  303.7 0.7 copy_bitcast_fusion
  304.4 4.9 %all-to-all-start.4 = ((bf16[32,128,32]{1,2,0:T(8,128)(2,1)}), bf16[32,128,32]{1,2,0:T(8,128)(2,1)S(1)}, u32[]{:S(2)}, u32[]{:S(2)}) async-start(bf16[32,128,32]{1,2,0:T(8,128)(2,1)} %copy_bitcast_fusion), calls=%async_computation.4 | async-start | bytes 524288 | tf_op jit(solution)/shard_map/all_to_all | solution.py:204
  310.0 10.5 %all-to-all-done.4 = bf16[32,128,32]{1,2,0:T(8,128)(2,1)S(1)} async-done(((bf16[32,128,32]{1,2,0:T(8,128)(2,1)}), bf16[32,128,32]{1,2,0:T(8,128)(2,1)S(1)}, u32[]{:S(2)}, u32[]{:S(2)}) %all-to-all-start.4) | async-done | bytes 262176 | tf_op jit(solution)/shard_map/all_to_all | solution.py:204
  321.1 3.4 %fusion.4 = f32[128]{0:T(128)S(1)} fusion(bf16[512,4096]{1,0:T(8,128)(2,1)} %reshape.264, bf16[1,128,4096]{2,1,0:T(8,128)(2,1)S(1)} %copy-done, f32[128]{0:T(128)S(1)} %get-tuple-element.35, f32[128]{0:T(128)S(1)} %broadcast_multiply_fusion, bf16[128,512]{1,0:T(8,128)(2,1)S(1)} %get-tuple-element.34, f32[128]{0:T(128)S(1)} %get-tuple-element.36, ...), kind=kOutput, calls=%fused_computation.10 | convolution fusion | flops 540278656 | bytes 5376512 | tf_op jit(solution)/shard_map/dot_general | solution.py:123
  324.5 0.5 bitcast_select_fusion.1
  (62 shorter events, 6.1 us)
Async XLA Ops:
  7.2 131.6 %all-gather.2.cloned.1.call-start = ((), (), s32[]{:S(2)}) async-start(), calls=%async_computation.5 | async-start | bytes 15790080 | tf_op jit(solution)/shard_map/all_gather | solution.py:108
  11.5 0.6 copy-start.4
  15.8 147.3 %all-to-all-start = ((bf16[32,1,64]{2,1,0:T(2,128)(2,1)}), bf16[32,1,64]{2,1,0:T(2,128)(2,1)S(1)}, u32[]{:S(2)}, u32[]{:S(2)}) async-start(bf16[32,1,64]{2,1,0:T(2,128)(2,1)} %broadcast_in_dim.69), calls=%async_computation | async-start | bytes 32768 | tf_op jit(solution)/shard_map/all_to_all | solution.py:174
  163.1 36.2 %all-to-all-start.1 = ((bf16[32,64,192]{2,1,0:T(8,128)(2,1)}), bf16[32,64,192]{2,1,0:T(8,128)(2,1)}, u32[]{:S(2)}, u32[]{:S(2)}) async-start(bf16[32,64,192]{2,1,0:T(8,128)(2,1)} %copy.45), calls=%async_computation.1 | async-start | bytes 2097152 | tf_op jit(solution)/shard_map/all_to_all | solution.py:170
  212.9 17.2 %copy-start.6 = (s32[1,128]{1,0:T(1,128)S(1)}, s32[1,128]{1,0:T(1,128)}, u32[]{:S(2)}) copy-start(s32[1,128]{1,0:T(1,128)} %param.17) | copy-start | bytes 1540
  224.6 17.4 %all-to-all-start.2 = ((bf16[32,2,2048]{2,1,0:T(2,128)(2,1)}), bf16[32,2,2048]{2,1,0:T(2,128)(2,1)}, u32[]{:S(2)}, u32[]{:S(2)}) async-start(bf16[32,2,2048]{2,1,0:T(2,128)(2,1)} %reshape.289), calls=%async_computation.2 | async-start | bytes 524288 | tf_op jit(solution)/shard_map/all_to_all | solution.py:178
  247.9 1.4 copy-start.3
  247.9 1.4 copy-start.5
  247.9 1.4 copy-start.7
  247.9 1.4 copy-start.8
  248.1 1.6 copy-start.1
  251.4 26.6 %all-to-all-start.3 = ((bf16[32,128,96]{1,2,0:T(8,128)(2,1)}), bf16[32,128,96]{1,2,0:T(8,128)(2,1)S(1)}, u32[]{:S(2)}, u32[]{:S(2)}) async-start(bf16[32,128,96]{1,2,0:T(8,128)(2,1)} %bitcast.18), calls=%async_computation.3 | async-start | bytes 1572864 | tf_op jit(solution)/shard_map/all_to_all | solution.py:198
  283.1 26.3 %copy-start = (bf16[1,128,4096]{2,1,0:T(8,128)(2,1)S(1)}, bf16[1,128,4096]{2,1,0:T(8,128)(2,1)}, u32[]{:S(2)}) copy-start(bf16[1,128,4096]{2,1,0:T(8,128)(2,1)} %param.13) | copy-start | bytes 3145732
  304.4 16.1 %all-to-all-start.4 = ((bf16[32,128,32]{1,2,0:T(8,128)(2,1)}), bf16[32,128,32]{1,2,0:T(8,128)(2,1)S(1)}, u32[]{:S(2)}, u32[]{:S(2)}) async-start(bf16[32,128,32]{1,2,0:T(8,128)(2,1)} %copy_bitcast_fusion), calls=%async_computation.4 | async-start | bytes 524288 | tf_op jit(solution)/shard_map/all_to_all | solution.py:204
  320.9 3.6 %copy-start.2 = (bf16[128,512]{1,0:T(8,128)(2,1)}, bf16[128,512]{1,0:T(8,128)(2,1)S(1)}, u32[]{:S(2)}) copy-start(bf16[128,512]{1,0:T(8,128)(2,1)S(1)} %get-tuple-element.34) | copy-start | bytes 393220
Sparse Core Ops, SparseCore 0:
  12.4 126.3 all-gather.1

commit v6 on v3

--- a/solution.py
+++ b/solution.py
@@ -49,20 +49,22 @@
     layout = packed.reshape(row_count, 3, heads, head_size)
     layout = jnp.repeat(layout, query_parts, axis=2)
     layout = layout.reshape(row_count, 3, seq_count, local_heads, head_size).transpose(
-        2, 0, 1, 3, 4
-    )
-    return layout.reshape(seq_count, row_count, 3 * local_heads * head_size)
+        2, 1, 0, 3, 4
+    )
+    return layout.reshape(seq_count, 3, row_count, local_heads * head_size)
 
 
 def attend_heads(incoming, key_ok, heads, query_part, query_parts):
-    sources, row_count, triple_width = incoming.shape
+    sources, _, row_count, piece_width = incoming.shape
     local_heads = max(heads // sources, 1)
-    head_size = triple_width // (3 * local_heads)
+    head_size = piece_width // local_heads
     all_rows = sources * row_count
-    layout = incoming.reshape(all_rows, 3, local_heads, head_size)
+    thirds = [
+        incoming[:, third].reshape(all_rows, local_heads, head_size) for third in range(3)
+    ]
     query_rows = all_rows // query_parts
-    queries = lax.dynamic_slice_in_dim(layout[:, 0], query_part * query_rows, query_rows, 0)
-    return attend_rows(queries, layout[:, 1], layout[:, 2], key_ok)
+    queries = lax.dynamic_slice_in_dim(thirds[0], query_part * query_rows, query_rows, 0)
+    return attend_rows(queries, thirds[1], thirds[2], key_ok)
 
 
 def place_rows(mixed_part, all_rows, query_part, sources):
@@ -154,7 +156,7 @@
     in_marks = lax.all_to_all(key_marks, "seq", split_axis=0, concat_axis=0, tiled=True)
     key_ok = in_marks.reshape(-1) > 0.5
     mixed_part = attend_heads(incoming, key_ok, ENC_HEADS, enc_part, enc_parts)
-    returning = place_rows(mixed_part, incoming.shape[0] * incoming.shape[1], enc_part, seq_count)
+    returning = place_rows(mixed_part, incoming.shape[0] * incoming.shape[2], enc_part, seq_count)
     returned = lax.all_to_all(returning, "seq", split_axis=0, concat_axis=0, tiled=True)
     mixed_rows = collect_heads(returned, ENC_HEADS, enc_parts)
     encoded = kept_rows.astype(jnp.float32) + weight_dot(mixed_rows, full_merge)
@@ -180,7 +182,7 @@
         (incoming, dec_weights[1], dec_weights[2])
     )
     mixed_part = attend_heads(incoming, None, DEC_HEADS, dec_part, dec_parts)
-    returning = place_rows(mixed_part, incoming.shape[0] * incoming.shape[1], dec_part, seq_count)
+    returning = place_rows(mixed_part, incoming.shape[0] * incoming.shape[2], dec_part, seq_count)
     returned = lax.all_to_all(returning, "seq", split_axis=0, concat_axis=0, tiled=True)
     mixed_rows = collect_heads(returned, DEC_HEADS, dec_parts)
     decoded = (

time: 322 us -> 310 us (0.963)
  local copies, waits for them, and re-layouts: 77.6 us -> 71.9 us
  waiting for transfers between devices: 147 us -> 142 us
    reshape x3 -> x0, local copies, waits for them, and re-layouts: 5.48 us -> none  [the longest x2 3.86 us: attend_heads(): layout = incoming.reshape(all_rows, 3, local_heads, head_size)]
    all_to_all x2, waiting for transfers between devices: 18.4 us -> 13.1 us  [shards(): lax.all_to_all(outgoing, 'seq', split_axis=0, concat_axis=0, tiled=True)]
    unnamed x25 -> x26, local copies, waits for them, and re-layouts: 5.67 us -> 7.56 us
where the time goes in v6:
time: 310 us; the launch traced here: 309 us
  waiting for transfers between devices  142 us (46%)
  local copies, waits for them, and re-layouts  71.9 us (23%)
  matrix products  34.2 us (11%)
  starting transfers between devices  33.5 us (11%)
  between operations  14.5 us (5%)
  other arithmetic  12.6 us (4%)
    all_gather x1, waiting for transfers between devices, gather_weights(): every = lax.all_gather(flat, ('dp', 'seq'), axis=0, tiled=True)  106 us
    reshape x6, local copies, waits for them, and re-layouts, gather_weights(): wholes.append(part.reshape(sources * piece.shape[0], piece.shape[1]))  27.5 us
    all_to_all x2, waiting for transfers between devices, shards(): lax.all_to_all(returning, 'seq', split_axis=0, concat_axis=0, tiled=True)  22.4 us
    slice x6, local copies, waits for them, and re-layouts, gather_weights(): part = tiles[:, start // lane:(start + size) // lane, :]  21.5 us
    all_to_all x2, waiting for transfers between devices, shards(): lax.all_to_all(outgoing, 'seq', split_axis=0, concat_axis=0, tiled=True)  13.1 us
    all_to_all x2, starting transfers between devices, shards(): lax.all_to_all(outgoing, 'seq', split_axis=0, concat_axis=0, tiled=True)  12 us
    dot_general x6, matrix products, one_block(): jnp.einsum('qk,kd->qd', weights, values_one, preferred_element_type=jnp.f...  11.6 us
    all_to_all x1, starting transfers between devices, shards(): lax.all_to_all(key_marks, 'seq', split_axis=0, concat_axis=0, tiled=True)  11.4 us
  transfers between devices with their start and end apart: 6, of which 5 were waited for; matrix products, arithmetic and copies ran while one was open for 21% of the time, Pallas kernels for 0%

profile of v6, /device:TPU:32, one launch (start us, length us, event | category | flops | bytes accessed | tf_op | source)
XLA Modules:
  0.0 308.6 jit_solution(3105786579131473163)
XLA Ops:
  7.2 0.7 copy.80
  8.0 0.7 copy.82
  8.6 0.7 reshape.225
  9.4 0.7 copy.83
  10.0 0.7 copy.84
  10.8 0.7 bitcast_dynamic-update-slice_fusion
  11.5 0.6 copy-done.6
  12.1 0.8 copy.50
  13.2 1.3 fusion.62
  14.5 0.6 compare_convert_fusion
  15.2 0.6 broadcast_in_dim.98
  15.8 11.4 %all-to-all-start = ((bf16[32,1,64]{2,1,0:T(2,128)(2,1)}), bf16[32,1,64]{2,1,0:T(2,128)(2,1)S(1)}, u32[]{:S(2)}, u32[]{:S(2)}) async-start(bf16[32,1,64]{2,1,0:T(2,128)(2,1)} %broadcast_in_dim.98), calls=%async_computation | async-start | bytes 32768 | tf_op jit(solution)/shard_map/all_to_all | solution.py:156
  27.2 5.2 %fusion.63 = (f32[64]{0:T(128)S(1)}, f32[64,1024]{1,0:T(8,128)S(1)}) fusion(bf16[4096,1024]{1,0:T(8,128)(2,1)} %param.18, bf16[1,128,4096]{2,1,0:T(8,128)(2,1)} %param.17, bf16[128,1024]{1,0:T(8,128)(2,1)} %param.20, f32[1024]{0:T(1024)} %param.19, s32[128]{0:T(128)S(1)} %get-tuple-element.125), kind=kOutput, calls=%fused_computation.119 | convolution fusion | flops 1091248128 | bytes 9966336 | tf_op jit(solution)/shard_map/dot_general | solution.py:145
  32.6 106.2 %all-gather.2.cloned.1.call-done = bf16[7864320]{0:T(1024)(128)(2,1)} async-done(((bf16[30720]{0:T(1024)(128)(2,1)}), bf16[7864320]{0:T(1024)(128)(2,1)}) %all-gather.2.cloned.1.call-update) | async-done | bytes 15728656 | tf_op jit(solution)/shard_map/all_gather | solution.py:90
  138.8 6.6 %slice.50 = bf16[256,96,128]{2,1,0:T(8,128)(2,1)} slice(bf16[256,240,128]{2,1,0:T(8,128)(2,1)} %bitcast.134), slice={[0:256], [0:96], [0:128]} | slice | bytes 12582912 | tf_op jit(solution)/shard_map/slice | solution.py:98
  145.4 10.3 %reshape.229 = bf16[1024,3072]{1,0:T(8,128)(2,1)} reshape(bf16[256,96,128]{2,1,0:T(8,128)(2,1)} %slice.50) | data formatting | bytes 12582912 | tf_op jit(solution)/shard_map/reshape | solution.py:99
  155.7 4.0 %convolution_convert_fusion = bf16[64,3072]{1,0:T(8,128)(2,1)S(1)} fusion(bf16[1024,3072]{1,0:T(8,128)(2,1)} %reshape.229, f32[64,1024]{1,0:T(8,128)S(1)} %get-tuple-element.127, f32[64]{0:T(128)S(1)} %add_rsqrt_fusion.4, f32[64]{0:T(128)S(1)} %broadcast_multiply_fusion.4), kind=kOutput, calls=%fused_computation.31 | convolution fusion | flops 403046400 | bytes 6947328 | tf_op jit(solution)/shard_map/dot_general | solution.py:105
  160.9 1.9 reshape.259
  162.8 7.5 %all-to-all-start.1 = ((bf16[32,2,6144]{2,1,0:T(2,128)(2,1)}), bf16[32,2,6144]{2,1,0:T(2,128)(2,1)}, u32[]{:S(2)}, u32[]{:S(2)}) async-start(bf16[32,2,6144]{2,1,0:T(2,128)(2,1)} %reshape.259), calls=%async_computation.1 | async-start | bytes 1572864 | tf_op jit(solution)/shard_map/all_to_all | solution.py:152
  170.5 3.3 %slice.51 = bf16[256,32,128]{2,1,0:T(8,128)(2,1)} slice(bf16[256,240,128]{2,1,0:T(8,128)(2,1)} %bitcast.135), slice={[0:256], [96:128], [0:128]} | slice | bytes 4194304 | tf_op jit(solution)/shard_map/slice | solution.py:98
  173.8 2.9 slice.53
  176.7 2.4 slice.52
  179.1 2.8 reshape.232
  182.0 4.3 %reshape.234 = bf16[512,1536]{1,0:T(8,128)(2,1)} reshape(bf16[256,24,128]{2,1,0:T(8,128)(2,1)} %slice.53) | data formatting | bytes 3145728 | tf_op jit(solution)/shard_map/reshape | solution.py:99
  186.2 2.5 reshape.233
  188.7 5.0 %all-to-all-done.1 = bf16[32,2,6144]{2,1,0:T(2,128)(2,1)} async-done(((bf16[32,2,6144]{2,1,0:T(2,128)(2,1)}), bf16[32,2,6144]{2,1,0:T(2,128)(2,1)}, u32[]{:S(2)}, u32[]{:S(2)}) %all-to-all-start.1) | async-done | bytes 786464 | tf_op jit(solution)/shard_map/all_to_all | solution.py:152
  193.7 3.8 %reshape.260 = bf16[32,3,64,64]{3,2,1,0:T(8,128)(2,1)} reshape(bf16[32,2,6144]{2,1,0:T(2,128)(2,1)} %all-to-all-done.1) | data formatting | bytes 1572864 | tf_op jit(solution)/shard_map/optimization_barrier | solution.py:153
  197.5 2.3 fusion.60
  199.8 6.1 %while.20 = (s32[]{:T(128)}, bf16[2,512,64]{1,2,0:T(8,128)(2,1)S(1)}, pred[2048]{0:T(1024)(128)(4,1)S(1)}, bf16[2,512,64]{2,1,0:T(8,128)(2,1)S(1)}, bf16[2048,64...) while((s32[]{:T(128)}, bf16[2,512,64]{1,2,0:T(8,128)(2,1)S(1)}, pred[2048]{0:T(1024)(128)(4,1)S(1)}, ...), condition=%wide.region_7.8_spmd, body=%wide.region_4.7_spmd.sunk | while | flops 281050112 | bytes 14893169 | solution.py:40
  199.8 0.8 fusion.92
  200.6 0.9 fusion.93
  201.6 1.3 fusion.94
  202.9 0.8 fusion.92
  203.7 0.9 fusion.93
  204.6 1.3 fusion.94
  206.7 1.1 reshape.261
  207.8 5.1 %all-to-all-start.2 = ((bf16[32,2,2048]{2,1,0:T(2,128)(2,1)}), bf16[32,2,2048]{2,1,0:T(2,128)(2,1)S(1)}, u32[]{:S(2)}, u32[]{:S(2)}) async-start(bf16[32,2,2048]{2,1,0:T(2,128)(2,1)} %reshape.261), calls=%async_computation.2 | async-start | bytes 524288 | tf_op jit(solution)/shard_map/all_to_all | solution.py:160
  213.0 11.8 %all-to-all-done.2 = bf16[32,2,2048]{2,1,0:T(2,128)(2,1)S(1)} async-done(((bf16[32,2,2048]{2,1,0:T(2,128)(2,1)}), bf16[32,2,2048]{2,1,0:T(2,128)(2,1)S(1)}, u32[]{:S(2)}, u32[]{:S(2)}) %all-to-all-start.2) | async-done | bytes 262176 | tf_op jit(solution)/shard_map/all_to_all | solution.py:160
  226.1 1.7 fusion.45
  227.8 0.8 gather_fusion
  229.7 1.0 broadcast_in_dim.104
  230.7 4.6 %all-to-all-start.3 = ((bf16[32,3,128,32]{2,3,1,0:T(8,128)(2,1)}), bf16[32,3,128,32]{2,3,1,0:T(8,128)(2,1)S(1)}, u32[]{:S(2)}, u32[]{:S(2)}) async-start(bf16[32,3,128,32]{2,3,1,0:T(8,128)(2,1)} %bitcast.22), calls=%async_computation.3 | async-start | bytes 1572864 | tf_op jit(solution)/shard_map/all_to_all | solution.py:180
  235.3 5.2 %slice.55 = bf16[256,64,128]{2,1,0:T(8,128)(2,1)} slice(bf16[256,240,128]{2,1,0:T(8,128)(2,1)} %bitcast.138), slice={[0:256], [176:240], [0:128]} | slice | bytes 8388608 | tf_op jit(solution)/shard_map/slice | solution.py:98
  240.5 1.1 slice.54
  241.6 7.3 %reshape.242 = bf16[512,4096]{1,0:T(8,128)(2,1)} reshape(bf16[256,64,128]{2,1,0:T(8,128)(2,1)} %slice.55) | data formatting | bytes 8388608 | tf_op jit(solution)/shard_map/reshape | solution.py:99
  249.2 8.1 %all-to-all-done.3 = bf16[32,3,128,32]{2,3,1,0:T(8,128)(2,1)S(1)} async-done(((bf16[32,3,128,32]{2,3,1,0:T(8,128)(2,1)}), bf16[32,3,128,32]{2,3,1,0:T(8,128)(2,1)S(1)}, u32[]{:S(2)}, u32[]{:S(2)}) %all-to-all-start.3) | async-done | bytes 786464 | tf_op jit(solution)/shard_map/all_to_all | solution.py:180
  258.4 1.3 copy.70
  259.8 20.5 %while.21 = (s32[]{:T(128)}, bf16[4,512,32]{1,2,0:T(8,128)(2,1)S(1)}, bf16[4,512,32]{2,1,0:T(8,128)(2,1)S(1)}, bf16[4096,32]{1,0:T(8,128)(2,1)S(1)}, bf16[4096,32]{1,0:T(8,128)(2,1)}, /*index=5*/s32[]{:T(128)}) while((s32[]{:T(128)}, bf16[4,512,32]{1,2,0:T(8,128)(2,1)S(1)}, bf16[4,512,32]{2,1,0:T(8,128)(2,1)S(1)}, ...), condition=%wide.region_16.17_spmd, body=%wide.region_13.16_spmd.sunk | while | flops 287325184 | bytes 28485736 | solution.py:40
  259.8 1.3 multiply_reduce_fusion.4
  261.1 1.5 fusion.97
  262.6 2.3 fusion.98
  264.9 1.3 multiply_reduce_fusion.4
  266.2 1.5 fusion.97
  267.8 2.3 fusion.98
  270.0 1.3 multiply_reduce_fusion.4
  271.4 1.5 fusion.97
  272.9 2.3 fusion.98
  275.2 1.3 multiply_reduce_fusion.4
  276.5 1.5 fusion.97
  278.0 2.3 fusion.98
  280.4 0.7 copy_bitcast_fusion
  281.1 4.9 %all-to-all-start.4 = ((bf16[32,128,32]{1,2,0:T(8,128)(2,1)}), bf16[32,128,32]{1,2,0:T(8,128)(2,1)S(1)}, u32[]{:S(2)}, u32[]{:S(2)}) async-start(bf16[32,128,32]{1,2,0:T(8,128)(2,1)} %copy_bitcast_fusion), calls=%async_computation.4 | async-start | bytes 524288 | tf_op jit(solution)/shard_map/all_to_all | solution.py:186
  286.7 10.6 %all-to-all-done.4 = bf16[32,128,32]{1,2,0:T(8,128)(2,1)S(1)} async-done(((bf16[32,128,32]{1,2,0:T(8,128)(2,1)}), bf16[32,128,32]{1,2,0:T(8,128)(2,1)S(1)}, u32[]{:S(2)}, u32[]{:S(2)}) %all-to-all-start.4) | async-done | bytes 262176 | tf_op jit(solution)/shard_map/all_to_all | solution.py:186
  297.9 3.4 %fusion.26 = f32[128]{0:T(128)S(1)} fusion(bf16[512,4096]{1,0:T(8,128)(2,1)} %reshape.242, bf16[1,128,4096]{2,1,0:T(8,128)(2,1)S(1)} %copy-done, f32[128]{0:T(128)S(1)} %get-tuple-element.132, f32[128]{0:T(128)S(1)} %broadcast_multiply_fusion, bf16[128,512]{1,0:T(8,128)(2,1)S(1)} %get-tuple-element.131, f32[128]{0:T(128)S(1)} %get-tuple-element.133, ...), kind=kOutput, calls=%fused_computation.38 | convolution fusion | flops 540278656 | bytes 5376512 | tf_op jit(solution)/shard_map/dot_general | solution.py:105
  (86 shorter events, 8.3 us)
Async XLA Ops:
  7.2 131.6 %all-gather.2.cloned.1.call-start = ((), (), s32[]{:S(2)}) async-start(), calls=%async_computation.5 | async-start | bytes 15790080 | tf_op jit(solution)/shard_map/all_gather | solution.py:90
  11.5 0.6 copy-start.6
  15.8 147.0 %all-to-all-start = ((bf16[32,1,64]{2,1,0:T(2,128)(2,1)}), bf16[32,1,64]{2,1,0:T(2,128)(2,1)S(1)}, u32[]{:S(2)}, u32[]{:S(2)}) async-start(bf16[32,1,64]{2,1,0:T(2,128)(2,1)} %broadcast_in_dim.98), calls=%async_computation | async-start | bytes 32768 | tf_op jit(solution)/shard_map/all_to_all | solution.py:156
  162.8 30.9 %all-to-all-start.1 = ((bf16[32,2,6144]{2,1,0:T(2,128)(2,1)}), bf16[32,2,6144]{2,1,0:T(2,128)(2,1)}, u32[]{:S(2)}, u32[]{:S(2)}) async-start(bf16[32,2,6144]{2,1,0:T(2,128)(2,1)} %reshape.259), calls=%async_computation.1 | async-start | bytes 1572864 | tf_op jit(solution)/shard_map/all_to_all | solution.py:152
  199.8 13.2 %copy-start.8 = (s32[1,128]{1,0:T(1,128)S(1)}, s32[1,128]{1,0:T(1,128)}, u32[]{:S(2)}) copy-start(s32[1,128]{1,0:T(1,128)} %param.21) | copy-start | bytes 1540
  199.8 1.8 copy-start.4
  202.9 1.7 copy-start.4
  207.8 17.0 %all-to-all-start.2 = ((bf16[32,2,2048]{2,1,0:T(2,128)(2,1)}), bf16[32,2,2048]{2,1,0:T(2,128)(2,1)S(1)}, u32[]{:S(2)}, u32[]{:S(2)}) async-start(bf16[32,2,2048]{2,1,0:T(2,128)(2,1)} %reshape.261), calls=%async_computation.2 | async-start | bytes 524288 | tf_op jit(solution)/shard_map/all_to_all | solution.py:160
  213.0 15.6 %copy-start.5 = (bf16[128,512]{1,0:T(8,128)(2,1)S(1)}, bf16[128,512]{1,0:T(8,128)(2,1)}, u32[]{:S(2)}) copy-start(bf16[128,512]{1,0:T(8,128)(2,1)} %param.26) | copy-start | bytes 393220
  213.0 15.6 %copy-start.7 = (f32[512]{0:T(512)S(1)}, f32[512]{0:T(512)}, u32[]{:S(2)}) copy-start(f32[512]{0:T(512)} %param.25) | copy-start | bytes 6148
  225.9 3.1 %copy-start.1 = (bf16[512,1536]{1,0:T(8,128)(2,1)S(1)}, bf16[512,1536]{1,0:T(8,128)(2,1)}, u32[]{:S(2)}) copy-start(bf16[512,1536]{1,0:T(8,128)(2,1)} %reshape.234) | copy-start | bytes 4718596
  230.7 26.6 %all-to-all-start.3 = ((bf16[32,3,128,32]{2,3,1,0:T(8,128)(2,1)}), bf16[32,3,128,32]{2,3,1,0:T(8,128)(2,1)S(1)}, u32[]{:S(2)}, u32[]{:S(2)}) async-start(bf16[32,3,128,32]{2,3,1,0:T(8,128)(2,1)} %bitcast.22), calls=%async_computation.3 | async-start | bytes 1572864 | tf_op jit(solution)/shard_map/all_to_all | solution.py:180
  259.8 26.3 %copy-start = (bf16[1,128,4096]{2,1,0:T(8,128)(2,1)S(1)}, bf16[1,128,4096]{2,1,0:T(8,128)(2,1)}, u32[]{:S(2)}) copy-start(bf16[1,128,4096]{2,1,0:T(8,128)(2,1)} %param.17) | copy-start | bytes 3145732
  261.1 1.5 copy-start.2
  266.2 1.5 copy-start.2
  271.4 1.5 copy-start.2
  276.5 1.5 copy-start.2
  281.1 16.2 %all-to-all-start.4 = ((bf16[32,128,32]{1,2,0:T(8,128)(2,1)}), bf16[32,128,32]{1,2,0:T(8,128)(2,1)S(1)}, u32[]{:S(2)}, u32[]{:S(2)}) async-start(bf16[32,128,32]{1,2,0:T(8,128)(2,1)} %copy_bitcast_fusion), calls=%async_computation.4 | async-start | bytes 524288 | tf_op jit(solution)/shard_map/all_to_all | solution.py:186
  297.6 3.6 %copy-start.3 = (bf16[128,512]{1,0:T(8,128)(2,1)}, bf16[128,512]{1,0:T(8,128)(2,1)S(1)}, u32[]{:S(2)}) copy-start(bf16[128,512]{1,0:T(8,128)(2,1)S(1)} %get-tuple-element.131) | copy-start | bytes 393220
Sparse Core Ops, SparseCore 0:
  12.4 126.3 all-gather.1

commit v7 on v6

--- a/solution.py
+++ b/solution.py
@@ -150,14 +150,13 @@
     key_marks = jnp.broadcast_to(present.astype(jnp.bfloat16)[None, :], (seq_count, slab_max))
     outgoing = spread_heads(packed, ENC_HEADS, seq_count)
     incoming = lax.all_to_all(outgoing, "seq", split_axis=0, concat_axis=0, tiled=True)
-    incoming, full_merge, full_lift, dec_weights[0] = lax.optimization_barrier(
-        (incoming, full_merge, full_lift, dec_weights[0])
-    )
+    incoming, full_merge, full_lift = lax.optimization_barrier((incoming, full_merge, full_lift))
     in_marks = lax.all_to_all(key_marks, "seq", split_axis=0, concat_axis=0, tiled=True)
     key_ok = in_marks.reshape(-1) > 0.5
     mixed_part = attend_heads(incoming, key_ok, ENC_HEADS, enc_part, enc_parts)
     returning = place_rows(mixed_part, incoming.shape[0] * incoming.shape[2], enc_part, seq_count)
     returned = lax.all_to_all(returning, "seq", split_axis=0, concat_axis=0, tiled=True)
+    returned, dec_weights[0] = lax.optimization_barrier((returned, dec_weights[0]))
     mixed_rows = collect_heads(returned, ENC_HEADS, enc_parts)
     encoded = kept_rows.astype(jnp.float32) + weight_dot(mixed_rows, full_merge)
     lifted_list = [
@@ -178,12 +177,11 @@
     ).astype(jnp.bfloat16)
     outgoing = spread_heads(dec_packed, DEC_HEADS, seq_count)
     incoming = lax.all_to_all(outgoing, "seq", split_axis=0, concat_axis=0, tiled=True)
-    incoming, dec_weights[1], dec_weights[2] = lax.optimization_barrier(
-        (incoming, dec_weights[1], dec_weights[2])
-    )
+    incoming, dec_weights[2] = lax.optimization_barrier((incoming, dec_weights[2]))
     mixed_part = attend_heads(incoming, None, DEC_HEADS, dec_part, dec_parts)
     returning = place_rows(mixed_part, incoming.shape[0] * incoming.shape[2], dec_part, seq_count)
     returned = lax.all_to_all(returning, "seq", split_axis=0, concat_axis=0, tiled=True)
+    returned, dec_weights[1] = lax.optimization_barrier((returned, dec_weights[1]))
     mixed_rows = collect_heads(returned, DEC_HEADS, dec_parts)
     decoded = (
         dec_in.astype(jnp.float32)

time: 310 us -> 313 us (level)
    all_to_all x2, waiting for transfers between devices: 13.1 us -> 21.8 us  [shards(): lax.all_to_all(outgoing, 'seq', split_axis=0, concat_axis=0, tiled=True)]
    all_to_all x2, waiting for transfers between devices: 22.4 us -> 13.9 us  [shards(): lax.all_to_all(returning, 'seq', split_axis=0, concat_axis=0, tiled=True)]
    unnamed x26 -> x24, local copies, waits for them, and re-layouts: 7.56 us -> 7.54 us
where the time goes in v7:
time: 313 us; the launch traced here: 311 us
  waiting for transfers between devices  142 us (45%)
  local copies, waits for them, and re-layouts  72.1 us (23%)
  matrix products  35.5 us (11%)
  starting transfers between devices  34 us (11%)
  between operations  14.5 us (5%)
  other arithmetic  12.6 us (4%)
    all_gather x1, waiting for transfers between devices, gather_weights(): every = lax.all_gather(flat, ('dp', 'seq'), axis=0, tiled=True)  106 us
    reshape x6, local copies, waits for them, and re-layouts, gather_weights(): wholes.append(part.reshape(sources * piece.shape[0], piece.shape[1]))  27.5 us
    all_to_all x2, waiting for transfers between devices, shards(): lax.all_to_all(outgoing, 'seq', split_axis=0, concat_axis=0, tiled=True)  21.8 us
    slice x6, local copies, waits for them, and re-layouts, gather_weights(): part = tiles[:, start // lane:(start + size) // lane, :]  21.6 us
    all_to_all x2, waiting for transfers between devices, shards(): lax.all_to_all(returning, 'seq', split_axis=0, concat_axis=0, tiled=True)  13.9 us
    all_to_all x2, starting transfers between devices, shards(): lax.all_to_all(outgoing, 'seq', split_axis=0, concat_axis=0, tiled=True)  12.6 us
    dot_general x6, matrix products, weight_dot(): return jnp.dot(rows, weight, preferred_element_type=jnp.float32)  11.8 us
    dot_general x6, matrix products, one_block(): jnp.einsum('qk,kd->qd', weights, values_one, preferred_element_type=jnp.f...  11.6 us
  transfers between devices with their start and end apart: 6, of which 5 were waited for; matrix products, arithmetic and copies ran while one was open for 21% of the time, Pallas kernels for 0%

profile of v7, /device:TPU:32, one launch (start us, length us, event | category | flops | bytes accessed | tf_op | source)
XLA Modules:
  0.0 310.8 jit_solution(17480880759049136996)
XLA Ops:
  7.2 0.7 copy.80
  8.0 0.7 copy.82
  8.6 0.7 reshape.225
  9.4 0.7 copy.83
  10.0 0.7 copy.84
  10.8 0.7 bitcast_dynamic-update-slice_fusion
  11.5 0.6 copy-done.5
  12.1 0.8 copy.50
  13.2 1.3 fusion.58
  14.5 0.6 compare_convert_fusion
  15.8 11.4 %all-to-all-start = ((bf16[32,1,64]{2,1,0:T(2,128)(2,1)}), bf16[32,1,64]{2,1,0:T(2,128)(2,1)S(1)}, u32[]{:S(2)}, u32[]{:S(2)}) async-start(bf16[32,1,64]{2,1,0:T(2,128)(2,1)} %broadcast_in_dim.98), calls=%async_computation | async-start | bytes 32768 | tf_op jit(solution)/shard_map/all_to_all | solution.py:154
  27.2 5.2 %fusion.62 = (f32[64]{0:T(128)S(1)}, f32[64,1024]{1,0:T(8,128)S(1)}) fusion(bf16[4096,1024]{1,0:T(8,128)(2,1)} %param.18, bf16[1,128,4096]{2,1,0:T(8,128)(2,1)} %param.17, bf16[128,1024]{1,0:T(8,128)(2,1)} %param.20, f32[1024]{0:T(1024)} %param.19, s32[128]{0:T(128)S(1)} %get-tuple-element.128), kind=kOutput, calls=%fused_computation.118 | convolution fusion | flops 1091248128 | bytes 9966336 | tf_op jit(solution)/shard_map/dot_general | solution.py:145
  32.6 106.2 %all-gather.2.cloned.1.call-done = bf16[7864320]{0:T(1024)(128)(2,1)} async-done(((bf16[30720]{0:T(1024)(128)(2,1)}), bf16[7864320]{0:T(1024)(128)(2,1)}) %all-gather.2.cloned.1.call-update) | async-done | bytes 15728656 | tf_op jit(solution)/shard_map/all_gather | solution.py:90
  138.8 6.6 %slice.50 = bf16[256,96,128]{2,1,0:T(8,128)(2,1)} slice(bf16[256,240,128]{2,1,0:T(8,128)(2,1)} %bitcast.133), slice={[0:256], [0:96], [0:128]} | slice | bytes 12582912 | tf_op jit(solution)/shard_map/slice | solution.py:98
  145.4 10.3 %reshape.229 = bf16[1024,3072]{1,0:T(8,128)(2,1)} reshape(bf16[256,96,128]{2,1,0:T(8,128)(2,1)} %slice.50) | data formatting | bytes 12582912 | tf_op jit(solution)/shard_map/reshape | solution.py:99
  155.7 4.0 %convolution_convert_fusion = bf16[64,3072]{1,0:T(8,128)(2,1)S(1)} fusion(bf16[1024,3072]{1,0:T(8,128)(2,1)} %reshape.229, f32[64,1024]{1,0:T(8,128)S(1)} %get-tuple-element.131, f32[64]{0:T(128)S(1)} %add_rsqrt_fusion.4, f32[64]{0:T(128)S(1)} %broadcast_multiply_fusion.4), kind=kOutput, calls=%fused_computation.31 | convolution fusion | flops 403046400 | bytes 6947328 | tf_op jit(solution)/shard_map/dot_general | solution.py:105
  160.9 1.9 reshape.259
  162.8 7.5 %all-to-all-start.1 = ((bf16[32,2,6144]{2,1,0:T(2,128)(2,1)}), bf16[32,2,6144]{2,1,0:T(2,128)(2,1)}, u32[]{:S(2)}, u32[]{:S(2)}) async-start(bf16[32,2,6144]{2,1,0:T(2,128)(2,1)} %reshape.259), calls=%async_computation.1 | async-start | bytes 1572864 | tf_op jit(solution)/shard_map/all_to_all | solution.py:152
  170.4 3.3 %slice.51 = bf16[256,32,128]{2,1,0:T(8,128)(2,1)} slice(bf16[256,240,128]{2,1,0:T(8,128)(2,1)} %bitcast.134), slice={[0:256], [96:128], [0:128]} | slice | bytes 4194304 | tf_op jit(solution)/shard_map/slice | solution.py:98
  173.8 2.5 slice.52
  176.3 2.8 reshape.232
  179.1 2.5 reshape.233
  181.6 12.1 %all-to-all-done.1 = bf16[32,2,6144]{2,1,0:T(2,128)(2,1)} async-done(((bf16[32,2,6144]{2,1,0:T(2,128)(2,1)}), bf16[32,2,6144]{2,1,0:T(2,128)(2,1)}, u32[]{:S(2)}, u32[]{:S(2)}) %all-to-all-start.1) | async-done | bytes 786464 | tf_op jit(solution)/shard_map/all_to_all | solution.py:152
  193.7 3.8 %reshape.260 = bf16[32,3,64,64]{3,2,1,0:T(8,128)(2,1)} reshape(bf16[32,2,6144]{2,1,0:T(2,128)(2,1)} %all-to-all-done.1) | data formatting | bytes 1572864 | tf_op jit(solution)/shard_map/optimization_barrier | solution.py:153
  197.5 2.3 fusion.60
  199.8 6.1 %while.20 = (s32[]{:T(128)}, bf16[2,512,64]{1,2,0:T(8,128)(2,1)S(1)}, pred[2048]{0:T(1024)(128)(4,1)S(1)}, bf16[2,512,64]{2,1,0:T(8,128)(2,1)S(1)}, bf16[2048,64...) while((s32[]{:T(128)}, bf16[2,512,64]{1,2,0:T(8,128)(2,1)S(1)}, pred[2048]{0:T(1024)(128)(4,1)S(1)}, ...), condition=%wide.region_7.8_spmd, body=%wide.region_4.7_spmd.sunk | while | flops 281050112 | bytes 14893169 | solution.py:40
  199.8 0.8 fusion.91
  200.6 0.9 fusion.92
  201.6 1.3 fusion.93
  202.9 0.8 fusion.91
  203.6 0.9 fusion.92
  204.6 1.3 fusion.93
  206.7 1.1 reshape.261
  207.8 5.1 %all-to-all-start.2 = ((bf16[32,2,2048]{2,1,0:T(2,128)(2,1)}), bf16[32,2,2048]{2,1,0:T(2,128)(2,1)S(1)}, u32[]{:S(2)}, u32[]{:S(2)}) async-start(bf16[32,2,2048]{2,1,0:T(2,128)(2,1)} %reshape.261), calls=%async_computation.2 | async-start | bytes 524288 | tf_op jit(solution)/shard_map/all_to_all | solution.py:158
  213.0 2.9 slice.53
  215.9 4.3 %reshape.235 = bf16[512,1536]{1,0:T(8,128)(2,1)} reshape(bf16[256,24,128]{2,1,0:T(8,128)(2,1)} %slice.53) | data formatting | bytes 3145728 | tf_op jit(solution)/shard_map/reshape | solution.py:99
  220.1 4.7 %all-to-all-done.2 = bf16[32,2,2048]{2,1,0:T(2,128)(2,1)S(1)} async-done(((bf16[32,2,2048]{2,1,0:T(2,128)(2,1)}), bf16[32,2,2048]{2,1,0:T(2,128)(2,1)S(1)}, u32[]{:S(2)}, u32[]{:S(2)}) %all-to-all-start.2) | async-done | bytes 262176 | tf_op jit(solution)/shard_map/all_to_all | solution.py:158
  226.1 1.6 fusion.45
  227.7 0.8 gather_fusion
  228.9 1.8 convolution_convert_fusion.1
  231.0 1.0 broadcast_in_dim.104
  232.0 5.1 %all-to-all-start.3 = ((bf16[32,3,128,32]{2,3,1,0:T(8,128)(2,1)}), bf16[32,3,128,32]{2,3,1,0:T(8,128)(2,1)S(1)}, u32[]{:S(2)}, u32[]{:S(2)}) async-start(bf16[32,3,128,32]{2,3,1,0:T(8,128)(2,1)} %bitcast.22), calls=%async_computation.3 | async-start | bytes 1572864 | tf_op jit(solution)/shard_map/all_to_all | solution.py:179
  237.1 5.2 %slice.54 = bf16[256,64,128]{2,1,0:T(8,128)(2,1)} slice(bf16[256,240,128]{2,1,0:T(8,128)(2,1)} %bitcast.137), slice={[0:256], [176:240], [0:128]} | slice | bytes 8388608 | tf_op jit(solution)/shard_map/slice | solution.py:98
  242.3 7.3 %reshape.241 = bf16[512,4096]{1,0:T(8,128)(2,1)} reshape(bf16[256,64,128]{2,1,0:T(8,128)(2,1)} %slice.54) | data formatting | bytes 8388608 | tf_op jit(solution)/shard_map/reshape | solution.py:99
  249.7 9.7 %all-to-all-done.3 = bf16[32,3,128,32]{2,3,1,0:T(8,128)(2,1)S(1)} async-done(((bf16[32,3,128,32]{2,3,1,0:T(8,128)(2,1)}), bf16[32,3,128,32]{2,3,1,0:T(8,128)(2,1)S(1)}, u32[]{:S(2)}, u32[]{:S(2)}) %all-to-all-start.3) | async-done | bytes 786464 | tf_op jit(solution)/shard_map/all_to_all | solution.py:179
  260.4 1.3 copy.70
  261.8 20.5 %while.21 = (s32[]{:T(128)}, bf16[4,512,32]{1,2,0:T(8,128)(2,1)S(1)}, bf16[4,512,32]{2,1,0:T(8,128)(2,1)S(1)}, bf16[4096,32]{1,0:T(8,128)(2,1)S(1)}, bf16[4096,32]{1,0:T(8,128)(2,1)}, /*index=5*/s32[]{:T(128)}) while((s32[]{:T(128)}, bf16[4,512,32]{1,2,0:T(8,128)(2,1)S(1)}, bf16[4,512,32]{2,1,0:T(8,128)(2,1)S(1)}, ...), condition=%wide.region_16.17_spmd, body=%wide.region_13.16_spmd.sunk | while | flops 287325184 | bytes 28485736 | solution.py:40
  261.8 1.3 multiply_reduce_fusion.4
  263.1 1.5 fusion.96
  264.6 2.3 fusion.97
  266.9 1.3 multiply_reduce_fusion.4
  268.3 1.5 fusion.96
  269.8 2.3 fusion.97
  272.0 1.3 multiply_reduce_fusion.4
  273.4 1.5 fusion.96
  274.9 2.3 fusion.97
  277.2 1.3 multiply_reduce_fusion.4
  278.5 1.5 fusion.96
  280.0 2.3 fusion.97
  282.4 0.8 copy_bitcast_fusion
  283.1 4.9 %all-to-all-start.4 = ((bf16[32,128,32]{1,2,0:T(8,128)(2,1)}), bf16[32,128,32]{1,2,0:T(8,128)(2,1)S(1)}, u32[]{:S(2)}, u32[]{:S(2)}) async-start(bf16[32,128,32]{1,2,0:T(8,128)(2,1)} %copy_bitcast_fusion), calls=%async_computation.4 | async-start | bytes 524288 | tf_op jit(solution)/shard_map/all_to_all | solution.py:183
  288.8 1.1 slice.55
  290.2 9.2 %all-to-all-done.4 = bf16[32,128,32]{1,2,0:T(8,128)(2,1)S(1)} async-done(((bf16[32,128,32]{1,2,0:T(8,128)(2,1)}), bf16[32,128,32]{1,2,0:T(8,128)(2,1)S(1)}, u32[]{:S(2)}, u32[]{:S(2)}) %all-to-all-start.4) | async-done | bytes 262176 | tf_op jit(solution)/shard_map/all_to_all | solution.py:183
  300.0 3.4 %fusion.26 = f32[128]{0:T(128)S(1)} fusion(bf16[512,4096]{1,0:T(8,128)(2,1)} %reshape.241, bf16[1,128,4096]{2,1,0:T(8,128)(2,1)S(1)} %copy-done, f32[128]{0:T(128)S(1)} %get-tuple-element.136, f32[128]{0:T(128)S(1)} %broadcast_multiply_fusion, bf16[128,512]{1,0:T(8,128)(2,1)S(1)} %get-tuple-element.135, f32[128]{0:T(128)S(1)} %get-tuple-element.137, ...), kind=kOutput, calls=%fused_computation.38 | convolution fusion | flops 540278656 | bytes 5376512 | tf_op jit(solution)/shard_map/dot_general | solution.py:105
  (84 shorter events, 8.5 us)
Async XLA Ops:
  7.2 131.6 %all-gather.2.cloned.1.call-start = ((), (), s32[]{:S(2)}) async-start(), calls=%async_computation.5 | async-start | bytes 15790080 | tf_op jit(solution)/shard_map/all_gather | solution.py:90
  11.5 0.6 copy-start.5
  15.8 147.0 %all-to-all-start = ((bf16[32,1,64]{2,1,0:T(2,128)(2,1)}), bf16[32,1,64]{2,1,0:T(2,128)(2,1)S(1)}, u32[]{:S(2)}, u32[]{:S(2)}) async-start(bf16[32,1,64]{2,1,0:T(2,128)(2,1)} %broadcast_in_dim.98), calls=%async_computation | async-start | bytes 32768 | tf_op jit(solution)/shard_map/all_to_all | solution.py:154
  162.8 30.9 %all-to-all-start.1 = ((bf16[32,2,6144]{2,1,0:T(2,128)(2,1)}), bf16[32,2,6144]{2,1,0:T(2,128)(2,1)}, u32[]{:S(2)}, u32[]{:S(2)}) async-start(bf16[32,2,6144]{2,1,0:T(2,128)(2,1)} %reshape.259), calls=%async_computation.1 | async-start | bytes 1572864 | tf_op jit(solution)/shard_map/all_to_all | solution.py:152
  199.8 13.2 %copy-start.7 = (s32[1,128]{1,0:T(1,128)S(1)}, s32[1,128]{1,0:T(1,128)}, u32[]{:S(2)}) copy-start(s32[1,128]{1,0:T(1,128)} %param.21) | copy-start | bytes 1540
  199.8 1.7 copy-start.3
  202.8 1.7 copy-start.3
  207.8 17.0 %all-to-all-start.2 = ((bf16[32,2,2048]{2,1,0:T(2,128)(2,1)}), bf16[32,2,2048]{2,1,0:T(2,128)(2,1)S(1)}, u32[]{:S(2)}, u32[]{:S(2)}) async-start(bf16[32,2,2048]{2,1,0:T(2,128)(2,1)} %reshape.261), calls=%async_computation.2 | async-start | bytes 524288 | tf_op jit(solution)/shard_map/all_to_all | solution.py:158
  220.1 8.3 %copy-start.4 = (bf16[128,512]{1,0:T(8,128)(2,1)S(1)}, bf16[128,512]{1,0:T(8,128)(2,1)}, u32[]{:S(2)}) copy-start(bf16[128,512]{1,0:T(8,128)(2,1)} %param.26) | copy-start | bytes 393220
  220.1 8.3 %copy-start.6 = (f32[512]{0:T(512)S(1)}, f32[512]{0:T(512)}, u32[]{:S(2)}) copy-start(f32[512]{0:T(512)} %param.25) | copy-start | bytes 6148
  232.0 27.3 %all-to-all-start.3 = ((bf16[32,3,128,32]{2,3,1,0:T(8,128)(2,1)}), bf16[32,3,128,32]{2,3,1,0:T(8,128)(2,1)S(1)}, u32[]{:S(2)}, u32[]{:S(2)}) async-start(bf16[32,3,128,32]{2,3,1,0:T(8,128)(2,1)} %bitcast.22), calls=%async_computation.3 | async-start | bytes 1572864 | tf_op jit(solution)/shard_map/all_to_all | solution.py:179
  261.8 26.3 %copy-start = (bf16[1,128,4096]{2,1,0:T(8,128)(2,1)S(1)}, bf16[1,128,4096]{2,1,0:T(8,128)(2,1)}, u32[]{:S(2)}) copy-start(bf16[1,128,4096]{2,1,0:T(8,128)(2,1)} %param.17) | copy-start | bytes 3145732
  263.1 1.5 copy-start.1
  268.2 1.5 copy-start.1
  273.4 1.5 copy-start.1
  278.5 1.5 copy-start.1
  283.1 16.3 %all-to-all-start.4 = ((bf16[32,128,32]{1,2,0:T(8,128)(2,1)}), bf16[32,128,32]{1,2,0:T(8,128)(2,1)S(1)}, u32[]{:S(2)}, u32[]{:S(2)}) async-start(bf16[32,128,32]{1,2,0:T(8,128)(2,1)} %copy_bitcast_fusion), calls=%async_computation.4 | async-start | bytes 524288 | tf_op jit(solution)/shard_map/all_to_all | solution.py:183
  299.8 3.6 %copy-start.2 = (bf16[128,512]{1,0:T(8,128)(2,1)}, bf16[128,512]{1,0:T(8,128)(2,1)S(1)}, u32[]{:S(2)}) copy-start(bf16[128,512]{1,0:T(8,128)(2,1)S(1)} %get-tuple-element.135) | copy-start | bytes 393220
Sparse Core Ops, SparseCore 0:
  12.4 126.3 all-gather.1

commit v8 on v6

--- a/solution.py
+++ b/solution.py
@@ -126,8 +126,27 @@
     dec_parts = max(seq_count // DEC_HEADS, 1)
     enc_part = seq_place % enc_parts
     dec_part = seq_place % dec_parts
-    (full_project, full_merge, full_lift, *dec_weights) = gather_weights(
-        (enc_project, enc_merge, dec_lift, dec_project, dec_merge, dec_predict)
+    project_rows, project_width = enc_project.shape
+    tile_rows = 2 * project_rows
+    partner = lax.ppermute(
+        enc_project, "seq", perm=[(place, place ^ 1) for place in range(seq_count)]
+    )
+    half = seq_place % 2
+    tile_block = jnp.where(
+        half == 0,
+        jnp.concatenate([enc_project, partner], axis=0),
+        jnp.concatenate([partner, enc_project], axis=0),
+    )
+    own_width = project_width // 2
+    own_block = lax.dynamic_slice_in_dim(tile_block, half * own_width, own_width, axis=1)
+    own_block = own_block.reshape(tile_rows, own_width // 128, 128).transpose(1, 0, 2).reshape(-1, 128)
+    (tiled_project, full_merge, full_lift, *dec_weights) = gather_weights(
+        (own_block, enc_merge, dec_lift, dec_project, dec_merge, dec_predict)
+    )
+    full_project = (
+        tiled_project.reshape(-1, 2, own_width // 128, tile_rows, 128)
+        .transpose(0, 3, 1, 2, 4)
+        .reshape(-1, project_width)
     )
     tok_local = voxels.shape[1]
     slab_max = tok_local // 2

time: 310 us -> 299 us (0.965)
  local copies, waits for them, and re-layouts: 71.9 us -> 59.2 us
    reshape x6 -> x5, local copies, waits for them, and re-layouts: 27.5 us -> 17.2 us  [gather_weights(): wholes.append(part.reshape(sources * piece.shape[0], piece.shape[1]))]
    unnamed x26 -> x24, local copies, waits for them, and re-layouts: 7.56 us -> 6.81 us
  transfers between devices with their start and end apart: 6 -> 7, of which waited for: 5 -> 5; matrix products, arithmetic and copies ran while one was open for 21% -> 18% of each run, Pallas kernels for 0% -> 0%
where the time goes in v8:
time: 299 us; the launch traced here: 298 us
  waiting for transfers between devices  142 us (47%)
  local copies, waits for them, and re-layouts  59.2 us (20%)
  starting transfers between devices  34.8 us (12%)
  matrix products  33.9 us (11%)
  between operations  14.5 us (5%)
  other arithmetic  13.5 us (5%)
    all_gather x1, waiting for transfers between devices, gather_weights(): every = lax.all_gather(flat, ('dp', 'seq'), axis=0, tiled=True)  106 us
    all_to_all x2, waiting for transfers between devices, shards(): lax.all_to_all(returning, 'seq', split_axis=0, concat_axis=0, tiled=True)  22.3 us
    slice x6, local copies, waits for them, and re-layouts, gather_weights(): part = tiles[:, start // lane:(start + size) // lane, :]  18.9 us
    reshape x5, local copies, waits for them, and re-layouts, gather_weights(): wholes.append(part.reshape(sources * piece.shape[0], piece.shape[1]))  17.2 us
    dot_general x6, matrix products, one_block(): jnp.einsum('qk,kd->qd', weights, values_one, preferred_element_type=jnp.f...  14.1 us
    all_to_all x2, waiting for transfers between devices, shards(): lax.all_to_all(outgoing, 'seq', split_axis=0, concat_axis=0, tiled=True)  13.1 us
    all_to_all x2, starting transfers between devices, shards(): lax.all_to_all(outgoing, 'seq', split_axis=0, concat_axis=0, tiled=True)  12 us
    all_to_all x1, starting transfers between devices, shards(): lax.all_to_all(key_marks, 'seq', split_axis=0, concat_axis=0, tiled=True)  10.7 us
  transfers between devices with their start and end apart: 7, of which 5 were waited for; matrix products, arithmetic and copies ran while one was open for 18% of the time, Pallas kernels for 0%

profile of v8, /device:TPU:32, one launch (start us, length us, event | category | flops | bytes accessed | tf_op | source)
XLA Modules:
  0.0 297.5 jit_solution(7742464117648100111)
XLA Ops:
  7.2 1.9 collective-permute-start
  9.1 0.7 copy.81
  9.8 0.7 reshape.225
  10.5 0.7 copy.82
  11.2 0.7 copy.83
  11.9 0.9 fusion.60
  12.8 0.7 bitcast_dynamic-update-slice_fusion
  13.6 0.6 copy-done.6
  14.2 0.8 copy.50
  15.3 1.3 fusion.67
  16.6 0.6 compare_convert_fusion
  17.9 10.7 %all-to-all-start = ((bf16[32,1,64]{2,1,0:T(2,128)(2,1)}), bf16[32,1,64]{2,1,0:T(2,128)(2,1)S(1)}, u32[]{:S(2)}, u32[]{:S(2)}) async-start(bf16[32,1,64]{2,1,0:T(2,128)(2,1)} %broadcast_in_dim.98), calls=%async_computation | async-start | bytes 32768 | tf_op jit(solution)/shard_map/all_to_all | solution.py:175
  28.6 5.2 %fusion.68 = (f32[64]{0:T(128)S(1)}, f32[64,1024]{1,0:T(8,128)S(1)}) fusion(bf16[4096,1024]{1,0:T(8,128)(2,1)} %param.18, bf16[1,128,4096]{2,1,0:T(8,128)(2,1)} %param.17, bf16[128,1024]{1,0:T(8,128)(2,1)} %param.20, f32[1024]{0:T(1024)} %param.19, s32[128]{0:T(128)S(1)} %get-tuple-element.125), kind=kOutput, calls=%fused_computation.127 | convolution fusion | flops 1091248128 | bytes 9966336 | tf_op jit(solution)/shard_map/dot_general | solution.py:164
  34.0 106.1 %all-gather.2.cloned.1.call-done = bf16[7864320]{0:T(1024)(128)(2,1)} async-done(((bf16[30720]{0:T(1024)(128)(2,1)}), bf16[7864320]{0:T(1024)(128)(2,1)}) %all-gather.2.cloned.1.call-update) | async-done | bytes 15728656 | tf_op jit(solution)/shard_map/all_gather | solution.py:90
  140.1 4.0 %slice.50 = bf16[256,96,128]{2,1,0:T(8,128)(2,1)S(1)} slice(bf16[256,240,128]{2,1,0:T(8,128)(2,1)} %bitcast.146), slice={[0:256], [0:96], [0:128]} | slice | bytes 12582912 | tf_op jit(solution)/shard_map/slice | solution.py:98
  144.1 1.3 convolution_convert_fusion
  146.5 1.9 reshape.259
  148.4 7.5 %all-to-all-start.1 = ((bf16[32,2,6144]{2,1,0:T(2,128)(2,1)}), bf16[32,2,6144]{2,1,0:T(2,128)(2,1)}, u32[]{:S(2)}, u32[]{:S(2)}) async-start(bf16[32,2,6144]{2,1,0:T(2,128)(2,1)} %reshape.259), calls=%async_computation.1 | async-start | bytes 1572864 | tf_op jit(solution)/shard_map/all_to_all | solution.py:171
  156.1 3.3 %slice.51 = bf16[256,32,128]{2,1,0:T(8,128)(2,1)} slice(bf16[256,240,128]{2,1,0:T(8,128)(2,1)} %bitcast.147), slice={[0:256], [96:128], [0:128]} | slice | bytes 4194304 | tf_op jit(solution)/shard_map/slice | solution.py:98
  159.4 2.9 slice.53
  162.3 2.4 slice.52
  164.7 2.8 reshape.232
  167.5 4.3 %reshape.234 = bf16[512,1536]{1,0:T(8,128)(2,1)} reshape(bf16[256,24,128]{2,1,0:T(8,128)(2,1)} %slice.53) | data formatting | bytes 3145728 | tf_op jit(solution)/shard_map/reshape | solution.py:99
  171.8 2.5 reshape.233
  174.3 5.0 %all-to-all-done.1 = bf16[32,2,6144]{2,1,0:T(2,128)(2,1)} async-done(((bf16[32,2,6144]{2,1,0:T(2,128)(2,1)}), bf16[32,2,6144]{2,1,0:T(2,128)(2,1)}, u32[]{:S(2)}, u32[]{:S(2)}) %all-to-all-start.1) | async-done | bytes 786464 | tf_op jit(solution)/shard_map/all_to_all | solution.py:171
  179.3 3.8 %reshape.260 = bf16[32,3,64,64]{3,2,1,0:T(8,128)(2,1)} reshape(bf16[32,2,6144]{2,1,0:T(2,128)(2,1)} %all-to-all-done.1) | data formatting | bytes 1572864 | tf_op jit(solution)/shard_map/optimization_barrier | solution.py:172
  183.1 2.3 fusion.65
  185.4 6.1 %while.20 = (s32[]{:T(128)}, bf16[2,512,64]{1,2,0:T(8,128)(2,1)S(1)}, pred[2048]{0:T(1024)(128)(4,1)S(1)}, bf16[2,512,64]{2,1,0:T(8,128)(2,1)S(1)}, bf16[2048,64...) while((s32[]{:T(128)}, bf16[2,512,64]{1,2,0:T(8,128)(2,1)S(1)}, pred[2048]{0:T(1024)(128)(4,1)S(1)}, ...), condition=%wide.region_7.8_spmd, body=%wide.region_4.7_spmd.sunk | while | flops 281050112 | bytes 14893169 | solution.py:40
  185.4 0.8 fusion.97
  186.2 0.9 fusion.98
  187.2 1.3 fusion.99
  188.5 0.8 fusion.97
  189.3 0.9 fusion.98
  190.2 1.3 fusion.99
  192.3 1.1 reshape.261
  193.4 5.1 %all-to-all-start.2 = ((bf16[32,2,2048]{2,1,0:T(2,128)(2,1)}), bf16[32,2,2048]{2,1,0:T(2,128)(2,1)S(1)}, u32[]{:S(2)}, u32[]{:S(2)}) async-start(bf16[32,2,2048]{2,1,0:T(2,128)(2,1)} %reshape.261), calls=%async_computation.2 | async-start | bytes 524288 | tf_op jit(solution)/shard_map/all_to_all | solution.py:179
  198.6 11.8 %all-to-all-done.2 = bf16[32,2,2048]{2,1,0:T(2,128)(2,1)S(1)} async-done(((bf16[32,2,2048]{2,1,0:T(2,128)(2,1)}), bf16[32,2,2048]{2,1,0:T(2,128)(2,1)S(1)}, u32[]{:S(2)}, u32[]{:S(2)}) %all-to-all-start.2) | async-done | bytes 262176 | tf_op jit(solution)/shard_map/all_to_all | solution.py:179
  211.8 1.7 fusion.45
  213.4 0.8 gather_fusion
  215.3 1.0 broadcast_in_dim.104
  216.3 4.6 %all-to-all-start.3 = ((bf16[32,3,128,32]{2,3,1,0:T(8,128)(2,1)}), bf16[32,3,128,32]{2,3,1,0:T(8,128)(2,1)S(1)}, u32[]{:S(2)}, u32[]{:S(2)}) async-start(bf16[32,3,128,32]{2,3,1,0:T(8,128)(2,1)} %bitcast.28), calls=%async_computation.3 | async-start | bytes 1572864 | tf_op jit(solution)/shard_map/all_to_all | solution.py:199
  220.9 5.2 %slice.55 = bf16[256,64,128]{2,1,0:T(8,128)(2,1)} slice(bf16[256,240,128]{2,1,0:T(8,128)(2,1)} %bitcast.150), slice={[0:256], [176:240], [0:128]} | slice | bytes 8388608 | tf_op jit(solution)/shard_map/slice | solution.py:98
  226.1 1.1 slice.54
  227.2 7.3 %reshape.242 = bf16[512,4096]{1,0:T(8,128)(2,1)} reshape(bf16[256,64,128]{2,1,0:T(8,128)(2,1)} %slice.55) | data formatting | bytes 8388608 | tf_op jit(solution)/shard_map/reshape | solution.py:99
  234.8 8.1 %all-to-all-done.3 = bf16[32,3,128,32]{2,3,1,0:T(8,128)(2,1)S(1)} async-done(((bf16[32,3,128,32]{2,3,1,0:T(8,128)(2,1)}), bf16[32,3,128,32]{2,3,1,0:T(8,128)(2,1)S(1)}, u32[]{:S(2)}, u32[]{:S(2)}) %all-to-all-start.3) | async-done | bytes 786464 | tf_op jit(solution)/shard_map/all_to_all | solution.py:199
  244.0 1.3 copy.70
  245.4 23.0 %while.21 = (s32[]{:T(128)}, bf16[4,512,32]{1,2,0:T(8,128)(2,1)}, bf16[4,512,32]{2,1,0:T(8,128)(2,1)S(1)}, bf16[4096,32]{1,0:T(8,128)(2,1)S(1)}, bf16[4096,32]{1,0:T(8,128)(2,1)}, /*index=5*/s32[]{:T(128)}) while((s32[]{:T(128)}, bf16[4,512,32]{1,2,0:T(8,128)(2,1)}, bf16[4,512,32]{2,1,0:T(8,128)(2,1)S(1)}, bf16[4096,32]{1,0:T(8,128)(2,1)S(1)}, ...), condition=%wide.region_16.17_spmd, body=%wide.region_13.16_spmd.sunk | while | flops 287325184 | bytes 27699812 | solution.py:40
  245.4 1.3 multiply_reduce_fusion.4
  246.7 1.5 fusion.102
  248.2 2.9 fusion.103
  251.1 1.3 multiply_reduce_fusion.4
  252.5 1.5 fusion.102
  254.0 2.9 fusion.103
  256.9 1.3 multiply_reduce_fusion.4
  258.2 1.5 fusion.102
  259.7 2.9 fusion.103
  262.6 1.3 multiply_reduce_fusion.4
  263.9 1.5 fusion.102
  265.4 2.9 fusion.103
  268.3 0.9 copy.79
  269.3 0.7 copy_bitcast_fusion
  270.0 4.9 %all-to-all-start.4 = ((bf16[32,128,32]{1,2,0:T(8,128)(2,1)}), bf16[32,128,32]{1,2,0:T(8,128)(2,1)S(1)}, u32[]{:S(2)}, u32[]{:S(2)}) async-start(bf16[32,128,32]{1,2,0:T(8,128)(2,1)} %copy_bitcast_fusion), calls=%async_computation.4 | async-start | bytes 524288 | tf_op jit(solution)/shard_map/all_to_all | solution.py:205
  275.6 10.5 %all-to-all-done.4 = bf16[32,128,32]{1,2,0:T(8,128)(2,1)S(1)} async-done(((bf16[32,128,32]{1,2,0:T(8,128)(2,1)}), bf16[32,128,32]{1,2,0:T(8,128)(2,1)S(1)}, u32[]{:S(2)}, u32[]{:S(2)}) %all-to-all-start.4) | async-done | bytes 262176 | tf_op jit(solution)/shard_map/all_to_all | solution.py:205
  286.7 3.4 %fusion.26 = f32[128]{0:T(128)S(1)} fusion(bf16[512,4096]{1,0:T(8,128)(2,1)} %reshape.242, bf16[1,128,4096]{2,1,0:T(8,128)(2,1)S(1)} %copy-done, f32[128]{0:T(128)S(1)} %get-tuple-element.132, f32[128]{0:T(128)S(1)} %broadcast_multiply_fusion, bf16[128,512]{1,0:T(8,128)(2,1)S(1)} %get-tuple-element.131, f32[128]{0:T(128)S(1)} %get-tuple-element.133, ...), kind=kOutput, calls=%fused_computation.38 | convolution fusion | flops 540278656 | bytes 5376512 | tf_op jit(solution)/shard_map/dot_general | solution.py:105
  (86 shorter events, 8.9 us)
Async XLA Ops:
  7.2 133.0 %all-gather.2.cloned.1.call-start = ((), (), s32[]{:S(2)}) async-start(), calls=%async_computation.5 | async-start | bytes 15790080 | tf_op jit(solution)/shard_map/all_gather | solution.py:90
  7.2 4.7 %collective-permute-start = (bf16[4,3072]{1,0:T(4,128)(2,1)}, bf16[4,3072]{1,0:T(4,128)(2,1)S(1)}, u32[]{:S(2)}, u32[]{:S(2)}) collective-permute-start(bf16[4,3072]{1,0:T(4,128)(2,1)} %param.22), channel_id=1, source_target_pairs={{0,1},{1,0},{2,3},{3,2},{4,5},{5,4},{6,7},{7,6},{8,9},{9,8},{10,11... | collective-permute-start | bytes 73736 | tf_op jit(solution)/shard_map/ppermute | solution.py:131
  13.5 0.6 copy-start.6
  17.9 130.6 %all-to-all-start = ((bf16[32,1,64]{2,1,0:T(2,128)(2,1)}), bf16[32,1,64]{2,1,0:T(2,128)(2,1)S(1)}, u32[]{:S(2)}, u32[]{:S(2)}) async-start(bf16[32,1,64]{2,1,0:T(2,128)(2,1)} %broadcast_in_dim.98), calls=%async_computation | async-start | bytes 32768 | tf_op jit(solution)/shard_map/all_to_all | solution.py:175
  148.4 30.9 %all-to-all-start.1 = ((bf16[32,2,6144]{2,1,0:T(2,128)(2,1)}), bf16[32,2,6144]{2,1,0:T(2,128)(2,1)}, u32[]{:S(2)}, u32[]{:S(2)}) async-start(bf16[32,2,6144]{2,1,0:T(2,128)(2,1)} %reshape.259), calls=%async_computation.1 | async-start | bytes 1572864 | tf_op jit(solution)/shard_map/all_to_all | solution.py:171
  185.4 13.2 %copy-start.8 = (s32[1,128]{1,0:T(1,128)S(1)}, s32[1,128]{1,0:T(1,128)}, u32[]{:S(2)}) copy-start(s32[1,128]{1,0:T(1,128)} %param.21) | copy-start | bytes 1540
  185.4 1.7 copy-start.4
  188.5 1.7 copy-start.4
  193.4 17.0 %all-to-all-start.2 = ((bf16[32,2,2048]{2,1,0:T(2,128)(2,1)}), bf16[32,2,2048]{2,1,0:T(2,128)(2,1)S(1)}, u32[]{:S(2)}, u32[]{:S(2)}) async-start(bf16[32,2,2048]{2,1,0:T(2,128)(2,1)} %reshape.261), calls=%async_computation.2 | async-start | bytes 524288 | tf_op jit(solution)/shard_map/all_to_all | solution.py:179
  198.6 15.6 %copy-start.5 = (bf16[128,512]{1,0:T(8,128)(2,1)S(1)}, bf16[128,512]{1,0:T(8,128)(2,1)}, u32[]{:S(2)}) copy-start(bf16[128,512]{1,0:T(8,128)(2,1)} %param.26) | copy-start | bytes 393220
  198.6 15.6 %copy-start.7 = (f32[512]{0:T(512)S(1)}, f32[512]{0:T(512)}, u32[]{:S(2)}) copy-start(f32[512]{0:T(512)} %param.25) | copy-start | bytes 6148
  211.5 3.1 %copy-start.1 = (bf16[512,1536]{1,0:T(8,128)(2,1)S(1)}, bf16[512,1536]{1,0:T(8,128)(2,1)}, u32[]{:S(2)}) copy-start(bf16[512,1536]{1,0:T(8,128)(2,1)} %reshape.234) | copy-start | bytes 4718596
  216.3 26.6 %all-to-all-start.3 = ((bf16[32,3,128,32]{2,3,1,0:T(8,128)(2,1)}), bf16[32,3,128,32]{2,3,1,0:T(8,128)(2,1)S(1)}, u32[]{:S(2)}, u32[]{:S(2)}) async-start(bf16[32,3,128,32]{2,3,1,0:T(8,128)(2,1)} %bitcast.28), calls=%async_computation.3 | async-start | bytes 1572864 | tf_op jit(solution)/shard_map/all_to_all | solution.py:199
  245.4 29.6 %copy-start = (bf16[1,128,4096]{2,1,0:T(8,128)(2,1)S(1)}, bf16[1,128,4096]{2,1,0:T(8,128)(2,1)}, u32[]{:S(2)}) copy-start(bf16[1,128,4096]{2,1,0:T(8,128)(2,1)} %param.17) | copy-start | bytes 3145732
  246.7 1.5 copy-start.2
  252.5 1.5 copy-start.2
  258.2 1.5 copy-start.2
  263.9 1.5 copy-start.2
  270.0 16.1 %all-to-all-start.4 = ((bf16[32,128,32]{1,2,0:T(8,128)(2,1)}), bf16[32,128,32]{1,2,0:T(8,128)(2,1)S(1)}, u32[]{:S(2)}, u32[]{:S(2)}) async-start(bf16[32,128,32]{1,2,0:T(8,128)(2,1)} %copy_bitcast_fusion), calls=%async_computation.4 | async-start | bytes 524288 | tf_op jit(solution)/shard_map/all_to_all | solution.py:205
  286.5 3.6 %copy-start.3 = (bf16[128,512]{1,0:T(8,128)(2,1)}, bf16[128,512]{1,0:T(8,128)(2,1)S(1)}, u32[]{:S(2)}) copy-start(bf16[128,512]{1,0:T(8,128)(2,1)S(1)} %get-tuple-element.131) | copy-start | bytes 393220
Sparse Core Ops, SparseCore 0:
  14.3 125.7 all-gather.1

commit v9 on v8

--- a/solution.py
+++ b/solution.py
@@ -83,6 +83,37 @@
     arranged = arranged.reshape(row_count, heads, query_parts, head_size)
     summed = jnp.sum(arranged.astype(jnp.float32), axis=2).astype(jnp.bfloat16)
     return summed.reshape(row_count, heads * head_size)
+
+
+def send_blocks(packed, heads, seq_count):
+    row_count = packed.shape[0]
+    head_size = packed.shape[1] // (3 * heads)
+    query_parts = seq_count // heads
+    part_rows = row_count // query_parts
+    layout = packed.reshape(row_count, 3, heads, head_size)
+    queries = layout[:, 0].reshape(query_parts, part_rows, heads, head_size).transpose(2, 0, 1, 3)
+    queries = queries.reshape(seq_count, 1, part_rows, head_size)
+    pairs = layout[:, 1:].transpose(2, 1, 0, 3).reshape(heads, 2 * query_parts, part_rows, head_size)
+    pairs = jnp.broadcast_to(pairs[:, None], (heads, query_parts) + pairs.shape[1:])
+    pairs = pairs.reshape(seq_count, 2 * query_parts, part_rows, head_size)
+    return jnp.concatenate([queries, pairs], axis=1)
+
+
+def attend_blocks(incoming, key_ok):
+    sources, blocks, part_rows, head_size = incoming.shape
+    query_parts = (blocks - 1) // 2
+    queries = incoming[:, 0].reshape(sources * part_rows, 1, head_size)
+    keys = incoming[:, 1 : 1 + query_parts].reshape(-1, 1, head_size)
+    values = incoming[:, 1 + query_parts :].reshape(-1, 1, head_size)
+    mixed = attend_rows(queries, keys, values, key_ok)
+    return mixed.reshape(sources, part_rows, head_size)
+
+
+def take_blocks(returned, heads):
+    seq_count, part_rows, head_size = returned.shape
+    query_parts = seq_count // heads
+    arranged = returned.reshape(heads, query_parts, part_rows, head_size).transpose(1, 2, 0, 3)
+    return arranged.reshape(query_parts * part_rows, heads * head_size)
 
 
 def gather_weights(pieces):
@@ -167,17 +198,16 @@
         layer_norm(kept_rows.astype(jnp.float32)).astype(jnp.bfloat16), full_project
     ).astype(jnp.bfloat16)
     key_marks = jnp.broadcast_to(present.astype(jnp.bfloat16)[None, :], (seq_count, slab_max))
-    outgoing = spread_heads(packed, ENC_HEADS, seq_count)
+    outgoing = send_blocks(packed, ENC_HEADS, seq_count)
     incoming = lax.all_to_all(outgoing, "seq", split_axis=0, concat_axis=0, tiled=True)
     incoming, full_merge, full_lift, dec_weights[0] = lax.optimization_barrier(
         (incoming, full_merge, full_lift, dec_weights[0])
     )
     in_marks = lax.all_to_all(key_marks, "seq", split_axis=0, concat_axis=0, tiled=True)
     key_ok = in_marks.reshape(-1) > 0.5
-    mixed_part = attend_heads(incoming, key_ok, ENC_HEADS, enc_part, enc_parts)
-    returning = place_rows(mixed_part, incoming.shape[0] * incoming.shape[2], enc_part, seq_count)
+    returning = attend_blocks(incoming, key_ok)
     returned = lax.all_to_all(returning, "seq", split_axis=0, concat_axis=0, tiled=True)
-    mixed_rows = collect_heads(returned, ENC_HEADS, enc_parts)
+    mixed_rows = take_blocks(returned, ENC_HEADS)
     encoded = kept_rows.astype(jnp.float32) + weight_dot(mixed_rows, full_merge)
     lifted_list = [
         weight_dot(layer_norm(encoded).astype(jnp.bfloat16), full_lift)
@@ -195,15 +225,14 @@
     dec_packed = weight_dot(
         layer_norm(dec_in.astype(jnp.float32)).astype(jnp.bfloat16), dec_weights[0]
     ).astype(jnp.bfloat16)
-    outgoing = spread_heads(dec_packed, DEC_HEADS, seq_count)
+    outgoing = send_blocks(dec_packed, DEC_HEADS, seq_count)
     incoming = lax.all_to_all(outgoing, "seq", split_axis=0, concat_axis=0, tiled=True)
     incoming, dec_weights[1], dec_weights[2] = lax.optimization_barrier(
         (incoming, dec_weights[1], dec_weights[2])
     )
-    mixed_part = attend_heads(incoming, None, DEC_HEADS, dec_part, dec_parts)
-    returning = place_rows(mixed_part, incoming.shape[0] * incoming.shape[2], dec_part, seq_count)
+    returning = attend_blocks(incoming, None)
     returned = lax.all_to_all(returning, "seq", split_axis=0, concat_axis=0, tiled=True)
-    mixed_rows = collect_heads(returned, DEC_HEADS, dec_parts)
+    mixed_rows = take_blocks(returned, DEC_HEADS)
     decoded = (
         dec_in.astype(jnp.float32)
         + weight_dot(mixed_rows, dec_weights[1])

time: 299 us -> 298 us (level)
  waiting for transfers between devices: 142 us -> 131 us
  local copies, waits for them, and re-layouts: 59.2 us -> 65.5 us
  starting transfers between devices: 34.8 us -> 38.1 us
    all_to_all x2, waiting for transfers between devices: 13.1 us -> 6.28 us  [shards(): lax.all_to_all(outgoing, 'seq', split_axis=0, concat_axis=0, tiled=True)]
    all_to_all x2, starting transfers between devices: 10 us -> 13.6 us  [shards(): lax.all_to_all(returning, 'seq', split_axis=0, concat_axis=0, tiled=True)]
    all_to_all x2, waiting for transfers between devices: 22.3 us -> 18.9 us  [shards(): lax.all_to_all(returning, 'seq', split_axis=0, concat_axis=0, tiled=True)]
    unnamed x24 -> x41, local copies, waits for them, and re-layouts: 6.81 us -> 10.1 us
    while x3 -> x5, local copies, waits for them, and re-layouts: 2.1 us -> 5.24 us  [attend_rows(): lax.map(one_block, query_blocks).reshape(query_rows, head_size)]
where the time goes in v9:
time: 298 us; the launch traced here: 296 us
  waiting for transfers between devices  131 us (44%)
  local copies, waits for them, and re-layouts  65.5 us (22%)
  starting transfers between devices  38.1 us (13%)
  matrix products  31.4 us (11%)
  other arithmetic  15.6 us (5%)
  between operations  14.6 us (5%)
    all_gather x1, waiting for transfers between devices, gather_weights(): every = lax.all_gather(flat, ('dp', 'seq'), axis=0, tiled=True)  106 us
    all_to_all x2, waiting for transfers between devices, shards(): lax.all_to_all(returning, 'seq', split_axis=0, concat_axis=0, tiled=True)  18.9 us
    slice x6, local copies, waits for them, and re-layouts, gather_weights(): part = tiles[:, start // lane:(start + size) // lane, :]  18.8 us
    reshape x5, local copies, waits for them, and re-layouts, gather_weights(): wholes.append(part.reshape(sources * piece.shape[0], piece.shape[1]))  17.2 us
    all_to_all x2, starting transfers between devices, shards(): lax.all_to_all(returning, 'seq', split_axis=0, concat_axis=0, tiled=True)  13.6 us
    all_to_all x2, starting transfers between devices, shards(): lax.all_to_all(outgoing, 'seq', split_axis=0, concat_axis=0, tiled=True)  11.8 us
    dot_general x6, matrix products, one_block(): jnp.einsum('qk,kd->qd', weights, values_one, preferred_element_type=jnp.f...  11.6 us
    all_to_all x1, starting transfers between devices, shards(): lax.all_to_all(key_marks, 'seq', split_axis=0, concat_axis=0, tiled=True)  10.7 us
  transfers between devices with their start and end apart: 7, of which 5 were waited for; matrix products, arithmetic and copies ran while one was open for 18% of the time, Pallas kernels for 0%

profile of v9, /device:TPU:32, one launch (start us, length us, event | category | flops | bytes accessed | tf_op | source)
XLA Modules:
  0.0 296.1 jit_solution(1052979018624724954)
XLA Ops:
  7.2 1.9 collective-permute-start
  11.9 0.9 fusion.60
  14.2 0.8 copy.52
  15.8 1.3 fusion.67
  18.4 10.7 %all-to-all-start = ((bf16[32,1,64]{2,1,0:T(2,128)(2,1)}), bf16[32,1,64]{2,1,0:T(2,128)(2,1)S(1)}, u32[]{:S(2)}, u32[]{:S(2)}) async-start(bf16[32,1,64]{2,1,0:T(2,128)(2,1)} %broadcast_in_dim.99), calls=%async_computation | async-start | bytes 32768 | tf_op jit(solution)/shard_map/all_to_all | solution.py:206
  29.2 5.2 %fusion.68 = (f32[64]{0:T(128)S(1)}, f32[64,1024]{1,0:T(8,128)S(1)}) fusion(bf16[4096,1024]{1,0:T(8,128)(2,1)} %param.18, bf16[1,128,4096]{2,1,0:T(8,128)(2,1)} %param.17, bf16[128,1024]{1,0:T(8,128)(2,1)} %param.20, f32[1024]{0:T(1024)} %param.19, s32[128]{0:T(128)S(1)} %get-tuple-element.118), kind=kOutput, calls=%fused_computation.125 | convolution fusion | flops 1091248128 | bytes 9966336 | tf_op jit(solution)/shard_map/dot_general | solution.py:195
  34.6 105.6 %all-gather.2.cloned.1.call-done = bf16[7864320]{0:T(1024)(128)(2,1)} async-done(((bf16[30720]{0:T(1024)(128)(2,1)}), bf16[7864320]{0:T(1024)(128)(2,1)}) %all-gather.2.cloned.1.call-update) | async-done | bytes 15728656 | tf_op jit(solution)/shard_map/all_gather | solution.py:121
  140.1 4.0 %slice.66 = bf16[256,96,128]{2,1,0:T(8,128)(2,1)S(1)} slice(bf16[256,240,128]{2,1,0:T(8,128)(2,1)} %bitcast.143), slice={[0:256], [0:96], [0:128]} | slice | bytes 12582912 | tf_op jit(solution)/shard_map/slice | solution.py:129
  144.1 1.3 convolution_convert_fusion
  146.8 1.6 reshape.253
  148.3 7.4 %all-to-all-start.1 = ((bf16[32,2,5120]{2,1,0:T(2,128)(2,1)}), bf16[32,2,5120]{2,1,0:T(2,128)(2,1)S(1)}, u32[]{:S(2)}, u32[]{:S(2)}) async-start(bf16[32,2,5120]{2,1,0:T(2,128)(2,1)} %reshape.253), calls=%async_computation.1 | async-start | bytes 1310720 | tf_op jit(solution)/shard_map/all_to_all | solution.py:202
  155.8 1.2 fusion.64
  157.2 3.3 %slice.69 = bf16[256,32,128]{2,1,0:T(8,128)(2,1)} slice(bf16[256,240,128]{2,1,0:T(8,128)(2,1)} %bitcast.144), slice={[0:256], [96:128], [0:128]} | slice | bytes 4194304 | tf_op jit(solution)/shard_map/slice | solution.py:129
  160.5 2.9 slice.71
  163.4 2.4 slice.70
  165.8 2.8 reshape.229
  168.6 4.3 %reshape.231 = bf16[512,1536]{1,0:T(8,128)(2,1)} reshape(bf16[256,24,128]{2,1,0:T(8,128)(2,1)} %slice.71) | data formatting | bytes 3145728 | tf_op jit(solution)/shard_map/reshape | solution.py:130
  172.9 2.5 reshape.230
  175.4 1.1 all-to-all-done.1
  176.5 1.8 reshape.254
  178.4 2.1 fusion.66
  180.4 1.0 slice.54
  181.4 7.4 %while.20 = (s32[]{:T(128)}, bf16[2,512,64]{1,2,0:T(8,128)(2,1)}, pred[2048]{0:T(1024)(128)(4,1)S(1)}, bf16[2,512,64]{2,1,0:T(8,128)(2,1)S(1)}, bf16[2048,64]{1,...) while((s32[]{:T(128)}, bf16[2,512,64]{1,2,0:T(8,128)(2,1)}, pred[2048]{0:T(1024)(128)(4,1)S(1)}, ...), condition=%wide.region_7.8_spmd, body=%wide.region_4.7_spmd.sunk | while | flops 281050112 | bytes 15941801 | solution.py:40
  181.5 0.8 fusion.97
  182.3 0.9 fusion.98
  183.2 1.3 fusion.99
  185.2 0.8 fusion.97
  186.0 0.9 fusion.98
  186.9 1.3 fusion.99
  188.8 1.1 copy.55
  189.9 0.9 reshape.255
  190.8 8.8 %all-to-all-start.2 = ((bf16[32,2,1024]{2,1,0:T(2,128)(2,1)}), bf16[32,2,1024]{2,1,0:T(2,128)(2,1)S(1)}, u32[]{:S(2)}, u32[]{:S(2)}) async-start(bf16[32,2,1024]{2,1,0:T(2,128)(2,1)} %reshape.255), calls=%async_computation.2 | async-start | bytes 262144 | tf_op jit(solution)/shard_map/all_to_all | solution.py:209
  199.6 9.7 %all-to-all-done.2 = bf16[32,2,1024]{2,1,0:T(2,128)(2,1)S(1)} async-done(((bf16[32,2,1024]{2,1,0:T(2,128)(2,1)}), bf16[32,2,1024]{2,1,0:T(2,128)(2,1)S(1)}, u32[]{:S(2)}, u32[]{:S(2)}) %all-to-all-start.2) | async-done | bytes 131104 | tf_op jit(solution)/shard_map/all_to_all | solution.py:209
  210.7 1.7 fusion.45
  212.4 0.8 gather_fusion
  216.1 1.5 reshape.257
  217.6 4.4 %all-to-all-start.3 = ((bf16[32,2,5120]{2,1,0:T(2,128)(2,1)}), bf16[32,2,5120]{2,1,0:T(2,128)(2,1)S(1)}, u32[]{:S(2)}, u32[]{:S(2)}) async-start(bf16[32,2,5120]{2,1,0:T(2,128)(2,1)} %reshape.257), calls=%async_computation.3 | async-start | bytes 1310720 | tf_op jit(solution)/shard_map/all_to_all | solution.py:229
  222.2 5.2 %slice.75 = bf16[256,64,128]{2,1,0:T(8,128)(2,1)} slice(bf16[256,240,128]{2,1,0:T(8,128)(2,1)} %bitcast.147), slice={[0:256], [176:240], [0:128]} | slice | bytes 8388608 | tf_op jit(solution)/shard_map/slice | solution.py:129
  227.4 1.1 slice.74
  228.5 7.3 %reshape.238 = bf16[512,4096]{1,0:T(8,128)(2,1)} reshape(bf16[256,64,128]{2,1,0:T(8,128)(2,1)} %slice.75) | data formatting | bytes 8388608 | tf_op jit(solution)/shard_map/reshape | solution.py:130
  236.1 5.2 %all-to-all-done.3 = bf16[32,2,5120]{2,1,0:T(2,128)(2,1)S(1)} async-done(((bf16[32,2,5120]{2,1,0:T(2,128)(2,1)}), bf16[32,2,5120]{2,1,0:T(2,128)(2,1)S(1)}, u32[]{:S(2)}, u32[]{:S(2)}) %all-to-all-start.3) | async-done | bytes 655392 | tf_op jit(solution)/shard_map/all_to_all | solution.py:229
  241.3 0.7 reshape.258
  242.0 0.9 fusion.65
  243.0 0.7 slice.61
  243.7 1.5 copy.71
  245.2 1.3 copy.72
  246.6 1.2 copy.70
  247.8 20.5 %while.21 = (s32[]{:T(128)}, bf16[4,512,32]{1,2,0:T(8,128)(2,1)S(1)}, bf16[4,512,32]{2,1,0:T(8,128)(2,1)S(1)}, bf16[4096,32]{1,0:T(8,128)(2,1)S(1)}, bf16[4096,32]{1,0:T(8,128)(2,1)}, /*index=5*/s32[]{:T(128)}) while((s32[]{:T(128)}, bf16[4,512,32]{1,2,0:T(8,128)(2,1)S(1)}, bf16[4,512,32]{2,1,0:T(8,128)(2,1)S(1)}, ...), condition=%wide.region_15.16_spmd, body=%wide.region_12.15_spmd.sunk | while | flops 287325184 | bytes 28485736 | solution.py:40
  247.8 1.3 multiply_reduce_fusion.4
  249.2 1.5 fusion.102
  250.7 2.3 fusion.103
  252.9 1.3 multiply_reduce_fusion.4
  254.3 1.5 fusion.102
  255.8 2.3 fusion.103
  258.1 1.3 multiply_reduce_fusion.4
  259.4 1.5 fusion.102
  260.9 2.3 fusion.103
  263.2 1.3 multiply_reduce_fusion.4
  264.6 1.5 fusion.102
  266.1 2.3 fusion.103
  268.8 0.8 reshape.259
  269.6 4.9 %all-to-all-start.4 = ((bf16[32,2,1024]{2,1,0:T(2,128)(2,1)}), bf16[32,2,1024]{2,1,0:T(2,128)(2,1)S(1)}, u32[]{:S(2)}, u32[]{:S(2)}) async-start(bf16[32,2,1024]{2,1,0:T(2,128)(2,1)} %reshape.259), calls=%async_computation.4 | async-start | bytes 262144 | tf_op jit(solution)/shard_map/all_to_all | solution.py:234
  274.9 9.2 %all-to-all-done.4 = bf16[32,2,1024]{2,1,0:T(2,128)(2,1)S(1)} async-done(((bf16[32,2,1024]{2,1,0:T(2,128)(2,1)}), bf16[32,2,1024]{2,1,0:T(2,128)(2,1)S(1)}, u32[]{:S(2)}, u32[]{:S(2)}) %all-to-all-start.4) | async-done | bytes 131104 | tf_op jit(solution)/shard_map/all_to_all | solution.py:234
  285.3 3.4 %fusion.26 = f32[128]{0:T(128)S(1)} fusion(bf16[512,4096]{1,0:T(8,128)(2,1)} %reshape.238, bf16[1,128,4096]{2,1,0:T(8,128)(2,1)S(1)} %copy-done, f32[128]{0:T(128)S(1)} %get-tuple-element.125, f32[128]{0:T(128)S(1)} %broadcast_multiply_fusion, bf16[128,512]{1,0:T(8,128)(2,1)S(1)} %get-tuple-element.124, f32[128]{0:T(128)S(1)} %get-tuple-element.126, ...), kind=kOutput, calls=%fused_computation.38 | convolution fusion | flops 540278656 | bytes 5376512 | tf_op jit(solution)/shard_map/dot_general | solution.py:136
  (116 shorter events, 16.6 us)
Async XLA Ops:
  7.2 133.0 %all-gather.2.cloned.1.call-start = ((), (), s32[]{:S(2)}) async-start(), calls=%async_computation.5 | async-start | bytes 15790080 | tf_op jit(solution)/shard_map/all_gather | solution.py:121
  7.2 4.7 %collective-permute-start = (bf16[4,3072]{1,0:T(4,128)(2,1)}, bf16[4,3072]{1,0:T(4,128)(2,1)S(1)}, u32[]{:S(2)}, u32[]{:S(2)}) collective-permute-start(bf16[4,3072]{1,0:T(4,128)(2,1)} %param.22), channel_id=1, source_target_pairs={{0,1},{1,0},{2,3},{3,2},{4,5},{5,4},{6,7},{7,6},{8,9},{9,8},{10,11... | collective-permute-start | bytes 73736 | tf_op jit(solution)/shard_map/ppermute | solution.py:162
  13.5 0.6 copy-start.11
  18.4 129.9 %all-to-all-start = ((bf16[32,1,64]{2,1,0:T(2,128)(2,1)}), bf16[32,1,64]{2,1,0:T(2,128)(2,1)S(1)}, u32[]{:S(2)}, u32[]{:S(2)}) async-start(bf16[32,1,64]{2,1,0:T(2,128)(2,1)} %broadcast_in_dim.99), calls=%async_computation | async-start | bytes 32768 | tf_op jit(solution)/shard_map/all_to_all | solution.py:206
  148.3 28.2 %all-to-all-start.1 = ((bf16[32,2,5120]{2,1,0:T(2,128)(2,1)}), bf16[32,2,5120]{2,1,0:T(2,128)(2,1)S(1)}, u32[]{:S(2)}, u32[]{:S(2)}) async-start(bf16[32,2,5120]{2,1,0:T(2,128)(2,1)} %reshape.253), calls=%async_computation.1 | async-start | bytes 1310720 | tf_op jit(solution)/shard_map/all_to_all | solution.py:202
  181.4 18.2 %copy-start.13 = (s32[128]{0:T(128)S(1)}, s32[128]{0:T(128)}, u32[]{:S(2)}) copy-start(s32[128]{0:T(128)} %get-tuple-element.84) | copy-start | bytes 1540
  181.4 18.2 %copy-start.15 = (s32[128]{0:T(128)S(1)}, s32[128]{0:T(128)}, u32[]{:S(2)}) copy-start(s32[128]{0:T(128)} %get-tuple-element.82) | copy-start | bytes 1540
  181.5 1.8 copy-start.6
  181.5 1.8 copy-start.8
  184.5 0.7 copy-start.9
  185.2 1.7 copy-start.6
  185.2 1.7 copy-start.8
  188.2 0.7 copy-start.9
  190.8 22.4 %copy-start.7 = (bf16[128,512]{1,0:T(8,128)(2,1)S(1)}, bf16[128,512]{1,0:T(8,128)(2,1)}, u32[]{:S(2)}) copy-start(bf16[128,512]{1,0:T(8,128)(2,1)} %param.26) | copy-start | bytes 393220
  190.8 22.4 %copy-start.12 = (f32[512]{0:T(512)S(1)}, f32[512]{0:T(512)}, u32[]{:S(2)}) copy-start(f32[512]{0:T(512)} %param.25) | copy-start | bytes 6148
  190.8 22.4 %copy-start.16 = (pred[128]{0:T(512)(128)(4,1)S(1)}, pred[128]{0:T(512)(128)(4,1)}, u32[]{:S(2)}) copy-start(pred[128]{0:T(512)(128)(4,1)} %fusion.64) | copy-start | bytes 388
  190.8 18.5 %all-to-all-start.2 = ((bf16[32,2,1024]{2,1,0:T(2,128)(2,1)}), bf16[32,2,1024]{2,1,0:T(2,128)(2,1)S(1)}, u32[]{:S(2)}, u32[]{:S(2)}) async-start(bf16[32,2,1024]{2,1,0:T(2,128)(2,1)} %reshape.255), calls=%async_computation.2 | async-start | bytes 262144 | tf_op jit(solution)/shard_map/all_to_all | solution.py:209
  210.5 3.5 %copy-start.1 = (bf16[512,1536]{1,0:T(8,128)(2,1)S(1)}, bf16[512,1536]{1,0:T(8,128)(2,1)}, u32[]{:S(2)}) copy-start(bf16[512,1536]{1,0:T(8,128)(2,1)} %reshape.231) | copy-start | bytes 4718596
  213.4 0.7 copy-start.2
  215.4 6.6 %copy-start = (bf16[1,128,4096]{2,1,0:T(8,128)(2,1)S(1)}, bf16[1,128,4096]{2,1,0:T(8,128)(2,1)}, u32[]{:S(2)}) copy-start(bf16[1,128,4096]{2,1,0:T(8,128)(2,1)} %param.17) | copy-start | bytes 3145732
  217.6 23.6 %all-to-all-start.3 = ((bf16[32,2,5120]{2,1,0:T(2,128)(2,1)}), bf16[32,2,5120]{2,1,0:T(2,128)(2,1)S(1)}, u32[]{:S(2)}, u32[]{:S(2)}) async-start(bf16[32,2,5120]{2,1,0:T(2,128)(2,1)} %reshape.257), calls=%async_computation.3 | async-start | bytes 1310720 | tf_op jit(solution)/shard_map/all_to_all | solution.py:229
  242.0 5.8 %copy-start.10 = (bf16[4,512,32]{1,2,0:T(8,128)(2,1)S(1)}, bf16[4,512,32]{1,2,0:T(8,128)(2,1)}, u32[]{:S(2)}) copy-start(bf16[4,512,32]{1,2,0:T(8,128)(2,1)} %custom-call.4) | copy-start | bytes 393220
  249.1 1.5 copy-start.4
  254.3 1.5 copy-start.4
  259.4 1.5 copy-start.4
  264.5 1.5 copy-start.4
  268.3 16.4 %copy-start.3 = (bf16[128,512]{1,0:T(8,128)(2,1)S(1)}, bf16[128,512]{1,0:T(8,128)(2,1)}, u32[]{:S(2)}) copy-start(bf16[128,512]{1,0:T(8,128)(2,1)} %copy-done.2) | copy-start | bytes 393220
  269.6 14.5 %all-to-all-start.4 = ((bf16[32,2,1024]{2,1,0:T(2,128)(2,1)}), bf16[32,2,1024]{2,1,0:T(2,128)(2,1)S(1)}, u32[]{:S(2)}, u32[]{:S(2)}) async-start(bf16[32,2,1024]{2,1,0:T(2,128)(2,1)} %reshape.259), calls=%async_computation.4 | async-start | bytes 262144 | tf_op jit(solution)/shard_map/all_to_all | solution.py:234
  285.1 3.6 %copy-start.5 = (bf16[128,512]{1,0:T(8,128)(2,1)}, bf16[128,512]{1,0:T(8,128)(2,1)S(1)}, u32[]{:S(2)}) copy-start(bf16[128,512]{1,0:T(8,128)(2,1)S(1)} %get-tuple-element.124) | copy-start | bytes 393220
  285.3 3.4 %copy-start.14 = (s32[1,128]{1,0:T(1,128)S(1)}, s32[1,128]{1,0:T(1,128)}, u32[]{:S(2)}) copy-start(s32[1,128]{1,0:T(1,128)} %param.21) | copy-start | bytes 1540
Sparse Core Ops, SparseCore 0:
  14.3 125.7 all-gather.1

commit v10 on v9

--- a/solution.py
+++ b/solution.py
@@ -200,13 +200,12 @@
     key_marks = jnp.broadcast_to(present.astype(jnp.bfloat16)[None, :], (seq_count, slab_max))
     outgoing = send_blocks(packed, ENC_HEADS, seq_count)
     incoming = lax.all_to_all(outgoing, "seq", split_axis=0, concat_axis=0, tiled=True)
-    incoming, full_merge, full_lift, dec_weights[0] = lax.optimization_barrier(
-        (incoming, full_merge, full_lift, dec_weights[0])
-    )
+    incoming, full_merge, full_lift = lax.optimization_barrier((incoming, full_merge, full_lift))
     in_marks = lax.all_to_all(key_marks, "seq", split_axis=0, concat_axis=0, tiled=True)
     key_ok = in_marks.reshape(-1) > 0.5
     returning = attend_blocks(incoming, key_ok)
     returned = lax.all_to_all(returning, "seq", split_axis=0, concat_axis=0, tiled=True)
+    returned, dec_weights[0] = lax.optimization_barrier((returned, dec_weights[0]))
     mixed_rows = take_blocks(returned, ENC_HEADS)
     encoded = kept_rows.astype(jnp.float32) + weight_dot(mixed_rows, full_merge)
     lifted_list = [

time: 298 us -> 300 us (level)
    all_to_all x2, waiting for transfers between devices: 6.28 us -> 16.3 us  [shards(): lax.all_to_all(outgoing, 'seq', split_axis=0, concat_axis=0, tiled=True)]
    all_to_all x2, waiting for transfers between devices: 18.9 us -> 11.1 us  [shards(): lax.all_to_all(returning, 'seq', split_axis=0, concat_axis=0, tiled=True)]
    all_to_all x2, starting transfers between devices: 13.6 us -> 9.97 us  [shards(): lax.all_to_all(returning, 'seq', split_axis=0, concat_axis=0, tiled=True)]
    all_to_all x2, starting transfers between devices: 11.8 us -> 15.4 us  [shards(): lax.all_to_all(outgoing, 'seq', split_axis=0, concat_axis=0, tiled=True)]
    unnamed x41 -> x42, local copies, waits for them, and re-layouts: 10.1 us -> 11 us
  transfers between devices with their start and end apart: 7 -> 7, of which waited for: 5 -> 5; matrix products, arithmetic and copies ran while one was open for 18% -> 17% of each run, Pallas kernels for 0% -> 0%
where the time goes in v10:
time: 300 us; the launch traced here: 299 us
  waiting for transfers between devices  133 us (44%)
  local copies, waits for them, and re-layouts  64.9 us (22%)
  starting transfers between devices  38.1 us (13%)
  matrix products  31.9 us (11%)
  other arithmetic  15.8 us (5%)
  between operations  14.6 us (5%)
    all_gather x1, waiting for transfers between devices, gather_weights(): every = lax.all_gather(flat, ('dp', 'seq'), axis=0, tiled=True)  106 us
    slice x6, local copies, waits for them, and re-layouts, gather_weights(): part = tiles[:, start // lane:(start + size) // lane, :]  17.8 us
    reshape x5, local copies, waits for them, and re-layouts, gather_weights(): wholes.append(part.reshape(sources * piece.shape[0], piece.shape[1]))  16.3 us
    all_to_all x2, waiting for transfers between devices, shards(): lax.all_to_all(outgoing, 'seq', split_axis=0, concat_axis=0, tiled=True)  16.3 us
    all_to_all x2, starting transfers between devices, shards(): lax.all_to_all(outgoing, 'seq', split_axis=0, concat_axis=0, tiled=True)  15.4 us
    dot_general x6, matrix products, one_block(): jnp.einsum('qk,kd->qd', weights, values_one, preferred_element_type=jnp.f...  11.6 us
    all_to_all x2, waiting for transfers between devices, shards(): lax.all_to_all(returning, 'seq', split_axis=0, concat_axis=0, tiled=True)  11.1 us
    unnamed x42, local copies, waits for them, and re-layouts  11 us
  transfers between devices with their start and end apart: 7, of which 5 were waited for; matrix products, arithmetic and copies ran while one was open for 17% of the time, Pallas kernels for 0%

profile of v10, /device:TPU:32, one launch (start us, length us, event | category | flops | bytes accessed | tf_op | source)
XLA Modules:
  0.0 298.9 jit_solution(12135142139404181705)
XLA Ops:
  7.2 1.9 collective-permute-start
  11.2 0.7 copy.80
  11.9 0.9 fusion.60
  14.2 0.8 copy.52
  15.3 1.3 fusion.63
  17.9 10.7 %all-to-all-start = ((bf16[32,1,64]{2,1,0:T(2,128)(2,1)}), bf16[32,1,64]{2,1,0:T(2,128)(2,1)S(1)}, u32[]{:S(2)}, u32[]{:S(2)}) async-start(bf16[32,1,64]{2,1,0:T(2,128)(2,1)} %broadcast_in_dim.99), calls=%async_computation | async-start | bytes 32768 | tf_op jit(solution)/shard_map/all_to_all | solution.py:204
  28.6 5.2 %fusion.67 = (f32[64]{0:T(128)S(1)}, f32[64,1024]{1,0:T(8,128)S(1)}) fusion(bf16[4096,1024]{1,0:T(8,128)(2,1)} %param.18, bf16[1,128,4096]{2,1,0:T(8,128)(2,1)} %param.17, bf16[128,1024]{1,0:T(8,128)(2,1)} %param.20, f32[1024]{0:T(1024)} %param.19, s32[128]{0:T(128)S(1)} %get-tuple-element.119), kind=kOutput, calls=%fused_computation.124 | convolution fusion | flops 1091248128 | bytes 9966336 | tf_op jit(solution)/shard_map/dot_general | solution.py:195
  34.0 106.1 %all-gather.2.cloned.1.call-done = bf16[7864320]{0:T(1024)(128)(2,1)} async-done(((bf16[30720]{0:T(1024)(128)(2,1)}), bf16[7864320]{0:T(1024)(128)(2,1)}) %all-gather.2.cloned.1.call-update) | async-done | bytes 15728656 | tf_op jit(solution)/shard_map/all_gather | solution.py:121
  140.1 4.0 %slice.66 = bf16[256,96,128]{2,1,0:T(8,128)(2,1)S(1)} slice(bf16[256,240,128]{2,1,0:T(8,128)(2,1)} %bitcast.143), slice={[0:256], [0:96], [0:128]} | slice | bytes 12582912 | tf_op jit(solution)/shard_map/slice | solution.py:129
  144.1 1.3 convolution_convert_fusion
  146.7 1.6 reshape.253
  148.3 7.5 %all-to-all-start.1 = ((bf16[32,2,5120]{2,1,0:T(2,128)(2,1)}), bf16[32,2,5120]{2,1,0:T(2,128)(2,1)}, u32[]{:S(2)}, u32[]{:S(2)}) async-start(bf16[32,2,5120]{2,1,0:T(2,128)(2,1)} %reshape.253), calls=%async_computation.1 | async-start | bytes 1310720 | tf_op jit(solution)/shard_map/all_to_all | solution.py:202
  156.5 3.4 %slice.69 = bf16[256,32,128]{2,1,0:T(8,128)(2,1)} slice(bf16[256,240,128]{2,1,0:T(8,128)(2,1)} %bitcast.144), slice={[0:256], [96:128], [0:128]} | slice | bytes 4194304 | tf_op jit(solution)/shard_map/slice | solution.py:129
  159.8 1.4 slice.70
  161.3 2.8 reshape.229
  164.1 1.5 reshape.230
  165.6 11.0 %all-to-all-done.1 = bf16[32,2,5120]{2,1,0:T(2,128)(2,1)} async-done(((bf16[32,2,5120]{2,1,0:T(2,128)(2,1)}), bf16[32,2,5120]{2,1,0:T(2,128)(2,1)}, u32[]{:S(2)}, u32[]{:S(2)}) %all-to-all-start.1) | async-done | bytes 655392 | tf_op jit(solution)/shard_map/all_to_all | solution.py:202
  176.6 2.5 reshape.254
  179.1 1.1 copy-done.2
  180.9 1.3 fusion.66
  182.2 7.9 %while.20 = (s32[]{:T(128)}, bf16[2,512,64]{1,2,0:T(8,128)(2,1)S(1)}, pred[2048]{0:T(1024)(128)(4,1)S(1)}, bf16[2,512,64]{2,1,0:T(8,128)(2,1)}, bf16[2048,64]{1,...) while((s32[]{:T(128)}, bf16[2,512,64]{1,2,0:T(8,128)(2,1)S(1)}, pred[2048]{0:T(1024)(128)(4,1)S(1)}, ...), condition=%wide.region_7.8_spmd, body=%wide.region_4.7_spmd.sunk | while | flops 281050112 | bytes 13582429 | solution.py:40
  182.2 1.7 fusion.96
  183.9 0.9 fusion.97
  184.9 1.3 fusion.98
  186.2 1.7 fusion.96
  187.9 0.9 fusion.97
  188.8 1.3 fusion.98
  190.3 0.8 reshape.255
  191.1 4.9 %all-to-all-start.2 = ((bf16[32,2,1024]{2,1,0:T(2,128)(2,1)}), bf16[32,2,1024]{2,1,0:T(2,128)(2,1)S(1)}, u32[]{:S(2)}, u32[]{:S(2)}) async-start(bf16[32,2,1024]{2,1,0:T(2,128)(2,1)} %reshape.255), calls=%async_computation.2 | async-start | bytes 262144 | tf_op jit(solution)/shard_map/all_to_all | solution.py:207
  196.6 2.9 slice.71
  199.5 4.4 %reshape.231 = bf16[512,1536]{1,0:T(8,128)(2,1)} reshape(bf16[256,24,128]{2,1,0:T(8,128)(2,1)} %slice.71) | data formatting | bytes 3145728 | tf_op jit(solution)/shard_map/reshape | solution.py:130
  203.9 1.9 all-to-all-done.2
  205.8 0.9 reshape.256
  206.7 1.8 copy.86
  208.5 1.1 reshape.233
  210.8 0.8 gather_fusion
  211.6 1.1 convert_reduce_fusion.1
  215.4 1.6 reshape.257
  217.0 7.9 %all-to-all-start.3 = ((bf16[32,2,5120]{2,1,0:T(2,128)(2,1)}), bf16[32,2,5120]{2,1,0:T(2,128)(2,1)S(1)}, u32[]{:S(2)}, u32[]{:S(2)}) async-start(bf16[32,2,5120]{2,1,0:T(2,128)(2,1)} %reshape.257), calls=%async_computation.3 | async-start | bytes 1310720 | tf_op jit(solution)/shard_map/all_to_all | solution.py:228
  225.2 1.1 slice.74
  226.3 5.1 %slice.75 = bf16[256,64,128]{2,1,0:T(8,128)(2,1)} slice(bf16[256,240,128]{2,1,0:T(8,128)(2,1)} %bitcast.148), slice={[0:256], [176:240], [0:128]} | slice | bytes 8388608 | tf_op jit(solution)/shard_map/slice | solution.py:129
  231.7 7.3 %reshape.238 = bf16[512,4096]{1,0:T(8,128)(2,1)} reshape(bf16[256,64,128]{2,1,0:T(8,128)(2,1)} %slice.75) | data formatting | bytes 8388608 | tf_op jit(solution)/shard_map/reshape | solution.py:130
  239.0 5.3 %all-to-all-done.3 = bf16[32,2,5120]{2,1,0:T(2,128)(2,1)S(1)} async-done(((bf16[32,2,5120]{2,1,0:T(2,128)(2,1)}), bf16[32,2,5120]{2,1,0:T(2,128)(2,1)S(1)}, u32[]{:S(2)}, u32[]{:S(2)}) %all-to-all-start.3) | async-done | bytes 655392 | tf_op jit(solution)/shard_map/all_to_all | solution.py:228
  244.4 0.7 reshape.258
  245.1 1.1 fusion.65
  246.6 1.5 copy.71
  248.1 2.4 copy.72
  250.5 20.5 %while.21 = (s32[]{:T(128)}, bf16[4,512,32]{1,2,0:T(8,128)(2,1)S(1)}, bf16[4,512,32]{2,1,0:T(8,128)(2,1)S(1)}, bf16[4096,32]{1,0:T(8,128)(2,1)S(1)}, bf16[4096,32]{1,0:T(8,128)(2,1)}, /*index=5*/s32[]{:T(128)}) while((s32[]{:T(128)}, bf16[4,512,32]{1,2,0:T(8,128)(2,1)S(1)}, bf16[4,512,32]{2,1,0:T(8,128)(2,1)S(1)}, ...), condition=%wide.region_15.16_spmd, body=%wide.region_12.15_spmd.sunk | while | flops 287325184 | bytes 28485744 | solution.py:40
  250.5 1.3 multiply_reduce_fusion.4
  251.8 1.5 fusion.101
  253.3 2.3 fusion.102
  255.6 1.3 multiply_reduce_fusion.4
  257.0 1.5 fusion.101
  258.5 2.3 fusion.102
  260.8 1.3 multiply_reduce_fusion.4
  262.1 1.5 fusion.101
  263.6 2.3 fusion.102
  265.9 1.3 multiply_reduce_fusion.4
  267.2 1.5 fusion.101
  268.7 2.3 fusion.102
  271.4 0.8 reshape.259
  272.3 5.0 %all-to-all-start.4 = ((bf16[32,2,1024]{2,1,0:T(2,128)(2,1)}), bf16[32,2,1024]{2,1,0:T(2,128)(2,1)S(1)}, u32[]{:S(2)}, u32[]{:S(2)}) async-start(bf16[32,2,1024]{2,1,0:T(2,128)(2,1)} %reshape.259), calls=%async_computation.4 | async-start | bytes 262144 | tf_op jit(solution)/shard_map/all_to_all | solution.py:233
  277.8 9.2 %all-to-all-done.4 = bf16[32,2,1024]{2,1,0:T(2,128)(2,1)S(1)} async-done(((bf16[32,2,1024]{2,1,0:T(2,128)(2,1)}), bf16[32,2,1024]{2,1,0:T(2,128)(2,1)S(1)}, u32[]{:S(2)}, u32[]{:S(2)}) %all-to-all-start.4) | async-done | bytes 131104 | tf_op jit(solution)/shard_map/all_to_all | solution.py:233
  288.2 3.4 %fusion.26 = f32[128]{0:T(128)S(1)} fusion(bf16[512,4096]{1,0:T(8,128)(2,1)} %reshape.238, bf16[1,128,4096]{2,1,0:T(8,128)(2,1)S(1)} %copy-done, f32[128]{0:T(128)S(1)} %get-tuple-element.127, f32[128]{0:T(128)S(1)} %broadcast_multiply_fusion, bf16[128,512]{1,0:T(8,128)(2,1)S(1)} %get-tuple-element.126, f32[128]{0:T(128)S(1)} %get-tuple-element.128, ...), kind=kOutput, calls=%fused_computation.38 | convolution fusion | flops 540278656 | bytes 5376512 | tf_op jit(solution)/shard_map/dot_general | solution.py:136
  (106 shorter events, 15.7 us)
Async XLA Ops:
  7.2 133.0 %all-gather.2.cloned.1.call-start = ((), (), s32[]{:S(2)}) async-start(), calls=%async_computation.5 | async-start | bytes 15790080 | tf_op jit(solution)/shard_map/all_gather | solution.py:121
  7.2 4.7 %collective-permute-start = (bf16[4,3072]{1,0:T(4,128)(2,1)}, bf16[4,3072]{1,0:T(4,128)(2,1)S(1)}, u32[]{:S(2)}, u32[]{:S(2)}) collective-permute-start(bf16[4,3072]{1,0:T(4,128)(2,1)} %param.22), channel_id=1, source_target_pairs={{0,1},{1,0},{2,3},{3,2},{4,5},{5,4},{6,7},{7,6},{8,9},{9,8},{10,11... | collective-permute-start | bytes 73736 | tf_op jit(solution)/shard_map/ppermute | solution.py:162
  13.5 0.6 copy-start.11
  17.9 130.4 %all-to-all-start = ((bf16[32,1,64]{2,1,0:T(2,128)(2,1)}), bf16[32,1,64]{2,1,0:T(2,128)(2,1)S(1)}, u32[]{:S(2)}, u32[]{:S(2)}) async-start(bf16[32,1,64]{2,1,0:T(2,128)(2,1)} %broadcast_in_dim.99), calls=%async_computation | async-start | bytes 32768 | tf_op jit(solution)/shard_map/all_to_all | solution.py:204
  33.8 110.3 %copy-start.3 = (f32[64,1024]{1,0:T(8,128)}, f32[64,1024]{1,0:T(8,128)S(1)}, u32[]{:S(2)}) copy-start(f32[64,1024]{1,0:T(8,128)S(1)} %get-tuple-element.122) | copy-start | bytes 786436
  146.1 9.6 %copy-start.13 = (s32[1,128]{1,0:T(1,128)S(1)}, s32[1,128]{1,0:T(1,128)}, u32[]{:S(2)}) copy-start(s32[1,128]{1,0:T(1,128)} %param.21) | copy-start | bytes 1540
  148.3 28.3 %all-to-all-start.1 = ((bf16[32,2,5120]{2,1,0:T(2,128)(2,1)}), bf16[32,2,5120]{2,1,0:T(2,128)(2,1)}, u32[]{:S(2)}, u32[]{:S(2)}) async-start(bf16[32,2,5120]{2,1,0:T(2,128)(2,1)} %reshape.253), calls=%async_computation.1 | async-start | bytes 1310720 | tf_op jit(solution)/shard_map/all_to_all | solution.py:202
  179.1 1.1 copy-start.2
  190.3 19.4 %copy-start.4 = (f32[64,1024]{1,0:T(8,128)S(1)}, f32[64,1024]{1,0:T(8,128)}, u32[]{:S(2)}) copy-start(f32[64,1024]{1,0:T(8,128)} %copy-done.3) | copy-start | bytes 786436
  191.1 14.6 %all-to-all-start.2 = ((bf16[32,2,1024]{2,1,0:T(2,128)(2,1)}), bf16[32,2,1024]{2,1,0:T(2,128)(2,1)S(1)}, u32[]{:S(2)}, u32[]{:S(2)}) async-start(bf16[32,2,1024]{2,1,0:T(2,128)(2,1)} %reshape.255), calls=%async_computation.2 | async-start | bytes 262144 | tf_op jit(solution)/shard_map/all_to_all | solution.py:207
  199.5 11.0 %copy-start.5 = (bf16[1024,512]{1,0:T(8,128)(2,1)S(1)}, bf16[1024,512]{1,0:T(8,128)(2,1)}, u32[]{:S(2)}) copy-start(bf16[1024,512]{1,0:T(8,128)(2,1)} %reshape.230) | copy-start | bytes 3145732
  203.9 7.7 %copy-start.12 = (f32[512]{0:T(512)S(1)}, f32[512]{0:T(512)}, u32[]{:S(2)}) copy-start(f32[512]{0:T(512)} %param.25) | copy-start | bytes 6148
  203.9 7.7 %copy-start.14 = (pred[128]{0:T(512)(128)(4,1)S(1)}, pred[128]{0:T(512)(128)(4,1)}, u32[]{:S(2)}) copy-start(pred[128]{0:T(512)(128)(4,1)} %fusion.64) | copy-start | bytes 388
  210.3 3.1 %copy-start.1 = (bf16[512,1536]{1,0:T(8,128)(2,1)S(1)}, bf16[512,1536]{1,0:T(8,128)(2,1)}, u32[]{:S(2)}) copy-start(bf16[512,1536]{1,0:T(8,128)(2,1)} %reshape.231) | copy-start | bytes 4718596
  212.7 0.7 copy-start.6
  214.7 10.2 %copy-start = (bf16[1,128,4096]{2,1,0:T(8,128)(2,1)S(1)}, bf16[1,128,4096]{2,1,0:T(8,128)(2,1)}, u32[]{:S(2)}) copy-start(bf16[1,128,4096]{2,1,0:T(8,128)(2,1)} %param.17) | copy-start | bytes 3145732
  217.0 27.3 %all-to-all-start.3 = ((bf16[32,2,5120]{2,1,0:T(2,128)(2,1)}), bf16[32,2,5120]{2,1,0:T(2,128)(2,1)S(1)}, u32[]{:S(2)}, u32[]{:S(2)}) async-start(bf16[32,2,5120]{2,1,0:T(2,128)(2,1)} %reshape.257), calls=%async_computation.3 | async-start | bytes 1310720 | tf_op jit(solution)/shard_map/all_to_all | solution.py:228
  245.1 5.4 %copy-start.10 = (bf16[4,512,32]{1,2,0:T(8,128)(2,1)S(1)}, bf16[4,512,32]{1,2,0:T(8,128)(2,1)}, u32[]{:S(2)}) copy-start(bf16[4,512,32]{1,2,0:T(8,128)(2,1)} %custom-call.4) | copy-start | bytes 393220
  251.8 1.5 copy-start.8
  257.0 1.5 copy-start.8
  262.1 1.5 copy-start.8
  267.2 1.5 copy-start.8
  271.0 16.6 %copy-start.7 = (bf16[128,512]{1,0:T(8,128)(2,1)S(1)}, bf16[128,512]{1,0:T(8,128)(2,1)}, u32[]{:S(2)}) copy-start(bf16[128,512]{1,0:T(8,128)(2,1)} %copy-done.6) | copy-start | bytes 393220
  272.3 14.7 %all-to-all-start.4 = ((bf16[32,2,1024]{2,1,0:T(2,128)(2,1)}), bf16[32,2,1024]{2,1,0:T(2,128)(2,1)S(1)}, u32[]{:S(2)}, u32[]{:S(2)}) async-start(bf16[32,2,1024]{2,1,0:T(2,128)(2,1)} %reshape.259), calls=%async_computation.4 | async-start | bytes 262144 | tf_op jit(solution)/shard_map/all_to_all | solution.py:233
  288.0 3.6 %copy-start.9 = (bf16[128,512]{1,0:T(8,128)(2,1)}, bf16[128,512]{1,0:T(8,128)(2,1)S(1)}, u32[]{:S(2)}) copy-start(bf16[128,512]{1,0:T(8,128)(2,1)S(1)} %get-tuple-element.126) | copy-start | bytes 393220
Sparse Core Ops, SparseCore 0:
  14.3 125.7 all-gather.1
